TPU v7x, 256 devices: a whole 4x4x8 slice. The times are simulated.
256 devices in a mesh: node: 16 (over y, x), batch: 16 (over z, core).
Axes of the slice: x: 4, y: 4, z: 8, core: 2. Of those that a mesh axis runs over, the one named last changes fastest.
Arguments:
- inputs: bfloat16 [16, 6, 64, 8192], P('batch', None, None, 'node'), may hold values from -6 to 6
- w_conv: bfloat16 [128, 128], replicated, may hold values from -0.5 to 0.5
- b_conv: float32 [128], replicated, may hold values from -3 to 3
- w_mix: bfloat16 [64, 320], replicated, may hold values from -0.3125 to 0.3125
- b_mix: float32 [64], replicated, may hold values from -3 to 3
- w_skip: bfloat16 [256, 64], replicated, may hold values from -0.75 to 0.75
- b_skip: float32 [256], replicated, may hold values from -3 to 3
- local_fwd: bfloat16 [8192, 384], P('node'), may hold values from -0.25 to 0.25
- local_bwd: bfloat16 [8192, 384], P('node'), may hold values from -0.25 to 0.25
- remote_fwd: bfloat16 [256, 128, 128], P('node'), may hold values from -0.25 to 0.25
- remote_bwd: bfloat16 [256, 128, 128], P('node'), may hold values from -0.25 to 0.25
- tile_src: int32 [256], P('node'), may hold values from 0 to 3, as said below
- tile_dst: int32 [256], P('node'), may hold values from -1 to 3, as said below
- residual_cotangent: bfloat16 [16, 4, 64, 8192], P('batch', None, None, 'node'), may hold values from -6 to 6
- cot_skip: bfloat16 [16, 256, 8192], P('batch', None, 'node'), may hold values from -6 to 6
Outputs:
- residual_out: bfloat16 [16, 4, 64, 8192], P('batch', None, None, 'node')
- skip_out: bfloat16 [16, 256, 8192], P('batch', None, 'node')
- grad_x: bfloat16 [16, 6, 64, 8192], P('batch', None, None, 'node')
- grad_w_conv: float32 [128, 128], replicated
- grad_b_conv: float32 [128], replicated
- grad_w_mix: float32 [64, 320], replicated
- grad_b_mix: float32 [64], replicated
- grad_w_skip: float32 [256, 64], replicated
- grad_b_skip: float32 [256], replicated
Inputs may be any that keep to these rules, and one draw needn't show every extreme that they name: `tile_src`: entry p * 16 + q is a block of device p. `tile_dst`: entry p * 16 + q is a block of device q, or -1 where device p holds no tile for device q, always -1 for q = p.
All inputs are finite; a program needn't handle non-finite values.
Results may differ from a plain program's by a relative error of at most 0.012.
Values may be sent and summed in bfloat16 or wider, within the bound.
No kernel may reach another device: no remote copies, remote signals or barrier semaphores. Data moves between devices by JAX's collectives and lax.ppermute only.
A program may use at most 128 MiB of HBM per device.

v0:
```python
import math

import jax
import jax.numpy as jnp
from jax import lax
from jax.sharding import PartitionSpec as P

DILATION_GAP = 2


def neighbor_stack(values, blocks, tile_width):
    row_count = values.shape[0]
    shaped = values.reshape(row_count, blocks, tile_width)
    zeros_blk = jnp.zeros((row_count, 1, tile_width), values.dtype)
    before = jnp.concatenate([zeros_blk, shaped[:, :-1]], axis=1)
    after_blk = jnp.concatenate([shaped[:, 1:], zeros_blk], axis=1)
    return jnp.concatenate([before, shaped, after_blk], axis=2)


def band_apply(values, weights):
    tile_width = weights.shape[1] // 3
    blocks = weights.shape[0] // tile_width
    stacked = neighbor_stack(values, blocks, tile_width)
    shaped_w = weights.reshape(blocks, tile_width, 3 * tile_width)
    result = jnp.einsum("mik,iak->mia", stacked, shaped_w, preferred_element_type=jnp.float32)
    return result.reshape(values.shape[0], blocks * tile_width)


def band_transpose(gradient, weights):
    tile_width = weights.shape[1] // 3
    blocks = weights.shape[0] // tile_width
    row_count = gradient.shape[0]
    shaped_w = weights.reshape(blocks, tile_width, 3 * tile_width)
    spread = jnp.einsum(
        "mia,iak->mik",
        gradient.reshape(row_count, blocks, tile_width),
        shaped_w,
        preferred_element_type=jnp.float32,
    )
    spread = spread.reshape(row_count, blocks, 3, tile_width)
    zeros_blk = jnp.zeros((row_count, 1, tile_width), jnp.float32)
    from_after = jnp.concatenate([spread[:, 1:, 0], zeros_blk], axis=1)
    from_before = jnp.concatenate([zeros_blk, spread[:, :-1, 2]], axis=1)
    return (spread[:, :, 1] + from_after + from_before).reshape(row_count, blocks * tile_width)


def pick_blocks(values, chooser):
    blocks = chooser.shape[1]
    shaped = values.reshape(values.shape[0], blocks, values.shape[1] // blocks)
    return jnp.einsum("qi,mic->qmc", chooser, shaped, preferred_element_type=jnp.float32).astype(
        jnp.bfloat16
    )


def place_blocks(pieces, chooser):
    result = jnp.einsum("qi,qmc->mic", chooser, pieces, preferred_element_type=jnp.float32)
    return result.reshape(result.shape[0], result.shape[1] * result.shape[2])


def tile_forward(pieces, tile_vals):
    return jnp.einsum("qmc,qac->qma", pieces, tile_vals, preferred_element_type=jnp.float32).astype(
        jnp.bfloat16
    )


def tile_backward(pieces, tile_vals):
    return jnp.einsum("qma,qac->qmc", pieces, tile_vals, preferred_element_type=jnp.float32)


def shards(
    inputs,
    w_conv,
    b_conv,
    w_mix,
    b_mix,
    w_skip,
    b_skip,
    local_fwd,
    local_bwd,
    remote_fwd,
    remote_bwd,
    tile_src,
    tile_dst,
    residual_cotangent,
    cot_skip,
):
    windows, input_steps, channel_count, local_nodes = inputs.shape
    output_steps = input_steps - DILATION_GAP
    tile_width = remote_fwd.shape[1]
    blocks = local_nodes // tile_width
    block_ids = jnp.arange(blocks, dtype=jnp.int32)
    own_src = (tile_src[:, None] == block_ids[None, :]).astype(jnp.bfloat16)
    own_dst = (tile_dst[:, None] == block_ids[None, :]).astype(jnp.bfloat16)
    row_count = windows * output_steps * channel_count
    shape4 = (windows, output_steps, channel_count, local_nodes)
    paired_taps = jnp.concatenate([inputs[:, :output_steps], inputs[:, DILATION_GAP:]], axis=2)
    pre_act = (
        jnp.einsum("oc,wtcn->wton", w_conv, paired_taps, preferred_element_type=jnp.float32)
        + b_conv[None, None, :, None]
    )
    filtered = jnp.tanh(pre_act[:, :, :channel_count])
    gate_val = jax.nn.sigmoid(pre_act[:, :, channel_count:])
    hidden = (filtered * gate_val).astype(jnp.bfloat16)
    flat_hidden = hidden.reshape(row_count, local_nodes)

    def push_hop(picked_fwd, picked_bwd):
        part_fwd = tile_forward(picked_fwd, remote_fwd)
        part_bwd = tile_forward(picked_bwd, remote_bwd)
        got_fwd, got_bwd, got_dst = (
            lax.all_to_all(part_fwd, "node", split_axis=0, concat_axis=0, tiled=True),
            lax.all_to_all(part_bwd, "node", split_axis=0, concat_axis=0, tiled=True),
            lax.all_to_all(own_dst, "node", split_axis=0, concat_axis=0, tiled=True),
        )
        return (place_blocks(got_fwd, got_dst), place_blocks(got_bwd, got_dst), got_dst)

    picked = pick_blocks(flat_hidden, own_src)
    far_fwd, far_bwd, recv_dst = push_hop(picked, picked)
    hop_fwd = (band_apply(flat_hidden, local_fwd) + far_fwd).astype(jnp.bfloat16)
    hop_bwd = (band_apply(flat_hidden, local_bwd) + far_bwd).astype(jnp.bfloat16)
    far_fwd, far_bwd, recv_dst = push_hop(
        pick_blocks(hop_fwd, own_src), pick_blocks(hop_bwd, own_src)
    )
    two_fwd = (band_apply(hop_fwd, local_fwd) + far_fwd).astype(jnp.bfloat16)
    two_bwd = (band_apply(hop_bwd, local_bwd) + far_bwd).astype(jnp.bfloat16)
    stacked_parts = jnp.concatenate(
        [
            hidden,
            hop_fwd.reshape(shape4),
            two_fwd.reshape(shape4),
            hop_bwd.reshape(shape4),
            two_bwd.reshape(shape4),
        ],
        axis=2,
    )
    mixed_features = (
        jnp.einsum("oc,wtcn->wton", w_mix, stacked_parts, preferred_element_type=jnp.float32)
        + b_mix[None, None, :, None]
    )
    residual_stream = (inputs[:, DILATION_GAP:].astype(jnp.float32) + mixed_features).astype(
        jnp.bfloat16
    )
    last_step = hidden[:, output_steps - 1]
    skip_sum = (
        jnp.einsum("sc,wcn->wsn", w_skip, last_step, preferred_element_type=jnp.float32)
        + b_skip[None, :, None]
    ).astype(jnp.bfloat16)
    grad_parts = jnp.einsum(
        "co,wtcn->wton", w_mix, residual_cotangent, preferred_element_type=jnp.float32
    )
    grad_mix = jnp.einsum(
        "wtcn,wton->co", residual_cotangent, stacked_parts, preferred_element_type=jnp.float32
    )
    grad_bmix = jnp.sum(residual_cotangent.astype(jnp.float32), axis=(0, 1, 3))
    grad_skip = jnp.einsum("wsn,wcn->sc", cot_skip, last_step, preferred_element_type=jnp.float32)
    grad_bskip = jnp.sum(cot_skip.astype(jnp.float32), axis=(0, 2))

    def group_of(index):
        return grad_parts[:, :, index * channel_count : (index + 1) * channel_count].reshape(
            row_count, local_nodes
        )

    back2_fwd = group_of(2).astype(jnp.bfloat16)
    back2_bwd = group_of(4).astype(jnp.bfloat16)

    def fetch_rows(grad_fwd, grad_bwd):
        return (
            lax.all_to_all(
                pick_blocks(grad_fwd, recv_dst), "node", split_axis=0, concat_axis=0, tiled=True
            ),
            lax.all_to_all(
                pick_blocks(grad_bwd, recv_dst), "node", split_axis=0, concat_axis=0, tiled=True
            ),
        )

    got_fwd, got_bwd = fetch_rows(back2_fwd, back2_bwd)
    near1_fwd = place_blocks(tile_backward(got_fwd, remote_fwd).astype(jnp.bfloat16), own_src)
    near1_bwd = place_blocks(tile_backward(got_bwd, remote_bwd).astype(jnp.bfloat16), own_src)
    back1_fwd = (group_of(1) + band_transpose(back2_fwd, local_fwd) + near1_fwd).astype(
        jnp.bfloat16
    )
    back1_bwd = (group_of(3) + band_transpose(back2_bwd, local_bwd) + near1_bwd).astype(
        jnp.bfloat16
    )
    got_fwd, got_bwd = fetch_rows(back1_fwd, back1_bwd)
    combined = (tile_backward(got_fwd, remote_fwd) + tile_backward(got_bwd, remote_bwd)).astype(
        jnp.bfloat16
    )
    far_total = place_blocks(combined, own_src)
    skip_back = jnp.einsum("sc,wsn->wcn", w_skip, cot_skip, preferred_element_type=jnp.float32)
    direct = (
        grad_parts[:, :, :channel_count]
        .at[:, output_steps - 1]
        .add(skip_back)
        .reshape(row_count, local_nodes)
    )
    summed = (
        direct
        + band_transpose(back1_fwd, local_fwd)
        + band_transpose(back1_bwd, local_bwd)
        + far_total
    )
    grad_hidden = summed.astype(jnp.bfloat16).reshape(shape4).astype(jnp.float32)
    grad_pre = jnp.concatenate(
        [
            grad_hidden * gate_val * (1.0 - filtered * filtered),
            grad_hidden * filtered * gate_val * (1.0 - gate_val),
        ],
        axis=2,
    ).astype(jnp.bfloat16)
    tap_gradients = jnp.einsum(
        "oc,wton->wtcn", w_conv, grad_pre, preferred_element_type=jnp.float32
    )
    input_gradient = jnp.zeros((windows, input_steps, channel_count, local_nodes), jnp.float32)
    input_gradient = input_gradient.at[:, :output_steps].add(tap_gradients[:, :, :channel_count])
    input_gradient = input_gradient.at[:, DILATION_GAP:].add(
        tap_gradients[:, :, channel_count:] + residual_cotangent.astype(jnp.float32)
    )
    grad_wconv = jnp.einsum(
        "wton,wtcn->oc", grad_pre, paired_taps, preferred_element_type=jnp.float32
    )
    grad_bconv = jnp.sum(grad_pre.astype(jnp.float32), axis=(0, 1, 3))
    totals = lax.psum(
        (grad_wconv, grad_bconv, grad_mix, grad_bmix, grad_skip, grad_bskip), ("node", "batch")
    )
    grad_count = (
        windows * lax.axis_size("batch") * local_nodes * lax.axis_size("node") * output_steps
    )
    grad_scale = 1.0 / math.sqrt(float(grad_count))
    return (
        residual_stream,
        skip_sum,
        input_gradient.astype(jnp.bfloat16),
        totals[0] * grad_scale,
        totals[1] * grad_scale,
        totals[2] * grad_scale,
        totals[3] * grad_scale,
        totals[4] * grad_scale,
        totals[5] * grad_scale,
    )


def solution(mesh):
    return jax.shard_map(
        shards,
        mesh=mesh,
        in_specs=(
            P("batch", None, None, "node"),
            P(),
            P(),
            P(),
            P(),
            P(),
            P(),
            P("node", None),
            P("node", None),
            P("node", None, None),
            P("node", None, None),
            P("node"),
            P("node"),
            P("batch", None, None, "node"),
            P("batch", None, "node"),
        ),
        out_specs=(
            P("batch", None, None, "node"),
            P("batch", None, "node"),
            P("batch", None, None, "node"),
            P(),
            P(),
            P(),
            P(),
            P(),
            P(),
        ),
        check_vma=False,
    )
```

profile of v0, /device:TPU:1, one launch (start us, length us, event | category | flops | bytes accessed | tf_op | source)
XLA Modules:
  0.0 565.4 jit_solution(11325167667413975181)
XLA Ops:
  8.6 7.6 %all-to-all-start.1 = ((bf16[16,1,4]{2,1,0:T(2,128)(2,1)}), bf16[16,1,4]{2,1,0:T(2,128)(2,1)S(1)}, u32[]{:S(2)}, u32[]{:S(2)}) async-start(bf16[16,1,4]{2,1,0:T(2,128)(2,1)} %compare_convert_fusion), calls=%async_computation.1 | async-start | bytes 16384 | tf_op jit(solution)/shard_map/all_to_all | solution.py:112
  20.1 1.6 copy.168
  21.8 2.1 fusion.153
  24.4 1.6 copy.180
  26.0 2.1 fusion.152
  33.9 1.7 fusion.43
  35.6 1.7 convolution_bitcast_fusion.16
  37.3 6.7 %all-to-all-start.3 = ((bf16[16,256,128]{2,1,0:T(8,128)(2,1)}), bf16[16,256,128]{2,1,0:T(8,128)(2,1)}, u32[]{:S(2)}, u32[]{:S(2)}) async-start(bf16[16,256,128]{2,1,0:T(8,128)(2,1)} %convolution_convert_fusion.10), calls=%async_computation.3 | async-start | bytes 2097152 | tf_op jit(solution)/shard_map/all_to_all | solution.py:111
  44.0 1.8 fusion.41
  45.8 1.9 slice.221
  47.7 1.9 slice.229
  49.6 2.0 copy.201
  51.6 2.0 copy.202
  53.6 2.1 copy.200
  55.6 2.0 reshape.437
  57.7 2.0 copy.206
  59.7 2.0 copy.207
  61.7 2.0 copy.205
  63.7 2.0 reshape.441
  65.7 1.8 copy.195
  72.7 6.6 %all-to-all-start = ((bf16[16,256,128]{2,1,0:T(8,128)(2,1)}), bf16[16,256,128]{2,1,0:T(8,128)(2,1)S(1)}, u32[]{:S(2)}, u32[]{:S(2)}) async-start(bf16[16,256,128]{2,1,0:T(8,128)(2,1)} %convolution_convert_fusion.12), calls=%async_computation | async-start | bytes 2097152 | tf_op jit(solution)/shard_map/all_to_all | solution.py:110
  79.4 2.7 fusion.53
  82.1 2.1 copy.159
  84.1 2.4 fusion.37
  87.7 1.9 fusion.155
  89.6 1.5 convolution_convert_fusion.4
  91.1 3.3 all-to-all-done
  94.4 4.9 all-to-all-start.5
  99.4 1.5 fusion.58
  102.1 1.6 fusion.35
  105.2 1.8 copy.150
  107.0 1.8 convert_element_type.202
  108.8 1.8 convert_element_type.195
  116.0 6.6 %all-to-all-start.6 = ((bf16[16,256,128]{2,1,0:T(8,128)(2,1)}), bf16[16,256,128]{2,1,0:T(8,128)(2,1)}, u32[]{:S(2)}, u32[]{:S(2)}) async-start(bf16[16,256,128]{2,1,0:T(8,128)(2,1)} %copy.184), calls=%async_computation.6 | async-start | bytes 2097152 | tf_op jit(solution)/shard_map/all_to_all | solution.py:170
  122.7 1.8 convolution_convert_fusion.8
  126.1 1.5 convolution_bitcast_fusion.3
  127.6 3.0 copy.175
  130.7 2.1 slice_bitcast_fusion.5
  132.7 4.1 all-to-all-done.6
  136.8 4.3 all-to-all-start.4
  141.2 2.2 fusion.92
  143.4 2.1 copy.178
  145.4 2.1 reshape.440
  147.5 1.8 convolution_convert_fusion.7
  150.9 1.5 convolution_bitcast_fusion.1
  152.4 3.0 copy.187
  155.5 6.6 %all-to-all-start.2 = ((bf16[16,256,128]{2,1,0:T(8,128)(2,1)}), bf16[16,256,128]{2,1,0:T(8,128)(2,1)}, u32[]{:S(2)}, u32[]{:S(2)}) async-start(bf16[16,256,128]{2,1,0:T(8,128)(2,1)} %convolution_convert_fusion.11), calls=%async_computation.2 | async-start | bytes 2097152 | tf_op jit(solution)/shard_map/all_to_all | solution.py:110
  163.3 1.9 fusion.90
  165.2 2.0 copy.190
  167.3 2.1 reshape.444
  169.3 1.5 convolution_convert_fusion.1
  175.4 5.2 all-to-all-start.7
  180.6 2.0 fusion.50
  183.9 1.7 convert_element_type.206
  185.7 2.0 fusion.55
  189.0 1.8 convert_element_type.199
  192.9 5.5 all-to-all-start.8
  200.5 2.1 fusion.44
  203.7 3.0 fusion.158
  206.7 4.3 all-to-all-done.8
  211.1 2.3 add_convert_fusion
  221.2 82.3 %all-reduce.15 = (f32[128]{0:T(128)S(1)}, f32[64]{0:T(128)S(1)}, f32[256]{0:T(256)S(1)}) all-reduce(f32[128]{0:T(128)S(1)} %convert_reduce_fusion, f32[64]{0:T(128)S(1)} %get-tuple-element.106, f32[256]{0:T(256)S(1)} %convert_reduce_fusion.2), channel_id=1, replica_groups=mesh['node'=16,'batch'=16] {'node','batch'}, use_global_device_ids=true, to_apply=%region_2.0 | all-reduce | flops 448 | bytes 3584 | tf_op jit(solution)/shard_map/psum | solution.py:222
  305.9 248.1 %all-reduce.19.cloned.1.call-done = (f32[128,128]{1,0:T(8,128)}, f32[64,320]{1,0:T(8,128)}, f32[256,64]{0,1:T(8,128)}) async-done(((f32[128,128]{1,0:T(8,128)}, f32[64,320]{1,0:T(8,128)}, f32[256,64]{0,1:T(8,128)}), (f32[128,128]{1,0:T(8,128)}, f32[64,320]{1,0:T(8,128)}, f32[256,64]{0,1:T(8,128)})) %all-reduce.19.cloned.1.call-update) | async-done | bytes 213008 | tf_op jit(solution)/shard_map/psum | solution.py:222
  554.1 1.5 broadcast_multiply_fusion
  (178 shorter events, 55.7 us)
Async XLA Ops:
  7.2 60.4 %copy-start = (bf16[16,128,128]{2,1,0:T(8,128)(2,1)S(1)}, bf16[16,128,128]{2,1,0:T(8,128)(2,1)}, u32[]{:S(2)}) copy-start(bf16[16,128,128]{2,1,0:T(8,128)(2,1)} %param.30) | copy-start | bytes 1572868
  8.6 28.7 %all-to-all-start.1 = ((bf16[16,1,4]{2,1,0:T(2,128)(2,1)}), bf16[16,1,4]{2,1,0:T(2,128)(2,1)S(1)}, u32[]{:S(2)}, u32[]{:S(2)}) async-start(bf16[16,1,4]{2,1,0:T(2,128)(2,1)} %compare_convert_fusion), calls=%async_computation.1 | async-start | bytes 16384 | tf_op jit(solution)/shard_map/all_to_all | solution.py:112
  17.7 2.0 copy-start.1
  17.8 2.0 copy-start.37
  19.8 2.0 copy-start.11
  21.8 2.2 copy-start.34
  24.0 2.0 copy-start.13
  26.0 2.2 copy-start.32
  26.0 3.0 copy-start.49
  26.0 3.0 copy-start.53
  28.2 0.7 copy-start.40
  28.2 0.8 copy-start.42
  29.3 1.7 copy-start.51
  30.2 0.7 copy-start.31
  30.2 2.3 copy-start.2
  31.0 0.7 copy-start.28
  31.7 2.2 copy-start.10
  31.7 2.2 copy-start.50
  33.9 10.1 %copy-start.52 = (f32[256]{0:T(256)S(1)}, f32[256]{0:T(256)}, u32[]{:S(2)}) copy-start(f32[256]{0:T(256)} %param.27) | copy-start | bytes 3076
  37.3 35.4 %all-to-all-start.3 = ((bf16[16,256,128]{2,1,0:T(8,128)(2,1)}), bf16[16,256,128]{2,1,0:T(8,128)(2,1)}, u32[]{:S(2)}, u32[]{:S(2)}) async-start(bf16[16,256,128]{2,1,0:T(8,128)(2,1)} %convolution_convert_fusion.10), calls=%async_computation.3 | async-start | bytes 2097152 | tf_op jit(solution)/shard_map/all_to_all | solution.py:111
  67.6 1.5 copy-start.12
  69.2 1.8 copy-start.14
  72.7 21.7 %all-to-all-start = ((bf16[16,256,128]{2,1,0:T(8,128)(2,1)}), bf16[16,256,128]{2,1,0:T(8,128)(2,1)S(1)}, u32[]{:S(2)}, u32[]{:S(2)}) async-start(bf16[16,256,128]{2,1,0:T(8,128)(2,1)} %convolution_convert_fusion.12), calls=%async_computation | async-start | bytes 2097152 | tf_op jit(solution)/shard_map/all_to_all | solution.py:110
  79.3 4.8 copy-start.29
  87.7 6.7 %copy-start.9 = (bf16[256,4,128]{2,1,0:T(4,128)(2,1)}, bf16[256,4,128]{2,1,0:T(4,128)(2,1)S(1)}, u32[]{:S(2)}) copy-start(bf16[256,4,128]{2,1,0:T(4,128)(2,1)S(1)} %copy.160) | copy-start | bytes 786436
  94.4 21.6 %all-to-all-start.5 = ((bf16[16,256,128]{2,1,0:T(8,128)(2,1)}), bf16[16,256,128]{2,1,0:T(8,128)(2,1)}, u32[]{:S(2)}, u32[]{:S(2)}) async-start(bf16[16,256,128]{2,1,0:T(8,128)(2,1)} %copy.172), calls=%async_computation.5 | async-start | bytes 2097152 | tf_op jit(solution)/shard_map/all_to_all | solution.py:167
  99.4 2.8 copy-start.30
  103.7 0.7 copy-start.26
  104.4 6.1 %copy-start.3 = (bf16[1,4,320,512]{3,2,1,0:T(8,128)(2,1)S(1)}, bf16[1,4,320,512]{3,2,1,0:T(8,128)(2,1)}, u32[]{:S(2)}) copy-start(bf16[1,4,320,512]{3,2,1,0:T(8,128)(2,1)} %get-tuple-element.89) | copy-start | bytes 3932164
  110.6 2.6 copy-start.4
  116.0 20.8 %all-to-all-start.6 = ((bf16[16,256,128]{2,1,0:T(8,128)(2,1)}), bf16[16,256,128]{2,1,0:T(8,128)(2,1)}, u32[]{:S(2)}, u32[]{:S(2)}) async-start(bf16[16,256,128]{2,1,0:T(8,128)(2,1)} %copy.184), calls=%async_computation.6 | async-start | bytes 2097152 | tf_op jit(solution)/shard_map/all_to_all | solution.py:170
  122.6 1.8 copy-start.19
  122.6 1.8 copy-start.20
  122.6 1.8 copy-start.23
  122.7 1.8 copy-start.24
  124.5 1.6 copy-start.38
  136.8 18.7 %all-to-all-start.4 = ((bf16[16,256,128]{2,1,0:T(8,128)(2,1)}), bf16[16,256,128]{2,1,0:T(8,128)(2,1)}, u32[]{:S(2)}, u32[]{:S(2)}) async-start(bf16[16,256,128]{2,1,0:T(8,128)(2,1)} %convolution_convert_fusion.9), calls=%async_computation.4 | async-start | bytes 2097152 | tf_op jit(solution)/shard_map/all_to_all | solution.py:111
  147.5 1.8 copy-start.17
  147.5 1.8 copy-start.18
  147.5 1.8 copy-start.21
  147.5 1.8 copy-start.22
  149.3 1.6 copy-start.35
  150.2 0.7 copy-start.7
  155.5 19.9 %all-to-all-start.2 = ((bf16[16,256,128]{2,1,0:T(8,128)(2,1)}), bf16[16,256,128]{2,1,0:T(8,128)(2,1)}, u32[]{:S(2)}, u32[]{:S(2)}) async-start(bf16[16,256,128]{2,1,0:T(8,128)(2,1)} %convolution_convert_fusion.11), calls=%async_computation.2 | async-start | bytes 2097152 | tf_op jit(solution)/shard_map/all_to_all | solution.py:110
  169.3 2.8 copy-start.8
  175.4 17.5 %all-to-all-start.7 = ((bf16[16,256,128]{2,1,0:T(8,128)(2,1)}), bf16[16,256,128]{2,1,0:T(8,128)(2,1)}, u32[]{:S(2)}, u32[]{:S(2)}) async-start(bf16[16,256,128]{2,1,0:T(8,128)(2,1)} %copy.191), calls=%async_computation.7 | async-start | bytes 2097152 | tf_op jit(solution)/shard_map/all_to_all | solution.py:167
  180.5 2.0 copy-start.25
  180.6 2.0 copy-start.36
  180.6 2.0 copy-start.44
  180.6 2.0 copy-start.45
  185.7 2.0 copy-start.27
  185.7 2.0 copy-start.39
  185.7 2.0 copy-start.46
  185.7 2.0 copy-start.47
  192.9 18.2 %all-to-all-start.8 = ((bf16[16,256,128]{2,1,0:T(8,128)(2,1)}), bf16[16,256,128]{2,1,0:T(8,128)(2,1)}, u32[]{:S(2)}, u32[]{:S(2)}) async-start(bf16[16,256,128]{2,1,0:T(8,128)(2,1)} %copy.192), calls=%async_computation.8 | async-start | bytes 2097152 | tf_op jit(solution)/shard_map/all_to_all | solution.py:170
  198.4 4.2 copy-start.48
  198.4 4.2 copy-start.54
  198.4 355.6 %all-reduce.19.cloned.1.call-start = ((), (), s32[]{:S(2)}) async-start(), calls=%async_computation.9 | async-start | bytes 458752 | tf_op jit(solution)/shard_map/psum | solution.py:222
  198.5 4.1 copy-start.33
  213.4 2.7 copy-start.15
  213.4 2.7 copy-start.16
  217.6 1.0 copy-start.41
  217.6 1.0 copy-start.43
  219.9 1.0 copy-start.5
  (1 other events, 0.7 us)
Sparse Core Ops, SparseCore 0:
  304.7 249.2 all-reduce.18
where the time goes:
time: 568 us; the launch traced here: 565 us
  waiting for transfers between devices  262 us (46%)
  local copies, waits for them, and re-layouts  83.4 us (15%)
  blocking collectives  82.3 us (14%)
  starting transfers between devices  54.1 us (10%)
  matrix products  52.7 us (9%)
  other arithmetic  15.6 us (3%)
  between operations  14.8 us (3%)
    psum x1, waiting for transfers between devices, shards(): lax.psum((grad_wconv, grad_bconv, grad_mix, grad_bmix, grad_skip, grad_bs...  248 us
    psum x1, blocking collectives, shards(): lax.psum((grad_wconv, grad_bconv, grad_mix, grad_bmix, grad_skip, grad_bs...  82.3 us
    unnamed x120, local copies, waits for them, and re-layouts  22.9 us
    all_to_all x2, starting transfers between devices, push_hop(): lax.all_to_all(part_fwd, 'node', split_axis=0, concat_axis=0, tiled=True)  13.2 us
    all_to_all x2, starting transfers between devices, fetch_rows(): lax.all_to_all(pick_blocks(grad_bwd, recv_dst), 'node', split_axis=0, con...  12.2 us
    dot_general x7, matrix products, place_blocks(): jnp.einsum('qi,qmc->mic', chooser, pieces, preferred_element_type=jnp.flo...  11.4 us
  transfers between devices with their start and end apart: 10, of which 6 were waited for; matrix products, arithmetic and copies ran while one was open for 23% of the time, Pallas kernels for 0%

commit v1 on v0

--- a/solution.py
+++ b/solution.py
@@ -65,6 +65,33 @@
 
 def tile_backward(pieces, tile_vals):
     return jnp.einsum("qma,qac->qmc", pieces, tile_vals, preferred_element_type=jnp.float32)
+
+
+def exchange_sum(pieces):
+    sizes = [piece.size for piece in pieces]
+    flat = jnp.concatenate([piece.reshape(-1) for piece in pieces])
+    node_count = lax.axis_size("node")
+    batch_count = lax.axis_size("batch")
+    group = node_count * batch_count
+    total = flat.shape[0]
+    padded = -(-total // group) * group
+    flat = jnp.pad(flat, (0, padded - total))
+    part = lax.all_to_all(
+        flat.reshape(node_count, padded // node_count), "node", 0, 0, tiled=True
+    ).sum(axis=0)
+    part = lax.all_to_all(
+        part.reshape(batch_count, padded // group), "batch", 0, 0, tiled=True
+    ).sum(axis=0)
+    spread = jnp.broadcast_to(part[None], (batch_count, padded // group))
+    spread = lax.all_to_all(spread, "batch", 0, 0, tiled=True).reshape(padded // node_count)
+    spread = jnp.broadcast_to(spread[None], (node_count, padded // node_count))
+    spread = lax.all_to_all(spread, "node", 0, 0, tiled=True).reshape(padded)
+    results = []
+    offset = 0
+    for piece, size in zip(pieces, sizes):
+        results.append(spread[offset : offset + size].reshape(piece.shape))
+        offset += size
+    return tuple(results)
 
 
 def shards(
@@ -219,9 +246,7 @@
         "wton,wtcn->oc", grad_pre, paired_taps, preferred_element_type=jnp.float32
     )
     grad_bconv = jnp.sum(grad_pre.astype(jnp.float32), axis=(0, 1, 3))
-    totals = lax.psum(
-        (grad_wconv, grad_bconv, grad_mix, grad_bmix, grad_skip, grad_bskip), ("node", "batch")
-    )
+    totals = exchange_sum((grad_wconv, grad_bconv, grad_mix, grad_bmix, grad_skip, grad_bskip))
     grad_count = (
         windows * lax.axis_size("batch") * local_nodes * lax.axis_size("node") * output_steps
     )

time: 568 us -> 289 us (0.51)
  waiting for transfers between devices: 262 us -> 32.5 us
  blocking collectives: 82.3 us -> 38.2 us
  between operations: 14.8 us -> 1.48 us
    psum x1 -> x0, waiting for transfers between devices: 248 us -> none  [shards(): lax.psum((grad_wconv, grad_bconv, grad_mix, grad_bmix, grad_skip, grad_bs...]
    psum x1 -> x0, blocking collectives: 82.3 us -> none  [shards(): lax.psum((grad_wconv, grad_bconv, grad_mix, grad_bmix, grad_skip, grad_bs...]
    all_to_all x0 -> x2, blocking collectives: none -> 38.2 us  [the longest x1 24.5 us: exchange_sum(): lax.all_to_all(part.reshape(batch_count, padded // group), 'batch', 0, 0,...]
    all_to_all x0 -> x2, waiting for transfers between devices: none -> 11.4 us  [the longest x1 6 us: exchange_sum(): spread = lax.all_to_all(spread, 'node', 0, 0, tiled=True).reshape(padded)]
    all_to_all x2, waiting for transfers between devices: 0.01 us -> 11.2 us  [push_hop(): lax.all_to_all(part_bwd, 'node', split_axis=0, concat_axis=0, tiled=True)]
    all_to_all x2, waiting for transfers between devices: 8.41 us -> 0.01 us  [fetch_rows(): lax.all_to_all(pick_blocks(grad_bwd, recv_dst), 'node', split_axis=0, con...]
    all_to_all x0 -> x2, starting transfers between devices: none -> 7.2 us  [the longest x1 3.68 us: exchange_sum(): lax.all_to_all(spread, 'batch', 0, 0, tiled=True)]
    unnamed x120 -> x129, local copies, waits for them, and re-layouts: 22.9 us -> 18.4 us
  transfers between devices with their start and end apart: 10 -> 11, of which waited for: 6 -> 7; matrix products, arithmetic and copies ran while one was open for 23% -> 46% of each run, Pallas kernels for 0% -> 0%
where the time goes in v1:
time: 289 us; the launch traced here: 286 us
  local copies, waits for them, and re-layouts  87.6 us (30%)
  starting transfers between devices  56.9 us (20%)
  matrix products  54.8 us (19%)
  blocking collectives  38.2 us (13%)
  waiting for transfers between devices  32.5 us (11%)
  other arithmetic  14.7 us (5%)
    all_to_all x1, blocking collectives, exchange_sum(): lax.all_to_all(part.reshape(batch_count, padded // group), 'batch', 0, 0,...  24.5 us
    unnamed x129, local copies, waits for them, and re-layouts  18.4 us
    all_to_all x1, blocking collectives, exchange_sum(): lax.all_to_all(flat.reshape(node_count, padded // node_count), 'node', 0,...  13.8 us
    all_to_all x2, starting transfers between devices, push_hop(): lax.all_to_all(part_bwd, 'node', split_axis=0, concat_axis=0, tiled=True)  13.4 us
    dot_general x7, matrix products, place_blocks(): jnp.einsum('qi,qmc->mic', chooser, pieces, preferred_element_type=jnp.flo...  12.1 us
    all_to_all x2, starting transfers between devices, fetch_rows(): lax.all_to_all(pick_blocks(grad_fwd, recv_dst), 'node', split_axis=0, con...  11.3 us
    all_to_all x2, waiting for transfers between devices, push_hop(): lax.all_to_all(part_bwd, 'node', split_axis=0, concat_axis=0, tiled=True)  11.2 us
    transpose x4, local copies, waits for them, and re-layouts, band_transpose(): jnp.einsum('mia,iak->mik', gradient.reshape(row_count, blocks, tile_width...  9.53 us
  transfers between devices with their start and end apart: 11, of which 7 were waited for; matrix products, arithmetic and copies ran while one was open for 46% of the time, Pallas kernels for 0%

profile of v1, /device:TPU:1, one launch (start us, length us, event | category | flops | bytes accessed | tf_op | source)
XLA Modules:
  0.0 286.1 jit_solution(18378273701421088832)
XLA Ops:
  2.1 7.6 %all-to-all-start.1 = ((bf16[16,1,4]{2,1,0:T(2,128)(2,1)}), bf16[16,1,4]{2,1,0:T(2,128)(2,1)S(1)}, u32[]{:S(2)}, u32[]{:S(2)}) async-start(bf16[16,1,4]{2,1,0:T(2,128)(2,1)} %compare_convert_fusion), calls=%async_computation.1 | async-start | bytes 16384 | tf_op jit(solution)/shard_map/all_to_all | solution.py:139
  9.6 1.5 convolution_bitcast_fusion.1
  11.2 1.6 copy-done.1
  13.3 1.7 copy.282
  15.0 2.2 fusion.153
  20.0 1.7 copy.294
  21.7 2.1 fusion.152
  23.8 1.9 slice.261
  29.3 2.0 copy.321
  31.3 2.0 copy.322
  34.3 2.1 reshape.482
  36.4 2.0 copy.326
  45.9 6.8 %all-to-all-start.3 = ((bf16[16,256,128]{2,1,0:T(8,128)(2,1)}), bf16[16,256,128]{2,1,0:T(8,128)(2,1)}, u32[]{:S(2)}, u32[]{:S(2)}) async-start(bf16[16,256,128]{2,1,0:T(8,128)(2,1)} %convolution_convert_fusion.10), calls=%async_computation.3 | async-start | bytes 2097152 | tf_op jit(solution)/shard_map/all_to_all | solution.py:138
  52.7 1.7 fusion.43
  54.5 1.8 fusion.157
  59.7 8.6 %all-to-all-done.3 = bf16[16,256,128]{2,1,0:T(8,128)(2,1)} async-done(((bf16[16,256,128]{2,1,0:T(8,128)(2,1)}), bf16[16,256,128]{2,1,0:T(8,128)(2,1)}, u32[]{:S(2)}, u32[]{:S(2)}) %all-to-all-start.3) | async-done | bytes 1048608 | tf_op jit(solution)/shard_map/all_to_all | solution.py:138
  68.2 4.4 %all-to-all-start = ((bf16[16,256,128]{2,1,0:T(8,128)(2,1)}), bf16[16,256,128]{2,1,0:T(8,128)(2,1)S(1)}, u32[]{:S(2)}, u32[]{:S(2)}) async-start(bf16[16,256,128]{2,1,0:T(8,128)(2,1)} %convolution_convert_fusion.12), calls=%async_computation | async-start | bytes 2097152 | tf_op jit(solution)/shard_map/all_to_all | solution.py:137
  74.4 2.8 fusion.53
  77.2 2.1 copy.273
  79.2 2.5 fusion.37
  82.9 1.6 convolution_convert_fusion.4
  84.4 3.1 %all-to-all-done = bf16[16,256,128]{2,1,0:T(8,128)(2,1)S(1)} async-done(((bf16[16,256,128]{2,1,0:T(8,128)(2,1)}), bf16[16,256,128]{2,1,0:T(8,128)(2,1)S(1)}, u32[]{:S(2)}, u32[]{:S(2)}) %all-to-all-start) | async-done | bytes 1048608 | tf_op jit(solution)/shard_map/all_to_all | solution.py:137
  87.6 4.7 %all-to-all-start.5 = ((bf16[16,256,128]{2,1,0:T(8,128)(2,1)}), bf16[16,256,128]{2,1,0:T(8,128)(2,1)}, u32[]{:S(2)}, u32[]{:S(2)}) async-start(bf16[16,256,128]{2,1,0:T(8,128)(2,1)} %copy.286), calls=%async_computation.5 | async-start | bytes 2097152 | tf_op jit(solution)/shard_map/all_to_all | solution.py:194
  95.0 2.3 fusion.35
  98.5 1.9 fusion.155
  103.8 2.6 all-to-all-done.5
  106.4 4.4 %all-to-all-start.6 = ((bf16[16,256,128]{2,1,0:T(8,128)(2,1)}), bf16[16,256,128]{2,1,0:T(8,128)(2,1)}, u32[]{:S(2)}, u32[]{:S(2)}) async-start(bf16[16,256,128]{2,1,0:T(8,128)(2,1)} %copy.298), calls=%async_computation.6 | async-start | bytes 2097152 | tf_op jit(solution)/shard_map/all_to_all | solution.py:197
  110.8 1.8 fusion.156
  112.6 1.8 convert_element_type.197
  114.4 1.7 convert_element_type.204
  117.3 1.6 convolution_convert_fusion.8
  120.6 1.5 convolution_bitcast_fusion.4
  122.0 3.1 %copy.289 = f32[256,4,384]{0,2,1:T(8,128)} copy(f32[256,4,384]{2,0,1:T(8,128)} %convolution_bitcast_fusion.4) | data formatting | bytes 3145728 | tf_op jit(solution)/shard_map/mia,iak->mik/transpose | solution.py:34
  125.1 6.6 %all-to-all-start.4 = ((bf16[16,256,128]{2,1,0:T(8,128)(2,1)}), bf16[16,256,128]{2,1,0:T(8,128)(2,1)}, u32[]{:S(2)}, u32[]{:S(2)}) async-start(bf16[16,256,128]{2,1,0:T(8,128)(2,1)} %convolution_convert_fusion.9), calls=%async_computation.4 | async-start | bytes 2097152 | tf_op jit(solution)/shard_map/all_to_all | solution.py:138
  132.9 1.9 fusion.92
  134.9 2.0 copy.292
  136.9 2.1 reshape.485
  139.0 1.8 convolution_convert_fusion.7
  140.8 1.6 fusion.40
  142.4 2.7 all-to-all-done.4
  145.1 4.3 %all-to-all-start.2 = ((bf16[16,256,128]{2,1,0:T(8,128)(2,1)}), bf16[16,256,128]{2,1,0:T(8,128)(2,1)}, u32[]{:S(2)}, u32[]{:S(2)}) async-start(bf16[16,256,128]{2,1,0:T(8,128)(2,1)} %convolution_convert_fusion.11), calls=%async_computation.2 | async-start | bytes 2097152 | tf_op jit(solution)/shard_map/all_to_all | solution.py:137
  149.4 2.6 convolution_bitcast_fusion.2
  152.0 3.1 %copy.301 = f32[256,4,384]{0,2,1:T(8,128)} copy(f32[256,4,384]{2,0,1:T(8,128)} %convolution_bitcast_fusion.2) | data formatting | bytes 3145728 | tf_op jit(solution)/shard_map/mia,iak->mik/transpose | solution.py:34
  156.3 1.9 fusion.90
  158.2 2.1 copy.304
  160.3 2.0 reshape.489
  165.0 6.6 %all-to-all-start.7 = ((bf16[16,256,128]{2,1,0:T(8,128)(2,1)}), bf16[16,256,128]{2,1,0:T(8,128)(2,1)}, u32[]{:S(2)}, u32[]{:S(2)}) async-start(bf16[16,256,128]{2,1,0:T(8,128)(2,1)} %copy.305), calls=%async_computation.7 | async-start | bytes 2097152 | tf_op jit(solution)/shard_map/all_to_all | solution.py:194
  174.4 2.0 fusion.50
  176.4 2.7 fusion.55
  180.2 4.0 %all-to-all-done.7 = bf16[16,256,128]{2,1,0:T(8,128)(2,1)} async-done(((bf16[16,256,128]{2,1,0:T(8,128)(2,1)}), bf16[16,256,128]{2,1,0:T(8,128)(2,1)}, u32[]{:S(2)}, u32[]{:S(2)}) %all-to-all-start.7) | async-done | bytes 1048608 | tf_op jit(solution)/shard_map/all_to_all | solution.py:194
  184.2 4.3 %all-to-all-start.8 = ((bf16[16,256,128]{2,1,0:T(8,128)(2,1)}), bf16[16,256,128]{2,1,0:T(8,128)(2,1)}, u32[]{:S(2)}, u32[]{:S(2)}) async-start(bf16[16,256,128]{2,1,0:T(8,128)(2,1)} %copy.306), calls=%async_computation.8 | async-start | bytes 2097152 | tf_op jit(solution)/shard_map/all_to_all | solution.py:197
  188.6 2.6 fusion.36
  192.1 1.8 convert_element_type.208
  193.9 1.9 copy.270
  195.7 1.8 convert_element_type.201
  201.7 3.0 %fusion.158 = f32[16,256,128]{2,1,0:T(8,128)} fusion(bf16[16,256,128]{2,1,0:T(8,128)(2,1)} %all-to-all-done.7, bf16[16,128,128]{2,1,0:T(8,128)(2,1)S(1)} %copy-done), kind=kOutput, calls=%fused_computation.206 | convolution fusion | flops 134217728 | bytes 3670016 | tf_op jit(solution)/shard_map/qma,qac->qmc/dot_general | solution.py:67
  204.7 2.3 add_convert_fusion
  208.8 1.9 fusion.83
  217.7 13.8 %all_to_all.80 = f32[16,1,3360]{2,1,0:T(1,128)} all-to-all(f32[16,1,3360]{2,1,0:T(1,128)S(1)} %all_to_all.61), channel_id=1, replica_groups=mesh['node'=16,'batch'=16] {'node'}, dimensions={0} | all-to-all | bytes 430080 | tf_op jit(solution)/shard_map/all_to_all | solution.py:79
  232.7 24.5 %all_to_all.81 = f32[16,1,210]{2,1,0:T(1,128)S(1)} all-to-all(f32[16,1,210]{2,1,0:T(1,128)S(1)} %all_to_all.63), channel_id=1, replica_groups=mesh['node'=16,'batch'=16] {'batch'}, dimensions={0} | all-to-all | bytes 26880 | tf_op jit(solution)/shard_map/all_to_all | solution.py:82
  257.8 3.7 %all-to-all-start.11 = ((f32[16,1,210]{2,1,0:T(1,128)}), f32[16,1,210]{2,1,0:T(1,128)S(1)}, u32[]{:S(2)}, u32[]{:S(2)}) async-start(f32[16,1,210]{2,1,0:T(1,128)} %broadcast_in_dim.6), calls=%async_computation.11 | async-start | bytes 32768 | tf_op jit(solution)/shard_map/all_to_all | solution.py:86
  263.4 5.4 %all-to-all-done.11 = f32[16,1,210]{2,1,0:T(1,128)S(1)} async-done(((f32[16,1,210]{2,1,0:T(1,128)}), f32[16,1,210]{2,1,0:T(1,128)S(1)}, u32[]{:S(2)}, u32[]{:S(2)}) %all-to-all-start.11) | async-done | bytes 13472 | tf_op jit(solution)/shard_map/all_to_all | solution.py:86
  269.8 3.5 %all-to-all-start.12 = ((f32[16,1,3360]{2,1,0:T(1,128)}), f32[16,1,3360]{2,1,0:T(1,128)S(1)}, u32[]{:S(2)}, u32[]{:S(2)}) async-start(f32[16,1,3360]{2,1,0:T(1,128)} %broadcast_in_dim.8), calls=%async_computation.12 | async-start | bytes 442368 | tf_op jit(solution)/shard_map/all_to_all | solution.py:88
  275.2 6.0 %all-to-all-done.12 = f32[16,1,3360]{2,1,0:T(1,128)S(1)} async-done(((f32[16,1,3360]{2,1,0:T(1,128)}), f32[16,1,3360]{2,1,0:T(1,128)S(1)}, u32[]{:S(2)}, u32[]{:S(2)}) %all-to-all-start.12) | async-done | bytes 215072 | tf_op jit(solution)/shard_map/all_to_all | solution.py:88
  (207 shorter events, 67.0 us)
Async XLA Ops:
  0.6 55.7 %copy-start = (bf16[16,128,128]{2,1,0:T(8,128)(2,1)S(1)}, bf16[16,128,128]{2,1,0:T(8,128)(2,1)}, u32[]{:S(2)}) copy-start(bf16[16,128,128]{2,1,0:T(8,128)(2,1)} %param.30) | copy-start | bytes 1572868
  2.1 43.8 %all-to-all-start.1 = ((bf16[16,1,4]{2,1,0:T(2,128)(2,1)}), bf16[16,1,4]{2,1,0:T(2,128)(2,1)S(1)}, u32[]{:S(2)}, u32[]{:S(2)}) async-start(bf16[16,1,4]{2,1,0:T(2,128)(2,1)} %compare_convert_fusion), calls=%async_computation.1 | async-start | bytes 16384 | tf_op jit(solution)/shard_map/all_to_all | solution.py:139
  9.6 3.3 %copy-start.36 = (bf16[512,384]{1,0:T(8,128)(2,1)S(1)}, bf16[512,384]{1,0:T(8,128)(2,1)}, u32[]{:S(2)}) copy-start(bf16[512,384]{1,0:T(8,128)(2,1)} %param.28) | copy-start | bytes 1179652
  11.2 1.6 copy-start.1
  12.9 2.1 copy-start.13
  15.0 3.3 %copy-start.2 = (f32[1,4,320,512]{3,2,1,0:T(8,128)S(1)}, f32[1,4,320,512]{3,2,1,0:T(8,128)}, u32[]{:S(2)}) copy-start(f32[1,4,320,512]{3,2,1,0:T(8,128)} %copy-done.1) | copy-start | bytes 7864324
  18.3 1.3 copy-start.34
  19.6 2.1 copy-start.15
  21.7 4.0 %copy-start.32 = (bf16[1,6,64,512]{3,2,1,0:T(8,128)(2,1)S(1)}, bf16[1,6,64,512]{3,2,1,0:T(8,128)(2,1)}, u32[]{:S(2)}) copy-start(bf16[1,6,64,512]{3,2,1,0:T(8,128)(2,1)} %param.21) | copy-start | bytes 1179652
  21.7 4.8 %copy-start.48 = (bf16[128,128]{1,0:T(8,128)(2,1)S(1)}, bf16[128,128]{1,0:T(8,128)(2,1)}, u32[]{:S(2)}) copy-start(bf16[128,128]{1,0:T(8,128)(2,1)} %param.22) | copy-start | bytes 98308
  21.7 4.8 %copy-start.57 = (f32[128]{0:T(128)S(1)}, f32[128]{0:T(128)}, u32[]{:S(2)}) copy-start(f32[128]{0:T(128)} %param.23) | copy-start | bytes 1540
  26.5 1.3 copy-start.11
  27.7 5.6 %copy-start.30 = (bf16[1,4,64,512]{3,2,1,0:T(8,128)(2,1)}, bf16[1,4,64,512]{3,2,1,0:T(8,128)(2,1)S(1)}, u32[]{:S(2)}) copy-start(bf16[1,4,64,512]{3,2,1,0:T(8,128)(2,1)S(1)} %get-tuple-element.102) | copy-start | bytes 786436
  34.3 4.1 %copy-start.31 = (f32[256,3,1,128]{0,3,2,1:T(8,128)S(1)}, f32[256,3,1,128]{0,3,2,1:T(8,128)}, u32[]{:S(2)}) copy-start(f32[256,3,1,128]{0,3,2,1:T(8,128)} %get-tuple-element.113) | copy-start | bytes 1179652
  34.3 5.1 %copy-start.21 = (f32[256,4,1,128]{0,3,2,1:T(8,128)S(1)}, f32[256,4,1,128]{0,3,2,1:T(8,128)}, u32[]{:S(2)}) copy-start(f32[256,4,1,128]{0,3,2,1:T(8,128)} %slice.261) | copy-start | bytes 1572868
  36.4 4.0 %copy-start.26 = (f32[1,4,64,512]{3,2,1,0:T(8,128)S(1)}, f32[1,4,64,512]{3,2,1,0:T(8,128)}, u32[]{:S(2)}) copy-start(f32[1,4,64,512]{3,2,1,0:T(8,128)} %get-tuple-element.104) | copy-start | bytes 1572868
  38.5 3.7 %copy-start.53 = (s32[16]{0:T(128)S(1)}, s32[16]{0:T(128)}, u32[]{:S(2)}) copy-start(s32[16]{0:T(128)} %param.32) | copy-start | bytes 196
  40.5 2.3 copy-start.3
  44.2 8.5 %copy-start.12 = (bf16[1,256,512]{2,1,0:T(8,128)(2,1)S(1)}, bf16[1,256,512]{2,1,0:T(8,128)(2,1)}, u32[]{:S(2)}) copy-start(bf16[1,256,512]{2,1,0:T(8,128)(2,1)} %param.35) | copy-start | bytes 786436
  45.9 6.9 %copy-start.50 = (bf16[256,64]{0,1:T(8,128)(2,1)S(1)}, bf16[256,64]{0,1:T(8,128)(2,1)}, u32[]{:S(2)}) copy-start(bf16[256,64]{0,1:T(8,128)(2,1)} %param.26) | copy-start | bytes 98308
  45.9 22.4 %all-to-all-start.3 = ((bf16[16,256,128]{2,1,0:T(8,128)(2,1)}), bf16[16,256,128]{2,1,0:T(8,128)(2,1)}, u32[]{:S(2)}, u32[]{:S(2)}) async-start(bf16[16,256,128]{2,1,0:T(8,128)(2,1)} %convolution_convert_fusion.10), calls=%async_computation.3 | async-start | bytes 2097152 | tf_op jit(solution)/shard_map/all_to_all | solution.py:138
  54.5 3.4 %copy-start.14 = (bf16[256,4,128]{2,1,0:T(4,128)(2,1)S(1)}, bf16[256,4,128]{2,1,0:T(4,128)(2,1)}, u32[]{:S(2)}) copy-start(bf16[256,4,128]{2,1,0:T(4,128)(2,1)} %copy-done.13) | copy-start | bytes 786436
  59.6 13.0 %copy-start.16 = (bf16[256,4,128]{2,1,0:T(4,128)(2,1)S(1)}, bf16[256,4,128]{2,1,0:T(4,128)(2,1)}, u32[]{:S(2)}) copy-start(bf16[256,4,128]{2,1,0:T(4,128)(2,1)} %copy-done.15) | copy-start | bytes 786436
  68.2 19.3 %all-to-all-start = ((bf16[16,256,128]{2,1,0:T(8,128)(2,1)}), bf16[16,256,128]{2,1,0:T(8,128)(2,1)S(1)}, u32[]{:S(2)}, u32[]{:S(2)}) async-start(bf16[16,256,128]{2,1,0:T(8,128)(2,1)} %convolution_convert_fusion.12), calls=%async_computation | async-start | bytes 2097152 | tf_op jit(solution)/shard_map/all_to_all | solution.py:137
  74.4 4.8 %copy-start.28 = (bf16[256,4,128]{2,0,1:T(8,128)(2,1)S(1)}, bf16[256,4,128]{2,0,1:T(8,128)(2,1)}, u32[]{:S(2)}) copy-start(bf16[256,4,128]{2,0,1:T(8,128)(2,1)} %copy.257) | copy-start | bytes 786436
  82.8 4.7 %copy-start.9 = (bf16[256,4,128]{2,1,0:T(4,128)(2,1)}, bf16[256,4,128]{2,1,0:T(4,128)(2,1)S(1)}, u32[]{:S(2)}) copy-start(bf16[256,4,128]{2,1,0:T(4,128)(2,1)S(1)} %copy.274) | copy-start | bytes 786436
  87.6 18.9 %all-to-all-start.5 = ((bf16[16,256,128]{2,1,0:T(8,128)(2,1)}), bf16[16,256,128]{2,1,0:T(8,128)(2,1)}, u32[]{:S(2)}, u32[]{:S(2)}) async-start(bf16[16,256,128]{2,1,0:T(8,128)(2,1)} %copy.286), calls=%async_computation.5 | async-start | bytes 2097152 | tf_op jit(solution)/shard_map/all_to_all | solution.py:194
  92.2 2.7 copy-start.29
  97.3 3.7 %copy-start.5 = (bf16[16,256,128]{2,0,1:T(8,128)(2,1)S(1)}, bf16[16,256,128]{2,0,1:T(8,128)(2,1)}, u32[]{:S(2)}) copy-start(bf16[16,256,128]{2,0,1:T(8,128)(2,1)} %convolution_convert_fusion.4) | copy-start | bytes 3145732
  98.5 3.9 %copy-start.10 = (bf16[256,4,128]{2,1,0:T(4,128)(2,1)}, bf16[256,4,128]{2,1,0:T(4,128)(2,1)S(1)}, u32[]{:S(2)}) copy-start(bf16[256,4,128]{2,1,0:T(4,128)(2,1)S(1)} %copy.264) | copy-start | bytes 786436
  103.8 12.3 %copy-start.4 = (bf16[1,4,320,512]{3,2,1,0:T(8,128)(2,1)S(1)}, bf16[1,4,320,512]{3,2,1,0:T(8,128)(2,1)}, u32[]{:S(2)}) copy-start(bf16[1,4,320,512]{3,2,1,0:T(8,128)(2,1)} %get-tuple-element.101) | copy-start | bytes 3932164
  106.4 18.7 %all-to-all-start.6 = ((bf16[16,256,128]{2,1,0:T(8,128)(2,1)}), bf16[16,256,128]{2,1,0:T(8,128)(2,1)}, u32[]{:S(2)}, u32[]{:S(2)}) async-start(bf16[16,256,128]{2,1,0:T(8,128)(2,1)} %copy.298), calls=%async_computation.6 | async-start | bytes 2097152 | tf_op jit(solution)/shard_map/all_to_all | solution.py:197
  116.1 2.8 copy-start.19
  116.1 2.8 copy-start.20
  116.1 2.8 copy-start.24
  116.1 2.8 copy-start.25
  119.0 1.6 copy-start.37
  125.1 19.9 %all-to-all-start.4 = ((bf16[16,256,128]{2,1,0:T(8,128)(2,1)}), bf16[16,256,128]{2,1,0:T(8,128)(2,1)}, u32[]{:S(2)}, u32[]{:S(2)}) async-start(bf16[16,256,128]{2,1,0:T(8,128)(2,1)} %convolution_convert_fusion.9), calls=%async_computation.4 | async-start | bytes 2097152 | tf_op jit(solution)/shard_map/all_to_all | solution.py:138
  139.0 1.8 copy-start.17
  139.0 1.8 copy-start.18
  139.0 1.8 copy-start.22
  139.0 1.8 copy-start.23
  145.1 19.9 %all-to-all-start.2 = ((bf16[16,256,128]{2,1,0:T(8,128)(2,1)}), bf16[16,256,128]{2,1,0:T(8,128)(2,1)}, u32[]{:S(2)}, u32[]{:S(2)}) async-start(bf16[16,256,128]{2,1,0:T(8,128)(2,1)} %convolution_convert_fusion.11), calls=%async_computation.2 | async-start | bytes 2097152 | tf_op jit(solution)/shard_map/all_to_all | solution.py:137
  165.0 19.2 %all-to-all-start.7 = ((bf16[16,256,128]{2,1,0:T(8,128)(2,1)}), bf16[16,256,128]{2,1,0:T(8,128)(2,1)}, u32[]{:S(2)}, u32[]{:S(2)}) async-start(bf16[16,256,128]{2,1,0:T(8,128)(2,1)} %copy.305), calls=%async_computation.7 | async-start | bytes 2097152 | tf_op jit(solution)/shard_map/all_to_all | solution.py:194
  174.4 4.7 %copy-start.27 = (bf16[256,4,128]{0,2,1:T(8,128)(2,1)S(1)}, bf16[256,4,128]{0,2,1:T(8,128)(2,1)}, u32[]{:S(2)}) copy-start(bf16[256,4,128]{0,2,1:T(8,128)(2,1)} %fusion.37) | copy-start | bytes 786436
  174.4 4.7 %copy-start.35 = (bf16[512,384]{1,0:T(8,128)(2,1)S(1)}, bf16[512,384]{1,0:T(8,128)(2,1)}, u32[]{:S(2)}) copy-start(bf16[512,384]{1,0:T(8,128)(2,1)} %param.29) | copy-start | bytes 1179652
  174.4 4.7 %copy-start.45 = (bf16[256,3,128]{0,2,1:T(8,128)(2,1)S(1)}, bf16[256,3,128]{0,2,1:T(8,128)(2,1)}, u32[]{:S(2)}) copy-start(bf16[256,3,128]{0,2,1:T(8,128)(2,1)} %get-tuple-element.120) | copy-start | bytes 589828
  174.4 4.7 %copy-start.46 = (bf16[256,3,128]{0,2,1:T(8,128)(2,1)S(1)}, bf16[256,3,128]{0,2,1:T(8,128)(2,1)}, u32[]{:S(2)}) copy-start(bf16[256,3,128]{0,2,1:T(8,128)(2,1)} %get-tuple-element.121) | copy-start | bytes 589828
  184.2 20.5 %all-to-all-start.8 = ((bf16[16,256,128]{2,1,0:T(8,128)(2,1)}), bf16[16,256,128]{2,1,0:T(8,128)(2,1)}, u32[]{:S(2)}, u32[]{:S(2)}) async-start(bf16[16,256,128]{2,1,0:T(8,128)(2,1)} %copy.306), calls=%async_computation.8 | async-start | bytes 2097152 | tf_op jit(solution)/shard_map/all_to_all | solution.py:197
  188.6 2.6 copy-start.43
  197.5 3.0 %copy-start.6 = (bf16[1,4,64,512]{3,2,1,0:T(8,128)(2,1)S(1)}, bf16[1,4,64,512]{3,2,1,0:T(8,128)(2,1)}, u32[]{:S(2)}) copy-start(bf16[1,4,64,512]{3,2,1,0:T(8,128)(2,1)} %param.34) | copy-start | bytes 786436
  210.7 1.0 copy-start.39
  210.7 1.0 copy-start.41
  210.9 1.7 copy-start.49
  213.0 1.0 copy-start.7
  213.0 1.2 copy-start.42
  213.0 1.2 copy-start.44
  213.9 47.5 %copy-start.51 = (bf16[256,64]{0,1:T(8,128)(2,1)S(1)}, bf16[256,64]{0,1:T(8,128)(2,1)}, u32[]{:S(2)}) copy-start(bf16[256,64]{0,1:T(8,128)(2,1)} %param.26) | copy-start | bytes 98308
  213.9 47.5 %copy-start.56 = (f32[256]{0:T(256)S(1)}, f32[256]{0:T(256)}, u32[]{:S(2)}) copy-start(f32[256]{0:T(256)} %param.27) | copy-start | bytes 3076
  215.8 57.6 %copy-start.33 = (bf16[1,6,64,512]{3,2,1,0:T(8,128)(2,1)S(1)}, bf16[1,6,64,512]{3,2,1,0:T(8,128)(2,1)}, u32[]{:S(2)}) copy-start(bf16[1,6,64,512]{3,2,1,0:T(8,128)(2,1)} %param.21) | copy-start | bytes 1179652
  215.8 57.6 %copy-start.47 = (bf16[64,320]{1,0:T(8,128)(2,1)S(1)}, bf16[64,320]{1,0:T(8,128)(2,1)}, u32[]{:S(2)}) copy-start(bf16[64,320]{1,0:T(8,128)(2,1)} %param.24) | copy-start | bytes 122884
  215.8 57.6 %copy-start.58 = (f32[64]{0:T(128)S(1)}, f32[64]{0:T(128)}, u32[]{:S(2)}) copy-start(f32[64]{0:T(128)} %param.25) | copy-start | bytes 772
  257.8 11.1 %all-to-all-start.11 = ((f32[16,1,210]{2,1,0:T(1,128)}), f32[16,1,210]{2,1,0:T(1,128)S(1)}, u32[]{:S(2)}, u32[]{:S(2)}) async-start(f32[16,1,210]{2,1,0:T(1,128)} %broadcast_in_dim.6), calls=%async_computation.11 | async-start | bytes 32768 | tf_op jit(solution)/shard_map/all_to_all | solution.py:86
  269.8 11.4 %all-to-all-start.12 = ((f32[16,1,3360]{2,1,0:T(1,128)}), f32[16,1,3360]{2,1,0:T(1,128)S(1)}, u32[]{:S(2)}, u32[]{:S(2)}) async-start(f32[16,1,3360]{2,1,0:T(1,128)} %broadcast_in_dim.8), calls=%async_computation.12 | async-start | bytes 442368 | tf_op jit(solution)/shard_map/all_to_all | solution.py:88
  (6 other events, 4.7 us)

commit v2 on v1

--- a/solution.py
+++ b/solution.py
@@ -72,19 +72,15 @@
     flat = jnp.concatenate([piece.reshape(-1) for piece in pieces])
     node_count = lax.axis_size("node")
     batch_count = lax.axis_size("batch")
-    group = node_count * batch_count
     total = flat.shape[0]
-    padded = -(-total // group) * group
+    padded = -(-total // node_count) * node_count
     flat = jnp.pad(flat, (0, padded - total))
     part = lax.all_to_all(
         flat.reshape(node_count, padded // node_count), "node", 0, 0, tiled=True
     ).sum(axis=0)
-    part = lax.all_to_all(
-        part.reshape(batch_count, padded // group), "batch", 0, 0, tiled=True
-    ).sum(axis=0)
-    spread = jnp.broadcast_to(part[None], (batch_count, padded // group))
-    spread = lax.all_to_all(spread, "batch", 0, 0, tiled=True).reshape(padded // node_count)
-    spread = jnp.broadcast_to(spread[None], (node_count, padded // node_count))
+    part = jnp.broadcast_to(part[None], (batch_count, padded // node_count))
+    part = lax.all_to_all(part, "batch", 0, 0, tiled=True).sum(axis=0)
+    spread = jnp.broadcast_to(part[None], (node_count, padded // node_count))
     spread = lax.all_to_all(spread, "node", 0, 0, tiled=True).reshape(padded)
     results = []
     offset = 0
@@ -133,11 +129,15 @@
     def push_hop(picked_fwd, picked_bwd):
         part_fwd = tile_forward(picked_fwd, remote_fwd)
         part_bwd = tile_forward(picked_bwd, remote_bwd)
-        got_fwd, got_bwd, got_dst = (
-            lax.all_to_all(part_fwd, "node", split_axis=0, concat_axis=0, tiled=True),
-            lax.all_to_all(part_bwd, "node", split_axis=0, concat_axis=0, tiled=True),
-            lax.all_to_all(own_dst, "node", split_axis=0, concat_axis=0, tiled=True),
+        got_both = lax.all_to_all(
+            jnp.concatenate([part_fwd, part_bwd], axis=1),
+            "node",
+            split_axis=0,
+            concat_axis=0,
+            tiled=True,
         )
+        got_fwd, got_bwd = got_both[:, :row_count], got_both[:, row_count:]
+        got_dst = lax.all_to_all(own_dst, "node", split_axis=0, concat_axis=0, tiled=True)
         return (place_blocks(got_fwd, got_dst), place_blocks(got_bwd, got_dst), got_dst)
 
     picked = pick_blocks(flat_hidden, own_src)
@@ -190,14 +190,16 @@
     back2_bwd = group_of(4).astype(jnp.bfloat16)
 
     def fetch_rows(grad_fwd, grad_bwd):
-        return (
-            lax.all_to_all(
-                pick_blocks(grad_fwd, recv_dst), "node", split_axis=0, concat_axis=0, tiled=True
+        got_both = lax.all_to_all(
+            jnp.concatenate(
+                [pick_blocks(grad_fwd, recv_dst), pick_blocks(grad_bwd, recv_dst)], axis=1
             ),
-            lax.all_to_all(
-                pick_blocks(grad_bwd, recv_dst), "node", split_axis=0, concat_axis=0, tiled=True
-            ),
+            "node",
+            split_axis=0,
+            concat_axis=0,
+            tiled=True,
         )
+        return got_both[:, :row_count], got_both[:, row_count:]
 
     got_fwd, got_bwd = fetch_rows(back2_fwd, back2_bwd)
     near1_fwd = place_blocks(tile_backward(got_fwd, remote_fwd).astype(jnp.bfloat16), own_src)

time: 289 us -> 247 us (0.85)
  blocking collectives: 38.2 us -> 14.3 us
  waiting for transfers between devices: 32.5 us -> 17.6 us
  matrix products: 54.8 us -> 46.6 us
  starting transfers between devices: 56.9 us -> 51 us
  other arithmetic: 14.7 us -> 20.4 us
  local copies, waits for them, and re-layouts: 87.6 us -> 92.9 us
    all_to_all x1 -> x0, blocking collectives: 24.5 us -> none  [exchange_sum(): lax.all_to_all(part.reshape(batch_count, padded // group), 'batch', 0, 0,...]
    all_to_all x9 -> x5, waiting for transfers between devices: 26.4 us -> 11.2 us  [the longest x1 8.9 us: exchange_sum(): part = lax.all_to_all(part, 'batch', 0, 0, tiled=True).sum(axis=0)]
    all_to_all x9 -> x5, starting transfers between devices: 45.8 us -> 39.9 us  [the longest x2 14.5 us: fetch_rows(): lax.all_to_all(jnp.concatenate([pick_blocks(grad_fwd, recv_dst), pick_blo...]
    slice x0 -> x2, local copies, waits for them, and re-layouts: none -> 5.38 us  [push_hop(): got_fwd, got_bwd = (got_both[:, :row_count], got_both[:, row_count:])]
    convert_element_type x4 -> x0, local copies, waits for them, and re-layouts: 5.05 us -> none  [pick_blocks(): jnp.einsum('qi,mic->qmc', chooser, shaped, preferred_element_type=jnp.flo...]
    dot_general x4, matrix products: 8.47 us -> 4.55 us  [band_apply(): jnp.einsum('mik,iak->mia', stacked, shaped_w, preferred_element_type=jnp....]
    dot_general x4, matrix products: 5.66 us -> 1.78 us  [tile_forward(): jnp.einsum('qmc,qac->qma', pieces, tile_vals, preferred_element_type=jnp....]
    concatenate x0 -> x2, local copies, waits for them, and re-layouts: none -> 3.79 us  [fetch_rows(): jnp.concatenate([pick_blocks(grad_fwd, recv_dst), pick_blocks(grad_bwd, r...]
  transfers between devices with their start and end apart: 11 -> 7, of which waited for: 7 -> 3; matrix products, arithmetic and copies ran while one was open for 46% -> 55% of each run, Pallas kernels for 0% -> 0%
where the time goes in v2:
time: 247 us; the launch traced here: 244 us
  local copies, waits for them, and re-layouts  92.9 us (38%)
  starting transfers between devices  51 us (21%)
  matrix products  46.6 us (19%)
  other arithmetic  20.4 us (8%)
  waiting for transfers between devices  17.6 us (7%)
  blocking collectives  14.3 us (6%)
    unnamed x119, local copies, waits for them, and re-layouts  17.7 us
    all_to_all x2, starting transfers between devices, fetch_rows(): lax.all_to_all(jnp.concatenate([pick_blocks(grad_fwd, recv_dst), pick_blo...  14.5 us
    all_to_all x1, blocking collectives, exchange_sum(): lax.all_to_all(flat.reshape(node_count, padded // node_count), 'node', 0,...  14.3 us
    all_to_all x2, starting transfers between devices, push_hop(): lax.all_to_all(jnp.concatenate([part_fwd, part_bwd], axis=1), 'node', spl...  13.4 us
    all_to_all x1, starting transfers between devices, exchange_sum(): part = lax.all_to_all(part, 'batch', 0, 0, tiled=True).sum(axis=0)  12 us
    transpose x4, local copies, waits for them, and re-layouts, band_transpose(): jnp.einsum('mia,iak->mik', gradient.reshape(row_count, blocks, tile_width...  10.8 us
    dot_general x7, matrix products, place_blocks(): jnp.einsum('qi,qmc->mic', chooser, pieces, preferred_element_type=jnp.flo...  9.36 us
    all_to_all x1, waiting for transfers between devices, exchange_sum(): part = lax.all_to_all(part, 'batch', 0, 0, tiled=True).sum(axis=0)  8.9 us
  transfers between devices with their start and end apart: 7, of which 3 were waited for; matrix products, arithmetic and copies ran while one was open for 55% of the time, Pallas kernels for 0%

profile of v2, /device:TPU:1, one launch (start us, length us, event | category | flops | bytes accessed | tf_op | source)
XLA Modules:
  0.0 244.3 jit_solution(12791400256744716794)
XLA Ops:
  2.1 7.6 %all-to-all-start.1 = ((bf16[16,1,4]{2,1,0:T(2,128)(2,1)}), bf16[16,1,4]{2,1,0:T(2,128)(2,1)S(1)}, u32[]{:S(2)}, u32[]{:S(2)}) async-start(bf16[16,1,4]{2,1,0:T(2,128)(2,1)} %compare_convert_fusion), calls=%async_computation.1 | async-start | bytes 16384 | tf_op jit(solution)/shard_map/all_to_all | solution.py:140
  9.6 1.5 convolution_bitcast_fusion.1
  13.2 1.6 copy.247
  24.0 1.8 reshape_reshape.2
  25.8 1.7 copy.210
  27.5 1.5 convolution_convert_fusion.6
  29.9 1.5 pad_maximum_fusion
  31.4 2.0 reshape.479
  33.5 6.7 %all-to-all-start = ((bf16[16,512,128]{2,1,0:T(8,128)(2,1)}), bf16[16,512,128]{2,1,0:T(8,128)(2,1)}, u32[]{:S(2)}, u32[]{:S(2)}) async-start(bf16[16,512,128]{2,1,0:T(8,128)(2,1)} %pad_maximum_fusion), calls=%async_computation | async-start | bytes 4194304 | tf_op jit(solution)/shard_map/all_to_all | solution.py:132
  40.2 2.6 %convolution_bitcast_fusion.5 = f32[256,4,384]{2,0,1:T(8,128)} fusion(bf16[4,128,384]{2,1,0:T(8,128)(2,1)} %bitcast.301, bf16[256,4,128]{2,1,0:T(4,128)(2,1)} %convert_element_type.211), kind=kOutput, calls=%fused_computation.24 | convolution fusion | flops 100663296 | bytes 2228224 | tf_op jit(solution)/shard_map/mia,iak->mik/dot_general | solution.py:34
  42.8 3.0 %copy.235 = f32[256,4,384]{0,2,1:T(8,128)} copy(f32[256,4,384]{2,0,1:T(8,128)} %convolution_bitcast_fusion.5) | data formatting | bytes 3145728 | tf_op jit(solution)/shard_map/mia,iak->mik/transpose | solution.py:34
  45.8 1.9 slice.285
  47.8 2.1 fusion.160
  49.8 2.0 copy.272
  51.8 2.0 copy.273
  53.8 2.1 copy.271
  55.9 2.0 reshape.475
  57.9 1.8 convolution_bitcast_fusion.17
  61.4 1.6 convert_reduce_fusion.2
  63.0 1.8 fusion.43
  64.8 1.8 fusion.165
  68.2 1.5 convolution_convert_fusion.3
  69.8 1.9 copy.239
  71.7 6.7 %all-to-all-start.3 = ((bf16[16,512,128]{2,1,0:T(8,128)(2,1)}), bf16[16,512,128]{2,1,0:T(8,128)(2,1)}, u32[]{:S(2)}, u32[]{:S(2)}) async-start(bf16[16,512,128]{2,1,0:T(8,128)(2,1)} %copy.239), calls=%async_computation.3 | async-start | bytes 4194304 | tf_op jit(solution)/shard_map/all_to_all | solution.py:193
  78.4 2.7 %fusion.159 = (bf16[16,256,128]{2,1,0:T(8,128)(2,1)S(1)}, bf16[16,256,128]{2,1,0:T(8,128)(2,1)}) fusion(bf16[16,512,128]{2,1,0:T(8,128)(2,1)} %all-to-all-done), kind=kLoop, calls=%fused_computation.211 | loop fusion | bytes 4194304 | tf_op jit(solution)/shard_map/slice | solution.py:139
  81.1 1.5 fusion.60
  82.6 2.1 copy.223
  84.7 2.7 %fusion.63 = f32[256,128,4]{1,2,0:T(4,128)} fusion(bf16[16,256,128]{2,1,0:T(8,128)(2,1)} %get-tuple-element.102, bf16[16,1,4]{0,2,1:T(4,128)(2,1)S(1)} %copy.215), kind=kOutput, calls=%fused_computation.91 | convolution fusion | flops 4194304 | bytes 1572992 | tf_op jit(solution)/shard_map/qi,qmc->mic/dot_general | solution.py:56
  87.4 2.1 copy.217
  89.5 2.6 %fusion.37 = bf16[256,4,128]{0,2,1:T(8,128)(2,1)} fusion(bf16[4,128,384]{2,1,0:T(8,128)(2,1)} %bitcast.297, f32[256,128,4]{0,1,2:T(8,128)} %copy.223, bf16[256,3,128]{2,0,1:T(8,128)(2,1)} %get-tuple-element.120, bf16[256,3,128]{2,0,1:T(8,128)(2,1)} %get-tuple-element.119, bf16[256,4,128]{2,0,1:T(8,128)(2,1)} %copy.210), kind=kOutput, calls=%fused_computation.65 | convolution fusion | flops 104857600 | bytes 1835008 | tf_op jit(solution)/shard_map/mik,iak->mia/dot_general | solution.py:25
  93.3 1.8 copy.224
  95.1 1.8 copy.218
  96.9 1.8 convert_element_type.196
  98.7 1.8 convert_element_type.204
  101.5 1.5 convolution_convert_fusion.4
  104.4 1.5 pad_maximum_fusion.1
  107.6 6.6 %all-to-all-start.2 = ((bf16[16,512,128]{2,1,0:T(8,128)(2,1)}), bf16[16,512,128]{2,1,0:T(8,128)(2,1)}, u32[]{:S(2)}, u32[]{:S(2)}) async-start(bf16[16,512,128]{2,1,0:T(8,128)(2,1)} %pad_maximum_fusion.1), calls=%async_computation.2 | async-start | bytes 4194304 | tf_op jit(solution)/shard_map/all_to_all | solution.py:132
  114.2 1.8 convolution_convert_fusion.7
  117.0 1.8 convolution_convert_fusion.8
  121.1 1.9 copy.257
  123.0 1.6 convolution_bitcast_fusion.4
  124.6 3.1 %copy.242 = f32[256,4,384]{0,2,1:T(8,128)} copy(f32[256,4,384]{2,0,1:T(8,128)} %convolution_bitcast_fusion.4) | data formatting | bytes 3145728 | tf_op jit(solution)/shard_map/mia,iak->mik/transpose | solution.py:34
  127.6 2.6 %convolution_bitcast_fusion.2 = f32[256,4,384]{2,0,1:T(8,128)} fusion(bf16[4,128,384]{2,1,0:T(8,128)(2,1)} %bitcast.298, bf16[256,4,128]{2,1,0:T(4,128)(2,1)} %copy-done.7), kind=kOutput, calls=%fused_computation.19 | convolution fusion | flops 100663296 | bytes 2228224 | tf_op jit(solution)/shard_map/mia,iak->mik/dot_general | solution.py:34
  130.2 3.1 %copy.253 = f32[256,4,384]{0,2,1:T(8,128)} copy(f32[256,4,384]{2,0,1:T(8,128)} %convolution_bitcast_fusion.2) | data formatting | bytes 3145728 | tf_op jit(solution)/shard_map/mia,iak->mik/transpose | solution.py:34
  134.6 1.9 fusion.97
  137.6 2.3 all-to-all-done.2
  139.9 7.8 %all-to-all-start.4 = ((bf16[16,512,128]{2,1,0:T(8,128)(2,1)}), bf16[16,512,128]{2,1,0:T(8,128)(2,1)}, u32[]{:S(2)}, u32[]{:S(2)}) async-start(bf16[16,512,128]{2,1,0:T(8,128)(2,1)} %copy.257), calls=%async_computation.4 | async-start | bytes 4194304 | tf_op jit(solution)/shard_map/all_to_all | solution.py:193
  147.7 2.2 fusion.95
  149.9 2.0 copy.245
  151.9 2.1 reshape.478
  154.0 2.0 copy.256
  156.1 2.1 reshape.482
  158.2 2.7 %fusion.158 = (bf16[16,256,128]{2,1,0:T(8,128)(2,1)S(1)}, bf16[16,256,128]{2,1,0:T(8,128)(2,1)}) fusion(bf16[16,512,128]{2,1,0:T(8,128)(2,1)} %all-to-all-done.2), kind=kLoop, calls=%fused_computation.210 | loop fusion | bytes 4194304 | tf_op jit(solution)/shard_map/slice | solution.py:139
  163.4 1.8 convert_element_type.206
  165.1 2.0 fusion.57
  168.5 1.8 convert_element_type.203
  174.4 1.6 fusion.48
  176.1 1.7 add_convert_fusion
  179.4 1.9 fusion.88
  186.8 14.3 %all_to_all.51 = f32[16,1,3356]{2,1,0:T(1,128)} all-to-all(f32[16,1,3356]{2,1,0:T(1,128)S(1)} %all_to_all.39), channel_id=1, replica_groups=mesh['node'=16,'batch'=16] {'node'}, dimensions={0} | all-to-all | bytes 429568 | tf_op jit(solution)/shard_map/all_to_all | solution.py:78
  203.0 12.0 %all-to-all-start.6 = ((f32[16,1,3356]{2,1,0:T(1,128)}), f32[16,1,3356]{2,1,0:T(1,128)}, u32[]{:S(2)}, u32[]{:S(2)}) async-start(f32[16,1,3356]{2,1,0:T(1,128)} %broadcast_in_dim.4), calls=%async_computation.6 | async-start | bytes 442368 | tf_op jit(solution)/shard_map/all_to_all | solution.py:82
  217.0 8.9 %all-to-all-done.6 = f32[16,1,3356]{2,1,0:T(1,128)} async-done(((f32[16,1,3356]{2,1,0:T(1,128)}), f32[16,1,3356]{2,1,0:T(1,128)}, u32[]{:S(2)}, u32[]{:S(2)}) %all-to-all-start.6) | async-done | bytes 214816 | tf_op jit(solution)/shard_map/all_to_all | solution.py:82
  227.8 3.5 %all-to-all-start.7 = ((f32[16,1,3356]{2,1,0:T(1,128)}), f32[16,1,3356]{2,1,0:T(1,128)S(1)}, u32[]{:S(2)}, u32[]{:S(2)}) async-start(f32[16,1,3356]{2,1,0:T(1,128)} %broadcast_in_dim.5), calls=%async_computation.7 | async-start | bytes 442368 | tf_op jit(solution)/shard_map/all_to_all | solution.py:84
  233.3 6.4 %all-to-all-done.7 = f32[16,1,3356]{2,1,0:T(1,128)S(1)} async-done(((f32[16,1,3356]{2,1,0:T(1,128)}), f32[16,1,3356]{2,1,0:T(1,128)S(1)}, u32[]{:S(2)}, u32[]{:S(2)}) %all-to-all-start.7) | async-done | bytes 214816 | tf_op jit(solution)/shard_map/all_to_all | solution.py:84
  (187 shorter events, 54.6 us)
Async XLA Ops:
  0.6 28.8 %copy-start = (bf16[16,128,128]{2,1,0:T(8,128)(2,1)S(1)}, bf16[16,128,128]{2,1,0:T(8,128)(2,1)}, u32[]{:S(2)}) copy-start(bf16[16,128,128]{2,1,0:T(8,128)(2,1)} %param.30) | copy-start | bytes 1572868
  2.1 31.4 %all-to-all-start.1 = ((bf16[16,1,4]{2,1,0:T(2,128)(2,1)}), bf16[16,1,4]{2,1,0:T(2,128)(2,1)S(1)}, u32[]{:S(2)}, u32[]{:S(2)}) async-start(bf16[16,1,4]{2,1,0:T(2,128)(2,1)} %compare_convert_fusion), calls=%async_computation.1 | async-start | bytes 16384 | tf_op jit(solution)/shard_map/all_to_all | solution.py:140
  9.6 3.2 %copy-start.25 = (bf16[512,384]{1,0:T(8,128)(2,1)S(1)}, bf16[512,384]{1,0:T(8,128)(2,1)}, u32[]{:S(2)}) copy-start(bf16[512,384]{1,0:T(8,128)(2,1)} %param.29) | copy-start | bytes 1179652
  11.2 1.5 copy-start.1
  12.8 2.0 copy-start.9
  14.8 2.4 copy-start.2
  19.2 3.0 %copy-start.23 = (bf16[1,6,64,512]{3,2,1,0:T(8,128)(2,1)S(1)}, bf16[1,6,64,512]{3,2,1,0:T(8,128)(2,1)}, u32[]{:S(2)}) copy-start(bf16[1,6,64,512]{3,2,1,0:T(8,128)(2,1)} %param.21) | copy-start | bytes 1179652
  20.2 2.1 copy-start.44
  20.2 2.1 copy-start.52
  22.3 0.7 copy-start.30
  22.3 0.8 copy-start.32
  23.1 4.4 %copy-start.48 = (s32[16]{0:T(128)S(1)}, s32[16]{0:T(128)}, u32[]{:S(2)}) copy-start(s32[16]{0:T(128)} %param.32) | copy-start | bytes 196
  24.0 5.0 %copy-start.3 = (bf16[16,128,128]{2,1,0:T(8,128)(2,1)S(1)}, bf16[16,128,128]{2,1,0:T(8,128)(2,1)}, u32[]{:S(2)}) copy-start(bf16[16,128,128]{2,1,0:T(8,128)(2,1)} %param.31) | copy-start | bytes 1572868
  33.5 38.3 %all-to-all-start = ((bf16[16,512,128]{2,1,0:T(8,128)(2,1)}), bf16[16,512,128]{2,1,0:T(8,128)(2,1)}, u32[]{:S(2)}, u32[]{:S(2)}) async-start(bf16[16,512,128]{2,1,0:T(8,128)(2,1)} %pad_maximum_fusion), calls=%async_computation | async-start | bytes 4194304 | tf_op jit(solution)/shard_map/all_to_all | solution.py:132
  71.7 35.8 %all-to-all-start.3 = ((bf16[16,512,128]{2,1,0:T(8,128)(2,1)}), bf16[16,512,128]{2,1,0:T(8,128)(2,1)}, u32[]{:S(2)}, u32[]{:S(2)}) async-start(bf16[16,512,128]{2,1,0:T(8,128)(2,1)} %copy.239), calls=%async_computation.3 | async-start | bytes 4194304 | tf_op jit(solution)/shard_map/all_to_all | solution.py:193
  89.5 2.7 %copy-start.22 = (bf16[256,4,128]{2,0,1:T(8,128)(2,1)S(1)}, bf16[256,4,128]{2,0,1:T(8,128)(2,1)}, u32[]{:S(2)}) copy-start(bf16[256,4,128]{2,0,1:T(8,128)(2,1)} %copy.210) | copy-start | bytes 786436
  89.5 2.7 %copy-start.27 = (bf16[512,384]{1,0:T(8,128)(2,1)S(1)}, bf16[512,384]{1,0:T(8,128)(2,1)}, u32[]{:S(2)}) copy-start(bf16[512,384]{1,0:T(8,128)(2,1)} %param.28) | copy-start | bytes 1179652
  89.5 2.7 %copy-start.34 = (f32[256,128,4]{0,1,2:T(8,128)S(1)}, f32[256,128,4]{0,1,2:T(8,128)}, u32[]{:S(2)}) copy-start(f32[256,128,4]{0,1,2:T(8,128)} %copy.217) | copy-start | bytes 1572868
  89.5 2.7 %copy-start.41 = (bf16[256,3,128]{2,0,1:T(8,128)(2,1)S(1)}, bf16[256,3,128]{2,0,1:T(8,128)(2,1)}, u32[]{:S(2)}) copy-start(bf16[256,3,128]{2,0,1:T(8,128)(2,1)} %get-tuple-element.119) | copy-start | bytes 589828
  89.5 2.7 %copy-start.42 = (bf16[256,3,128]{2,0,1:T(8,128)(2,1)S(1)}, bf16[256,3,128]{2,0,1:T(8,128)(2,1)}, u32[]{:S(2)}) copy-start(bf16[256,3,128]{2,0,1:T(8,128)(2,1)} %get-tuple-element.120) | copy-start | bytes 589828
  100.5 2.5 %copy-start.8 = (bf16[256,4,128]{2,1,0:T(4,128)(2,1)S(1)}, bf16[256,4,128]{2,1,0:T(4,128)(2,1)}, u32[]{:S(2)}) copy-start(bf16[256,4,128]{2,1,0:T(4,128)(2,1)} %copy.218) | copy-start | bytes 786436
  104.4 1.6 copy-start.20
  104.4 2.4 copy-start.18
  107.6 32.3 %all-to-all-start.2 = ((bf16[16,512,128]{2,1,0:T(8,128)(2,1)}), bf16[16,512,128]{2,1,0:T(8,128)(2,1)}, u32[]{:S(2)}, u32[]{:S(2)}) async-start(bf16[16,512,128]{2,1,0:T(8,128)(2,1)} %pad_maximum_fusion.1), calls=%async_computation.2 | async-start | bytes 4194304 | tf_op jit(solution)/shard_map/all_to_all | solution.py:132
  114.2 1.8 copy-start.10
  114.2 1.8 copy-start.11
  114.2 1.8 copy-start.14
  114.2 1.8 copy-start.15
  117.0 2.8 %copy-start.7 = (bf16[256,4,128]{2,1,0:T(4,128)(2,1)}, bf16[256,4,128]{2,1,0:T(4,128)(2,1)S(1)}, u32[]{:S(2)}) copy-start(bf16[256,4,128]{2,1,0:T(4,128)(2,1)S(1)} %fusion.40) | copy-start | bytes 786436
  117.0 1.8 copy-start.12
  117.0 1.8 copy-start.13
  117.0 1.8 copy-start.16
  117.0 1.9 copy-start.17
  121.1 1.9 copy-start.28
  133.3 3.3 %copy-start.4 = (f32[256,4,384]{0,2,1:T(8,128)S(1)}, f32[256,4,384]{0,2,1:T(8,128)}, u32[]{:S(2)}) copy-start(f32[256,4,384]{0,2,1:T(8,128)} %copy.253) | copy-start | bytes 4718596
  139.9 34.6 %all-to-all-start.4 = ((bf16[16,512,128]{2,1,0:T(8,128)(2,1)}), bf16[16,512,128]{2,1,0:T(8,128)(2,1)}, u32[]{:S(2)}, u32[]{:S(2)}) async-start(bf16[16,512,128]{2,1,0:T(8,128)(2,1)} %copy.257), calls=%async_computation.4 | async-start | bytes 4194304 | tf_op jit(solution)/shard_map/all_to_all | solution.py:193
  160.9 0.9 copy-start.21
  160.9 1.1 copy-start.26
  160.9 1.1 copy-start.39
  160.9 1.2 copy-start.40
  165.1 2.0 copy-start.19
  165.1 2.0 copy-start.29
  165.1 2.0 copy-start.37
  165.1 2.0 copy-start.38
  170.2 3.0 %copy-start.5 = (bf16[1,4,64,512]{3,2,1,0:T(8,128)(2,1)S(1)}, bf16[1,4,64,512]{3,2,1,0:T(8,128)(2,1)}, u32[]{:S(2)}) copy-start(bf16[1,4,64,512]{3,2,1,0:T(8,128)(2,1)} %param.34) | copy-start | bytes 786436
  181.4 1.0 copy-start.31
  181.4 1.0 copy-start.33
  181.6 1.7 copy-start.45
  183.7 1.0 copy-start.6
  183.7 1.2 copy-start.35
  183.7 1.2 copy-start.36
  184.6 0.8 copy-start.47
  184.6 0.8 copy-start.49
  184.6 0.8 copy-start.50
  184.9 30.1 %copy-start.46 = (bf16[256,64]{0,1:T(8,128)(2,1)S(1)}, bf16[256,64]{0,1:T(8,128)(2,1)}, u32[]{:S(2)}) copy-start(bf16[256,64]{0,1:T(8,128)(2,1)} %param.26) | copy-start | bytes 98308
  184.9 30.1 %copy-start.51 = (f32[256]{0:T(256)S(1)}, f32[256]{0:T(256)}, u32[]{:S(2)}) copy-start(f32[256]{0:T(256)} %param.27) | copy-start | bytes 3076
  186.8 44.5 %copy-start.24 = (bf16[1,6,64,512]{3,2,1,0:T(8,128)(2,1)S(1)}, bf16[1,6,64,512]{3,2,1,0:T(8,128)(2,1)}, u32[]{:S(2)}) copy-start(bf16[1,6,64,512]{3,2,1,0:T(8,128)(2,1)} %param.21) | copy-start | bytes 1179652
  186.8 44.5 %copy-start.43 = (bf16[64,320]{1,0:T(8,128)(2,1)S(1)}, bf16[64,320]{1,0:T(8,128)(2,1)}, u32[]{:S(2)}) copy-start(bf16[64,320]{1,0:T(8,128)(2,1)} %param.24) | copy-start | bytes 122884
  186.8 44.5 %copy-start.53 = (f32[64]{0:T(128)S(1)}, f32[64]{0:T(128)}, u32[]{:S(2)}) copy-start(f32[64]{0:T(128)} %param.25) | copy-start | bytes 772
  203.0 22.9 %all-to-all-start.6 = ((f32[16,1,3356]{2,1,0:T(1,128)}), f32[16,1,3356]{2,1,0:T(1,128)}, u32[]{:S(2)}, u32[]{:S(2)}) async-start(f32[16,1,3356]{2,1,0:T(1,128)} %broadcast_in_dim.4), calls=%async_computation.6 | async-start | bytes 442368 | tf_op jit(solution)/shard_map/all_to_all | solution.py:82
  227.8 11.8 %all-to-all-start.7 = ((f32[16,1,3356]{2,1,0:T(1,128)}), f32[16,1,3356]{2,1,0:T(1,128)S(1)}, u32[]{:S(2)}, u32[]{:S(2)}) async-start(f32[16,1,3356]{2,1,0:T(1,128)} %broadcast_in_dim.5), calls=%async_computation.7 | async-start | bytes 442368 | tf_op jit(solution)/shard_map/all_to_all | solution.py:84

commit v3 on v2

--- a/solution.py
+++ b/solution.py
@@ -8,59 +8,45 @@
 DILATION_GAP = 2
 
 
-def neighbor_stack(values, blocks, tile_width):
-    row_count = values.shape[0]
-    shaped = values.reshape(row_count, blocks, tile_width)
-    zeros_blk = jnp.zeros((row_count, 1, tile_width), values.dtype)
-    before = jnp.concatenate([zeros_blk, shaped[:, :-1]], axis=1)
-    after_blk = jnp.concatenate([shaped[:, 1:], zeros_blk], axis=1)
-    return jnp.concatenate([before, shaped, after_blk], axis=2)
-
-
-def band_apply(values, weights):
-    tile_width = weights.shape[1] // 3
-    blocks = weights.shape[0] // tile_width
-    stacked = neighbor_stack(values, blocks, tile_width)
-    shaped_w = weights.reshape(blocks, tile_width, 3 * tile_width)
-    result = jnp.einsum("mik,iak->mia", stacked, shaped_w, preferred_element_type=jnp.float32)
-    return result.reshape(values.shape[0], blocks * tile_width)
-
-
-def band_transpose(gradient, weights):
-    tile_width = weights.shape[1] // 3
-    blocks = weights.shape[0] // tile_width
-    row_count = gradient.shape[0]
-    shaped_w = weights.reshape(blocks, tile_width, 3 * tile_width)
-    spread = jnp.einsum(
-        "mia,iak->mik",
-        gradient.reshape(row_count, blocks, tile_width),
-        shaped_w,
-        preferred_element_type=jnp.float32,
-    )
-    spread = spread.reshape(row_count, blocks, 3, tile_width)
-    zeros_blk = jnp.zeros((row_count, 1, tile_width), jnp.float32)
-    from_after = jnp.concatenate([spread[:, 1:, 0], zeros_blk], axis=1)
-    from_before = jnp.concatenate([zeros_blk, spread[:, :-1, 2]], axis=1)
-    return (spread[:, :, 1] + from_after + from_before).reshape(row_count, blocks * tile_width)
-
-
-def pick_blocks(values, chooser):
-    blocks = chooser.shape[1]
-    shaped = values.reshape(values.shape[0], blocks, values.shape[1] // blocks)
-    return jnp.einsum("qi,mic->qmc", chooser, shaped, preferred_element_type=jnp.float32).astype(
-        jnp.bfloat16
-    )
-
-
-def place_blocks(pieces, chooser):
-    result = jnp.einsum("qi,qmc->mic", chooser, pieces, preferred_element_type=jnp.float32)
-    return result.reshape(result.shape[0], result.shape[1] * result.shape[2])
-
-
-def tile_forward(pieces, tile_vals):
-    return jnp.einsum("qmc,qac->qma", pieces, tile_vals, preferred_element_type=jnp.float32).astype(
-        jnp.bfloat16
-    )
+def dense_band(weights, blocks, tile_width):
+    shaped = weights.reshape(blocks, tile_width, 1, 3, tile_width)
+    row_ids = lax.broadcasted_iota(jnp.int32, (blocks, 1, blocks, 3, 1), 0)
+    col_ids = lax.broadcasted_iota(jnp.int32, (blocks, 1, blocks, 3, 1), 2)
+    offsets = lax.broadcasted_iota(jnp.int32, (blocks, 1, blocks, 3, 1), 3)
+    hits = (col_ids == row_ids + offsets - 1).astype(weights.dtype)
+    placed = (shaped * hits).sum(axis=3, dtype=jnp.float32).astype(weights.dtype)
+    return placed.reshape(blocks * tile_width, blocks * tile_width)
+
+
+def spread_onehot(chooser, tile_vals):
+    slots, blocks = chooser.shape
+    tile_width = tile_vals.shape[2]
+    placed = tile_vals[:, :, None, :] * chooser[:, None, :, None]
+    return placed.reshape(slots, tile_vals.shape[1], blocks * tile_width)
+
+
+def near_apply(values, dense):
+    return jnp.einsum("mn,kn->mk", values, dense, preferred_element_type=jnp.float32)
+
+
+def near_transpose(gradient, dense):
+    return jnp.einsum("mk,kn->mn", gradient, dense, preferred_element_type=jnp.float32)
+
+
+def tile_products(values, spread_tiles):
+    return jnp.einsum(
+        "mn,qan->qma", values, spread_tiles, preferred_element_type=jnp.float32
+    ).astype(jnp.bfloat16)
+
+
+def place_rows(pieces, placer):
+    return jnp.einsum("sma,san->mn", pieces, placer, preferred_element_type=jnp.float32)
+
+
+def pick_rows(values, placer):
+    return jnp.einsum(
+        "mn,san->sma", values, placer, preferred_element_type=jnp.float32
+    ).astype(jnp.bfloat16)
 
 
 def tile_backward(pieces, tile_vals):
@@ -125,30 +111,38 @@
     gate_val = jax.nn.sigmoid(pre_act[:, :, channel_count:])
     hidden = (filtered * gate_val).astype(jnp.bfloat16)
     flat_hidden = hidden.reshape(row_count, local_nodes)
-
-    def push_hop(picked_fwd, picked_bwd):
-        part_fwd = tile_forward(picked_fwd, remote_fwd)
-        part_bwd = tile_forward(picked_bwd, remote_bwd)
+    eye_tile = jnp.eye(tile_width, dtype=jnp.bfloat16)
+    eye_slots = jnp.broadcast_to(eye_tile, (own_src.shape[0], tile_width, tile_width))
+    dense_fwd = dense_band(local_fwd, blocks, tile_width)
+    dense_bwd = dense_band(local_bwd, blocks, tile_width)
+    spread_fwd = spread_onehot(own_src, remote_fwd)
+    spread_bwd = spread_onehot(own_src, remote_bwd)
+    src_placer = spread_onehot(own_src, eye_slots)
+    recv_dst = lax.all_to_all(own_dst, "node", split_axis=0, concat_axis=0, tiled=True)
+    dst_placer = spread_onehot(recv_dst, eye_slots)
+
+    def swap(first, second):
         got_both = lax.all_to_all(
-            jnp.concatenate([part_fwd, part_bwd], axis=1),
+            jnp.concatenate([first, second], axis=1),
             "node",
             split_axis=0,
             concat_axis=0,
             tiled=True,
         )
-        got_fwd, got_bwd = got_both[:, :row_count], got_both[:, row_count:]
-        got_dst = lax.all_to_all(own_dst, "node", split_axis=0, concat_axis=0, tiled=True)
-        return (place_blocks(got_fwd, got_dst), place_blocks(got_bwd, got_dst), got_dst)
-
-    picked = pick_blocks(flat_hidden, own_src)
-    far_fwd, far_bwd, recv_dst = push_hop(picked, picked)
-    hop_fwd = (band_apply(flat_hidden, local_fwd) + far_fwd).astype(jnp.bfloat16)
-    hop_bwd = (band_apply(flat_hidden, local_bwd) + far_bwd).astype(jnp.bfloat16)
-    far_fwd, far_bwd, recv_dst = push_hop(
-        pick_blocks(hop_fwd, own_src), pick_blocks(hop_bwd, own_src)
-    )
-    two_fwd = (band_apply(hop_fwd, local_fwd) + far_fwd).astype(jnp.bfloat16)
-    two_bwd = (band_apply(hop_bwd, local_bwd) + far_bwd).astype(jnp.bfloat16)
+        return got_both[:, :row_count], got_both[:, row_count:]
+
+    def push_hop(values_fwd, values_bwd):
+        got_fwd, got_bwd = swap(
+            tile_products(values_fwd, spread_fwd), tile_products(values_bwd, spread_bwd)
+        )
+        return place_rows(got_fwd, dst_placer), place_rows(got_bwd, dst_placer)
+
+    far_fwd, far_bwd = push_hop(flat_hidden, flat_hidden)
+    hop_fwd = (near_apply(flat_hidden, dense_fwd) + far_fwd).astype(jnp.bfloat16)
+    hop_bwd = (near_apply(flat_hidden, dense_bwd) + far_bwd).astype(jnp.bfloat16)
+    far_fwd, far_bwd = push_hop(hop_fwd, hop_bwd)
+    two_fwd = (near_apply(hop_fwd, dense_fwd) + far_fwd).astype(jnp.bfloat16)
+    two_bwd = (near_apply(hop_bwd, dense_bwd) + far_bwd).astype(jnp.bfloat16)
     stacked_parts = jnp.concatenate(
         [
             hidden,
@@ -190,31 +184,22 @@
     back2_bwd = group_of(4).astype(jnp.bfloat16)
 
     def fetch_rows(grad_fwd, grad_bwd):
-        got_both = lax.all_to_all(
-            jnp.concatenate(
-                [pick_blocks(grad_fwd, recv_dst), pick_blocks(grad_bwd, recv_dst)], axis=1
-            ),
-            "node",
-            split_axis=0,
-            concat_axis=0,
-            tiled=True,
-        )
-        return got_both[:, :row_count], got_both[:, row_count:]
+        return swap(pick_rows(grad_fwd, dst_placer), pick_rows(grad_bwd, dst_placer))
 
     got_fwd, got_bwd = fetch_rows(back2_fwd, back2_bwd)
-    near1_fwd = place_blocks(tile_backward(got_fwd, remote_fwd).astype(jnp.bfloat16), own_src)
-    near1_bwd = place_blocks(tile_backward(got_bwd, remote_bwd).astype(jnp.bfloat16), own_src)
-    back1_fwd = (group_of(1) + band_transpose(back2_fwd, local_fwd) + near1_fwd).astype(
-        jnp.bfloat16
-    )
-    back1_bwd = (group_of(3) + band_transpose(back2_bwd, local_bwd) + near1_bwd).astype(
+    near1_fwd = place_rows(tile_backward(got_fwd, remote_fwd).astype(jnp.bfloat16), src_placer)
+    near1_bwd = place_rows(tile_backward(got_bwd, remote_bwd).astype(jnp.bfloat16), src_placer)
+    back1_fwd = (group_of(1) + near_transpose(back2_fwd, dense_fwd) + near1_fwd).astype(
+        jnp.bfloat16
+    )
+    back1_bwd = (group_of(3) + near_transpose(back2_bwd, dense_bwd) + near1_bwd).astype(
         jnp.bfloat16
     )
     got_fwd, got_bwd = fetch_rows(back1_fwd, back1_bwd)
     combined = (tile_backward(got_fwd, remote_fwd) + tile_backward(got_bwd, remote_bwd)).astype(
         jnp.bfloat16
     )
-    far_total = place_blocks(combined, own_src)
+    far_total = place_rows(combined, src_placer)
     skip_back = jnp.einsum("sc,wsn->wcn", w_skip, cot_skip, preferred_element_type=jnp.float32)
     direct = (
         grad_parts[:, :, :channel_count]
@@ -224,8 +209,8 @@
     )
     summed = (
         direct
-        + band_transpose(back1_fwd, local_fwd)
-        + band_transpose(back1_bwd, local_bwd)
+        + near_transpose(back1_fwd, dense_fwd)
+        + near_transpose(back1_bwd, dense_bwd)
         + far_total
     )
     grad_hidden = summed.astype(jnp.bfloat16).reshape(shape4).astype(jnp.float32)

time: 247 us -> 233 us (0.943)
  local copies, waits for them, and re-layouts: 92.9 us -> 43.4 us
  waiting for transfers between devices: 17.6 us -> 61.9 us
  starting transfers between devices: 51 us -> 47.1 us
  matrix products: 46.6 us -> 44 us
    all_to_all x5, waiting for transfers between devices: 2.32 us -> 45.8 us  [the longest x4 45.8 us: swap(): lax.all_to_all(jnp.concatenate([first, second], axis=1), 'node', split_ax...]
    mul x0 -> x13, local copies, waits for them, and re-layouts: none -> 20.8 us  [the longest x9 19.7 us: spread_onehot(): placed = tile_vals[:, :, None, :] * chooser[:, None, :, None]]
    slice x9 -> x0, local copies, waits for them, and re-layouts: 15.2 us -> none  [the longest x2 5.38 us: push_hop(): got_fwd, got_bwd = (got_both[:, :row_count], got_both[:, row_count:])]
    convert_element_type x10 -> x0, local copies, waits for them, and re-layouts: 13.3 us -> none  [the longest x2 3.59 us: shards(): (band_apply(flat_hidden, local_fwd) + far_fwd).astype(jnp.bfloat16)]
    transpose x4 -> x0, local copies, waits for them, and re-layouts: 10.8 us -> none  [band_transpose(): jnp.einsum('mia,iak->mik', gradient.reshape(row_count, blocks, tile_width...]
    reshape x5 -> x0, local copies, waits for them, and re-layouts: 9.29 us -> none  [the longest x2 4.2 us: band_transpose(): (spread[:, :, 1] + from_after + from_before).reshape(row_count, blocks *...]
    unnamed x119 -> x104, local copies, waits for them, and re-layouts: 17.7 us -> 10.1 us
    dot_general x2 -> x0, local copies, waits for them, and re-layouts: 4.18 us -> none  [place_blocks(): jnp.einsum('qi,qmc->mic', chooser, pieces, preferred_element_type=jnp.flo...]
  transfers between devices with their start and end apart: 7 -> 7, of which waited for: 3 -> 6; matrix products, arithmetic and copies ran while one was open for 55% -> 34% of each run, Pallas kernels for 0% -> 0%
where the time goes in v3:
time: 233 us; the launch traced here: 232 us
  waiting for transfers between devices  61.9 us (27%)
  starting transfers between devices  47.1 us (20%)
  matrix products  44 us (19%)
  local copies, waits for them, and re-layouts  43.4 us (19%)
  other arithmetic  20 us (9%)
  blocking collectives  14 us (6%)
    all_to_all x4, waiting for transfers between devices, swap(): lax.all_to_all(jnp.concatenate([first, second], axis=1), 'node', split_ax...  45.8 us
    all_to_all x4, starting transfers between devices, swap(): lax.all_to_all(jnp.concatenate([first, second], axis=1), 'node', split_ax...  25.6 us
    mul x9, local copies, waits for them, and re-layouts, spread_onehot(): placed = tile_vals[:, :, None, :] * chooser[:, None, :, None]  19.7 us
    dot_general x7, matrix products, place_rows(): jnp.einsum('sma,san->mn', pieces, placer, preferred_element_type=jnp.floa...  18.1 us
    all_to_all x1, blocking collectives, exchange_sum(): lax.all_to_all(flat.reshape(node_count, padded // node_count), 'node', 0,...  14 us
    all_to_all x1, starting transfers between devices, exchange_sum(): part = lax.all_to_all(part, 'batch', 0, 0, tiled=True).sum(axis=0)  10.5 us
    unnamed x104, local copies, waits for them, and re-layouts  10.1 us
    all_to_all x1, waiting for transfers between devices, exchange_sum(): part = lax.all_to_all(part, 'batch', 0, 0, tiled=True).sum(axis=0)  9.63 us
  transfers between devices with their start and end apart: 7, of which 6 were waited for; matrix products, arithmetic and copies ran while one was open for 34% of the time, Pallas kernels for 0%

profile of v3, /device:TPU:1, one launch (start us, length us, event | category | flops | bytes accessed | tf_op | source)
XLA Modules:
  0.0 231.9 jit_solution(16134637197007980321)
XLA Ops:
  0.7 1.4 compare_convert_fusion
  2.0 7.6 %all-to-all-start.1 = ((bf16[16,1,4]{2,1,0:T(2,128)(2,1)}), bf16[16,1,4]{2,1,0:T(2,128)(2,1)S(1)}, u32[]{:S(2)}, u32[]{:S(2)}) async-start(bf16[16,1,4]{2,1,0:T(2,128)(2,1)} %compare_convert_fusion), calls=%async_computation.1 | async-start | bytes 16384 | tf_op jit(solution)/shard_map/all_to_all | solution.py:121
  10.3 1.2 fusion.207
  12.3 1.0 fusion.65
  13.3 0.9 constant_dynamic-update-slice_fusion.4
  14.3 3.6 %broadcast_multiply_fusion.1 = (bf16[16,128,4,128]{3,2,1,0:T(4,128)(2,1)}, bf16[16,128,4,128]{3,2,1,0:T(4,128)(2,1)}) fusion(bf16[16,4]{1,0:T(8,128)(2,1)S(1)} %fusion.201, bf16[16,128,128]{2,1,0:T(8,128)(2,1)S(1)} %copy-done.6, bf16[16,128,128]{2,1,0:T(8,128)(2,1)S(1)} %copy-done.16), kind=kLoop, calls=%fused_computation.135 | loop fusion | flops 2097152 | bytes 5243008 | tf_op jit(solution)/shard_map/mul | solution.py:24
  17.8 2.7 %mul.181 = bf16[16,128,512]{2,1,0:T(8,128)(2,1)S(1)} reshape(bf16[16,128,4,128]{3,2,1,0:T(4,128)(2,1)} %get-tuple-element.114) | data formatting | bytes 4194304 | tf_op jit(solution)/shard_map/mul | solution.py:24
  20.6 4.1 %mul.184 = bf16[16,128,512]{2,1,0:T(8,128)(2,1)} reshape(bf16[16,128,4,128]{3,2,1,0:T(4,128)(2,1)} %get-tuple-element.115) | data formatting | bytes 4194304 | tf_op jit(solution)/shard_map/mul | solution.py:24
  25.5 0.8 copy-done.2
  27.0 1.6 pad_maximum_fusion
  28.6 6.8 %all-to-all-start = ((bf16[16,512,128]{1,2,0:T(8,128)(2,1)}), bf16[16,512,128]{1,2,0:T(8,128)(2,1)}, u32[]{:S(2)}, u32[]{:S(2)}) async-start(bf16[16,512,128]{1,2,0:T(8,128)(2,1)} %pad_maximum_fusion), calls=%async_computation | async-start | bytes 4194304 | tf_op jit(solution)/shard_map/all_to_all | solution.py:125
  36.4 0.8 copy.101
  37.5 1.8 multiply_reduce_fusion
  40.1 2.1 mul.182
  42.2 4.2 %mul.195 = bf16[16,128,512]{2,1,0:T(8,128)(2,1)} reshape(bf16[16,128,4,128]{3,2,1,0:T(4,128)(2,1)} %mul.182) | data formatting | bytes 4194304 | tf_op jit(solution)/shard_map/mul | solution.py:24
  46.4 2.1 mul.178
  48.6 4.1 %mul.190 = bf16[16,128,512]{2,1,0:T(8,128)(2,1)} reshape(bf16[16,128,4,128]{3,2,1,0:T(4,128)(2,1)} %mul.178) | data formatting | bytes 4194304 | tf_op jit(solution)/shard_map/mul | solution.py:24
  53.3 0.9 fusion.206
  54.8 1.2 fusion.205
  56.3 1.8 fusion.52
  58.9 1.6 pad_maximum_fusion.2
  60.5 4.0 %all-to-all-done = bf16[16,512,128]{1,2,0:T(8,128)(2,1)} async-done(((bf16[16,512,128]{1,2,0:T(8,128)(2,1)}), bf16[16,512,128]{1,2,0:T(8,128)(2,1)}, u32[]{:S(2)}, u32[]{:S(2)}) %all-to-all-start) | async-done | bytes 2097184 | tf_op jit(solution)/shard_map/all_to_all | solution.py:125
  64.5 5.3 %all-to-all-start.3 = ((bf16[16,512,128]{1,2,0:T(8,128)(2,1)}), bf16[16,512,128]{1,2,0:T(8,128)(2,1)}, u32[]{:S(2)}, u32[]{:S(2)}) async-start(bf16[16,512,128]{1,2,0:T(8,128)(2,1)} %pad_maximum_fusion.2), calls=%async_computation.3 | async-start | bytes 4194304 | tf_op jit(solution)/shard_map/all_to_all | solution.py:125
  69.9 1.8 fusion.120
  71.7 2.0 fusion.85
  73.6 2.0 fusion.82
  76.3 1.0 copy-done.19
  78.1 0.8 copy-done.20
  78.9 0.7 fusion.61
  79.6 1.5 pad_maximum_fusion.1
  81.1 16.3 %all-to-all-done.3 = bf16[16,512,128]{1,2,0:T(8,128)(2,1)} async-done(((bf16[16,512,128]{1,2,0:T(8,128)(2,1)}), bf16[16,512,128]{1,2,0:T(8,128)(2,1)}, u32[]{:S(2)}, u32[]{:S(2)}) %all-to-all-start.3) | async-done | bytes 2097184 | tf_op jit(solution)/shard_map/all_to_all | solution.py:125
  97.4 6.2 %all-to-all-start.2 = ((bf16[16,512,128]{1,2,0:T(8,128)(2,1)}), bf16[16,512,128]{1,2,0:T(8,128)(2,1)}, u32[]{:S(2)}, u32[]{:S(2)}) async-start(bf16[16,512,128]{1,2,0:T(8,128)(2,1)} %pad_maximum_fusion.1), calls=%async_computation.2 | async-start | bytes 4194304 | tf_op jit(solution)/shard_map/all_to_all | solution.py:125
  103.9 0.8 copy.117
  104.6 1.6 reshape.445
  106.9 3.3 %fusion.76 = f32[256,512]{1,0:T(8,128)} fusion(bf16[16,128,128]{2,1,0:T(8,128)(2,1)} %param.31, bf16[16,512,128]{1,2,0:T(8,128)(2,1)} %all-to-all-done.3, bf16[16,512]{1,0:T(8,128)(2,1)S(1)} %bitcast.271, bf16[128,512]{1,0:T(8,128)(2,1)} %bitcast.258), kind=kOutput, calls=%fused_computation.64 | convolution fusion | flops 672661504 | bytes 2244608 | tf_op jit(solution)/shard_map/sma,san->mn/dot_general | solution.py:43
  110.2 1.5 fusion.108
  112.5 1.8 fusion.46
  114.2 3.1 %fusion.73 = f32[256,512]{1,0:T(8,128)} fusion(bf16[16,128,128]{2,1,0:T(8,128)(2,1)S(1)} %copy-done.7, bf16[16,512,128]{1,2,0:T(8,128)(2,1)} %all-to-all-done.3, bf16[16,512]{1,0:T(8,128)(2,1)S(1)} %bitcast.272, bf16[128,512]{1,0:T(8,128)(2,1)S(1)} %bitcast.262), kind=kOutput, calls=%fused_computation.63 | convolution fusion | flops 672661504 | bytes 2244608 | tf_op jit(solution)/shard_map/sma,san->mn/dot_general | solution.py:43
  117.3 1.6 fusion.107
  118.9 0.7 fusion.49
  120.2 1.6 pad_maximum_fusion.3
  121.8 8.4 %all-to-all-done.2 = bf16[16,512,128]{1,2,0:T(8,128)(2,1)} async-done(((bf16[16,512,128]{1,2,0:T(8,128)(2,1)}), bf16[16,512,128]{1,2,0:T(8,128)(2,1)}, u32[]{:S(2)}, u32[]{:S(2)}) %all-to-all-start.2) | async-done | bytes 2097184 | tf_op jit(solution)/shard_map/all_to_all | solution.py:125
  130.3 7.2 %all-to-all-start.4 = ((bf16[16,512,128]{1,2,0:T(8,128)(2,1)}), bf16[16,512,128]{1,2,0:T(8,128)(2,1)}, u32[]{:S(2)}, u32[]{:S(2)}) async-start(bf16[16,512,128]{1,2,0:T(8,128)(2,1)} %pad_maximum_fusion.3), calls=%async_computation.4 | async-start | bytes 4194304 | tf_op jit(solution)/shard_map/all_to_all | solution.py:125
  137.5 0.7 constant_dynamic-update-slice_fusion.3
  138.2 2.3 %convolution_add_fusion.2 = f32[256,512]{1,0:T(8,128)} fusion(f32[256,512]{1,0:T(8,128)} %bitcast.245, bf16[256,512]{1,0:T(8,128)(2,1)} %copy-done.28, bf16[64,8,4,128]{3,2,1,0:T(4,128)(2,1)S(1)} %bitcast.233), kind=kOutput, calls=%fused_computation.74 | convolution fusion | flops 134348800 | bytes 1835008 | tf_op jit(solution)/shard_map/mk,kn->mn/dot_general | solution.py:33
  140.5 2.1 fusion.88
  143.1 2.0 fusion.91
  145.4 1.1 copy-done.4
  147.1 17.1 %all-to-all-done.4 = bf16[16,512,128]{1,2,0:T(8,128)(2,1)} async-done(((bf16[16,512,128]{1,2,0:T(8,128)(2,1)}), bf16[16,512,128]{1,2,0:T(8,128)(2,1)}, u32[]{:S(2)}, u32[]{:S(2)}) %all-to-all-start.4) | async-done | bytes 2097184 | tf_op jit(solution)/shard_map/all_to_all | solution.py:125
  164.2 3.1 %fusion.126 = f32[16,256,128]{2,1,0:T(8,128)} fusion(bf16[16,128,128]{2,1,0:T(8,128)(2,1)S(1)} %copy-done.7, bf16[16,512,128]{1,2,0:T(8,128)(2,1)} %all-to-all-done.4), kind=kOutput, calls=%fused_computation.101 | convolution fusion | flops 134217728 | bytes 3670016 | tf_op jit(solution)/shard_map/qma,qac->qmc/dot_general | solution.py:53
  167.3 3.8 %fusion.79 = f32[256,512]{1,0:T(8,128)} fusion(f32[16,256,128]{2,1,0:T(8,128)} %fusion.126, bf16[16,128,128]{2,1,0:T(8,128)(2,1)S(1)} %copy-done.18, bf16[16,512,128]{1,2,0:T(8,128)(2,1)} %all-to-all-done.4, bf16[16,512]{1,0:T(8,128)(2,1)S(1)} %bitcast.273, bf16[128,512]{1,0:T(8,128)(2,1)S(1)} %bitcast.266), kind=kOutput, calls=%fused_computation.65 | convolution fusion | flops 673185792 | bytes 4341760 | tf_op jit(solution)/shard_map/sma,san->mn/dot_general | solution.py:43
  171.1 1.4 fusion.109
  173.0 0.9 convolution_bitcast_fusion
  175.3 2.6 %concatenate.59 = f32[53696]{0:T(1024)S(1)} concatenate(f32[16384]{0:T(1024)} %convolution_bitcast_fusion, f32[128]{0:T(128)S(1)} %convert_reduce_fusion, f32[20480]{0:T(1024)S(1)} %reshape.444, f32[64]{0:T(128)S(1)} %get-tuple-element.112, f32[16384]{0:T(1024)} %reshape.445, f32[256]{0:T(256)S(1)} %copy-done.45), dimensions={0} | concatenate | bytes 429568 | tf_op jit(solution)/shard_map/concatenate | solution.py:58
  178.2 14.0 %all_to_all.47 = f32[16,1,3356]{2,1,0:T(1,128)S(1)} all-to-all(f32[16,1,3356]{2,1,0:T(1,128)S(1)} %all_to_all.35), channel_id=1, replica_groups=mesh['node'=16,'batch'=16] {'node'}, dimensions={0} | all-to-all | bytes 429568 | tf_op jit(solution)/shard_map/all_to_all | solution.py:64
  192.4 0.8 broadcast_in_dim.4
  193.2 10.5 %all-to-all-start.6 = ((f32[16,1,3356]{2,1,0:T(1,128)}), f32[16,1,3356]{2,1,0:T(1,128)S(1)}, u32[]{:S(2)}, u32[]{:S(2)}) async-start(f32[16,1,3356]{2,1,0:T(1,128)} %broadcast_in_dim.4), calls=%async_computation.6 | async-start | bytes 442368 | tf_op jit(solution)/shard_map/all_to_all | solution.py:68
  203.9 0.8 copy.120
  204.8 9.6 %all-to-all-done.6 = f32[16,1,3356]{2,1,0:T(1,128)S(1)} async-done(((f32[16,1,3356]{2,1,0:T(1,128)}), f32[16,1,3356]{2,1,0:T(1,128)S(1)}, u32[]{:S(2)}, u32[]{:S(2)}) %all-to-all-start.6) | async-done | bytes 214816 | tf_op jit(solution)/shard_map/all_to_all | solution.py:68
  214.6 0.8 broadcast_in_dim.5
  215.3 3.5 %all-to-all-start.7 = ((f32[16,1,3356]{2,1,0:T(1,128)}), f32[16,1,3356]{2,1,0:T(1,128)S(1)}, u32[]{:S(2)}, u32[]{:S(2)}) async-start(f32[16,1,3356]{2,1,0:T(1,128)} %broadcast_in_dim.5), calls=%async_computation.7 | async-start | bytes 442368 | tf_op jit(solution)/shard_map/all_to_all | solution.py:70
  218.9 1.1 fusion.110
  220.0 0.8 convert_element_type.233
  220.8 6.4 %all-to-all-done.7 = f32[16,1,3356]{2,1,0:T(1,128)S(1)} async-done(((f32[16,1,3356]{2,1,0:T(1,128)}), f32[16,1,3356]{2,1,0:T(1,128)S(1)}, u32[]{:S(2)}, u32[]{:S(2)}) %all-to-all-start.7) | async-done | bytes 214816 | tf_op jit(solution)/shard_map/all_to_all | solution.py:70
  (146 shorter events, 19.4 us)
Async XLA Ops:
  0.6 52.1 %copy-start = (bf16[64,320]{1,0:T(8,128)(2,1)S(1)}, bf16[64,320]{1,0:T(8,128)(2,1)}, u32[]{:S(2)}) copy-start(bf16[64,320]{1,0:T(8,128)(2,1)} %param.24) | copy-start | bytes 122884
  2.0 26.6 %all-to-all-start.1 = ((bf16[16,1,4]{2,1,0:T(2,128)(2,1)}), bf16[16,1,4]{2,1,0:T(2,128)(2,1)S(1)}, u32[]{:S(2)}, u32[]{:S(2)}) async-start(bf16[16,1,4]{2,1,0:T(2,128)(2,1)} %compare_convert_fusion), calls=%async_computation.1 | async-start | bytes 16384 | tf_op jit(solution)/shard_map/all_to_all | solution.py:121
  10.3 3.9 %copy-start.6 = (bf16[16,128,128]{2,1,0:T(8,128)(2,1)S(1)}, bf16[16,128,128]{2,1,0:T(8,128)(2,1)}, u32[]{:S(2)}) copy-start(bf16[16,128,128]{2,1,0:T(8,128)(2,1)} %param.30) | copy-start | bytes 1572868
  10.3 3.9 %copy-start.16 = (bf16[16,128,128]{2,1,0:T(8,128)(2,1)S(1)}, bf16[16,128,128]{2,1,0:T(8,128)(2,1)}, u32[]{:S(2)}) copy-start(bf16[16,128,128]{2,1,0:T(8,128)(2,1)} %param.31) | copy-start | bytes 1572868
  11.5 0.7 copy-start.24
  11.5 0.8 copy-start.26
  24.7 1.6 copy-start.2
  28.6 7.7 %copy-start.33 = (bf16[512,384]{1,0:T(8,128)(2,1)S(1)}, bf16[512,384]{1,0:T(8,128)(2,1)}, u32[]{:S(2)}) copy-start(bf16[512,384]{1,0:T(8,128)(2,1)} %param.28) | copy-start | bytes 1179652
  28.6 35.9 %all-to-all-start = ((bf16[16,512,128]{1,2,0:T(8,128)(2,1)}), bf16[16,512,128]{1,2,0:T(8,128)(2,1)}, u32[]{:S(2)}, u32[]{:S(2)}) async-start(bf16[16,512,128]{1,2,0:T(8,128)(2,1)} %pad_maximum_fusion), calls=%async_computation | async-start | bytes 4194304 | tf_op jit(solution)/shard_map/all_to_all | solution.py:125
  35.4 1.8 copy-start.34
  37.4 2.6 %copy-start.17 = (bf16[16,128,128]{2,1,0:T(8,128)(2,1)S(1)}, bf16[16,128,128]{2,1,0:T(8,128)(2,1)}, u32[]{:S(2)}) copy-start(bf16[16,128,128]{2,1,0:T(8,128)(2,1)} %param.31) | copy-start | bytes 1572868
  42.2 4.2 %copy-start.7 = (bf16[16,128,128]{2,1,0:T(8,128)(2,1)S(1)}, bf16[16,128,128]{2,1,0:T(8,128)(2,1)}, u32[]{:S(2)}) copy-start(bf16[16,128,128]{2,1,0:T(8,128)(2,1)} %param.30) | copy-start | bytes 1572868
  48.6 4.2 %copy-start.8 = (bf16[1,4,64,512]{3,2,1,0:T(8,128)(2,1)S(1)}, bf16[1,4,64,512]{3,2,1,0:T(8,128)(2,1)}, u32[]{:S(2)}) copy-start(bf16[1,4,64,512]{3,2,1,0:T(8,128)(2,1)} %param.34) | copy-start | bytes 786436
  53.3 1.6 copy-start.1
  54.8 3.3 %copy-start.29 = (bf16[1,4,64,512]{3,2,1,0:T(8,128)(2,1)}, bf16[1,4,64,512]{3,2,1,0:T(8,128)(2,1)S(1)}, u32[]{:S(2)}) copy-start(bf16[1,4,64,512]{3,2,1,0:T(8,128)(2,1)S(1)} %get-tuple-element.106) | copy-start | bytes 786436
  56.2 1.9 copy-start.36
  60.5 9.3 %copy-start.10 = (bf16[1,256,512]{2,1,0:T(8,128)(2,1)S(1)}, bf16[1,256,512]{2,1,0:T(8,128)(2,1)}, u32[]{:S(2)}) copy-start(bf16[1,256,512]{2,1,0:T(8,128)(2,1)} %param.35) | copy-start | bytes 786436
  60.5 9.4 %copy-start.43 = (bf16[256,64]{0,1:T(8,128)(2,1)S(1)}, bf16[256,64]{0,1:T(8,128)(2,1)}, u32[]{:S(2)}) copy-start(bf16[256,64]{0,1:T(8,128)(2,1)} %param.26) | copy-start | bytes 98308
  64.5 32.9 %all-to-all-start.3 = ((bf16[16,512,128]{1,2,0:T(8,128)(2,1)}), bf16[16,512,128]{1,2,0:T(8,128)(2,1)}, u32[]{:S(2)}, u32[]{:S(2)}) async-start(bf16[16,512,128]{1,2,0:T(8,128)(2,1)} %pad_maximum_fusion.2), calls=%async_computation.3 | async-start | bytes 4194304 | tf_op jit(solution)/shard_map/all_to_all | solution.py:125
  69.8 3.8 %copy-start.37 = (bf16[16,8,4,128]{3,1,2,0:T(8,128)(2,1)S(1)}, bf16[16,8,4,128]{3,1,2,0:T(8,128)(2,1)}, u32[]{:S(2)}) copy-start(bf16[16,8,4,128]{3,1,2,0:T(8,128)(2,1)} %copy.178) | copy-start | bytes 393220
  75.6 1.7 copy-start.19
  76.0 2.1 copy-start.11
  76.3 1.7 copy-start.13
  77.3 1.6 copy-start.20
  97.4 32.8 %all-to-all-start.2 = ((bf16[16,512,128]{1,2,0:T(8,128)(2,1)}), bf16[16,512,128]{1,2,0:T(8,128)(2,1)}, u32[]{:S(2)}, u32[]{:S(2)}) async-start(bf16[16,512,128]{1,2,0:T(8,128)(2,1)} %pad_maximum_fusion.1), calls=%async_computation.2 | async-start | bytes 4194304 | tf_op jit(solution)/shard_map/all_to_all | solution.py:125
  106.9 3.3 %copy-start.30 = (bf16[1,4,64,512]{3,2,1,0:T(8,128)(2,1)S(1)}, bf16[1,4,64,512]{3,2,1,0:T(8,128)(2,1)}, u32[]{:S(2)}) copy-start(bf16[1,4,64,512]{3,2,1,0:T(8,128)(2,1)} %get-tuple-element.107) | copy-start | bytes 786436
  110.2 2.3 copy-start.38
  111.7 0.7 copy-start.31
  112.5 1.8 copy-start.39
  117.3 1.6 copy-start.40
  118.9 0.8 copy-start.28
  118.9 1.3 copy-start.23
  121.8 15.6 %copy-start.14 = (bf16[256,512]{1,0:T(8,128)(2,1)S(1)}, bf16[256,512]{1,0:T(8,128)(2,1)}, u32[]{:S(2)}) copy-start(bf16[256,512]{1,0:T(8,128)(2,1)} %copy-done.13) | copy-start | bytes 786436
  130.3 34.0 %all-to-all-start.4 = ((bf16[16,512,128]{1,2,0:T(8,128)(2,1)}), bf16[16,512,128]{1,2,0:T(8,128)(2,1)}, u32[]{:S(2)}, u32[]{:S(2)}) async-start(bf16[16,512,128]{1,2,0:T(8,128)(2,1)} %pad_maximum_fusion.3), calls=%async_computation.4 | async-start | bytes 4194304 | tf_op jit(solution)/shard_map/all_to_all | solution.py:125
  137.4 3.1 %copy-start.41 = (bf16[16,8,4,128]{3,1,2,0:T(8,128)(2,1)S(1)}, bf16[16,8,4,128]{3,1,2,0:T(8,128)(2,1)}, u32[]{:S(2)}) copy-start(bf16[16,8,4,128]{3,1,2,0:T(8,128)(2,1)} %copy.178) | copy-start | bytes 393220
  138.2 4.4 %copy-start.15 = (bf16[256,512]{1,0:T(8,128)(2,1)S(1)}, bf16[256,512]{1,0:T(8,128)(2,1)}, u32[]{:S(2)}) copy-start(bf16[256,512]{1,0:T(8,128)(2,1)} %copy-done.13) | copy-start | bytes 786436
  140.5 2.4 %copy-start.3 = (bf16[1,4,320,512]{3,2,1,0:T(8,128)(2,1)S(1)}, bf16[1,4,320,512]{3,2,1,0:T(8,128)(2,1)}, u32[]{:S(2)}) copy-start(bf16[1,4,320,512]{3,2,1,0:T(8,128)(2,1)} %constant_dynamic-update-slice_fusion.3) | copy-start | bytes 3932164
  140.5 2.5 %copy-start.12 = (bf16[256,512]{1,0:T(8,128)(2,1)S(1)}, bf16[256,512]{1,0:T(8,128)(2,1)}, u32[]{:S(2)}) copy-start(bf16[256,512]{1,0:T(8,128)(2,1)} %copy-done.11) | copy-start | bytes 786436
  145.4 1.1 copy-start.4
  147.0 20.3 %copy-start.18 = (bf16[16,128,128]{2,1,0:T(8,128)(2,1)S(1)}, bf16[16,128,128]{2,1,0:T(8,128)(2,1)}, u32[]{:S(2)}) copy-start(bf16[16,128,128]{2,1,0:T(8,128)(2,1)} %param.31) | copy-start | bytes 1572868
  147.0 20.3 %copy-start.42 = (bf16[16,8,4,128]{3,1,2,0:T(8,128)(2,1)S(1)}, bf16[16,8,4,128]{3,1,2,0:T(8,128)(2,1)}, u32[]{:S(2)}) copy-start(bf16[16,8,4,128]{3,1,2,0:T(8,128)(2,1)} %copy.178) | copy-start | bytes 393220
  167.3 3.8 %copy-start.21 = (f32[256,512]{1,0:T(8,128)S(1)}, f32[256,512]{1,0:T(8,128)}, u32[]{:S(2)}) copy-start(f32[256,512]{1,0:T(8,128)} %convolution_add_fusion.2) | copy-start | bytes 1572868
  167.3 3.8 %copy-start.32 = (bf16[256,512]{1,0:T(8,128)(2,1)S(1)}, bf16[256,512]{1,0:T(8,128)(2,1)}, u32[]{:S(2)}) copy-start(bf16[256,512]{1,0:T(8,128)(2,1)} %copy-done.31) | copy-start | bytes 786436
  171.1 1.9 copy-start.25
  171.1 1.9 copy-start.27
  172.6 1.4 copy-start.35
  174.0 1.0 copy-start.9
  174.3 0.9 copy-start.45
  174.9 28.7 %copy-start.46 = (f32[256]{0:T(256)S(1)}, f32[256]{0:T(256)}, u32[]{:S(2)}) copy-start(f32[256]{0:T(256)} %param.27) | copy-start | bytes 3076
  175.2 28.4 %copy-start.44 = (bf16[256,64]{0,1:T(8,128)(2,1)S(1)}, bf16[256,64]{0,1:T(8,128)(2,1)}, u32[]{:S(2)}) copy-start(bf16[256,64]{0,1:T(8,128)(2,1)} %param.26) | copy-start | bytes 98308
  175.2 43.7 %copy-start.5 = (bf16[1,4,320,512]{3,2,1,0:T(8,128)(2,1)S(1)}, bf16[1,4,320,512]{3,2,1,0:T(8,128)(2,1)}, u32[]{:S(2)}) copy-start(bf16[1,4,320,512]{3,2,1,0:T(8,128)(2,1)} %copy-done.4) | copy-start | bytes 3932164
  175.2 43.7 %copy-start.22 = (bf16[1,6,64,512]{3,2,1,0:T(8,128)(2,1)S(1)}, bf16[1,6,64,512]{3,2,1,0:T(8,128)(2,1)}, u32[]{:S(2)}) copy-start(bf16[1,6,64,512]{3,2,1,0:T(8,128)(2,1)} %param.21) | copy-start | bytes 1179652
  175.2 43.7 %copy-start.47 = (f32[64]{0:T(128)S(1)}, f32[64]{0:T(128)}, u32[]{:S(2)}) copy-start(f32[64]{0:T(128)} %param.25) | copy-start | bytes 772
  193.2 21.2 %all-to-all-start.6 = ((f32[16,1,3356]{2,1,0:T(1,128)}), f32[16,1,3356]{2,1,0:T(1,128)S(1)}, u32[]{:S(2)}, u32[]{:S(2)}) async-start(f32[16,1,3356]{2,1,0:T(1,128)} %broadcast_in_dim.4), calls=%async_computation.6 | async-start | bytes 442368 | tf_op jit(solution)/shard_map/all_to_all | solution.py:68
  215.3 11.8 %all-to-all-start.7 = ((f32[16,1,3356]{2,1,0:T(1,128)}), f32[16,1,3356]{2,1,0:T(1,128)S(1)}, u32[]{:S(2)}, u32[]{:S(2)}) async-start(f32[16,1,3356]{2,1,0:T(1,128)} %broadcast_in_dim.5), calls=%async_computation.7 | async-start | bytes 442368 | tf_op jit(solution)/shard_map/all_to_all | solution.py:70

commit v4 on v3

--- a/solution.py
+++ b/solution.py
@@ -121,28 +121,64 @@
     recv_dst = lax.all_to_all(own_dst, "node", split_axis=0, concat_axis=0, tiled=True)
     dst_placer = spread_onehot(recv_dst, eye_slots)
 
-    def swap(first, second):
-        got_both = lax.all_to_all(
-            jnp.concatenate([first, second], axis=1),
-            "node",
-            split_axis=0,
-            concat_axis=0,
-            tiled=True,
+    def swap(pieces):
+        got_all = lax.all_to_all(
+            jnp.concatenate(pieces, axis=1), "node", split_axis=0, concat_axis=0, tiled=True
         )
-        return got_both[:, :row_count], got_both[:, row_count:]
-
-    def push_hop(values_fwd, values_bwd):
-        got_fwd, got_bwd = swap(
-            tile_products(values_fwd, spread_fwd), tile_products(values_bwd, spread_bwd)
+        return [got_all[:, k * row_count : (k + 1) * row_count] for k in range(len(pieces))]
+
+    grad_parts = jnp.einsum(
+        "co,wtcn->wton", w_mix, residual_cotangent, preferred_element_type=jnp.float32
+    )
+
+    def group_of(index):
+        return grad_parts[:, :, index * channel_count : (index + 1) * channel_count].reshape(
+            row_count, local_nodes
         )
-        return place_rows(got_fwd, dst_placer), place_rows(got_bwd, dst_placer)
-
-    far_fwd, far_bwd = push_hop(flat_hidden, flat_hidden)
-    hop_fwd = (near_apply(flat_hidden, dense_fwd) + far_fwd).astype(jnp.bfloat16)
-    hop_bwd = (near_apply(flat_hidden, dense_bwd) + far_bwd).astype(jnp.bfloat16)
-    far_fwd, far_bwd = push_hop(hop_fwd, hop_bwd)
-    two_fwd = (near_apply(hop_fwd, dense_fwd) + far_fwd).astype(jnp.bfloat16)
-    two_bwd = (near_apply(hop_bwd, dense_bwd) + far_bwd).astype(jnp.bfloat16)
+
+    back2_fwd = group_of(2).astype(jnp.bfloat16)
+    back2_bwd = group_of(4).astype(jnp.bfloat16)
+
+    got_fwd, got_bwd, got2_fwd, got2_bwd = swap(
+        [
+            tile_products(flat_hidden, spread_fwd),
+            tile_products(flat_hidden, spread_bwd),
+            pick_rows(back2_fwd, dst_placer),
+            pick_rows(back2_bwd, dst_placer),
+        ]
+    )
+    hop_fwd = (near_apply(flat_hidden, dense_fwd) + place_rows(got_fwd, dst_placer)).astype(
+        jnp.bfloat16
+    )
+    hop_bwd = (near_apply(flat_hidden, dense_bwd) + place_rows(got_bwd, dst_placer)).astype(
+        jnp.bfloat16
+    )
+    near1_fwd = place_rows(tile_backward(got2_fwd, remote_fwd).astype(jnp.bfloat16), src_placer)
+    near1_bwd = place_rows(tile_backward(got2_bwd, remote_bwd).astype(jnp.bfloat16), src_placer)
+    back1_fwd = (group_of(1) + near_transpose(back2_fwd, dense_fwd) + near1_fwd).astype(
+        jnp.bfloat16
+    )
+    back1_bwd = (group_of(3) + near_transpose(back2_bwd, dense_bwd) + near1_bwd).astype(
+        jnp.bfloat16
+    )
+    got_fwd, got_bwd, got1_fwd, got1_bwd = swap(
+        [
+            tile_products(hop_fwd, spread_fwd),
+            tile_products(hop_bwd, spread_bwd),
+            pick_rows(back1_fwd, dst_placer),
+            pick_rows(back1_bwd, dst_placer),
+        ]
+    )
+    two_fwd = (near_apply(hop_fwd, dense_fwd) + place_rows(got_fwd, dst_placer)).astype(
+        jnp.bfloat16
+    )
+    two_bwd = (near_apply(hop_bwd, dense_bwd) + place_rows(got_bwd, dst_placer)).astype(
+        jnp.bfloat16
+    )
+    combined = (tile_backward(got1_fwd, remote_fwd) + tile_backward(got1_bwd, remote_bwd)).astype(
+        jnp.bfloat16
+    )
+    far_total = place_rows(combined, src_placer)
     stacked_parts = jnp.concatenate(
         [
             hidden,
@@ -165,9 +201,6 @@
         jnp.einsum("sc,wcn->wsn", w_skip, last_step, preferred_element_type=jnp.float32)
         + b_skip[None, :, None]
     ).astype(jnp.bfloat16)
-    grad_parts = jnp.einsum(
-        "co,wtcn->wton", w_mix, residual_cotangent, preferred_element_type=jnp.float32
-    )
     grad_mix = jnp.einsum(
         "wtcn,wton->co", residual_cotangent, stacked_parts, preferred_element_type=jnp.float32
     )
@@ -175,31 +208,6 @@
     grad_skip = jnp.einsum("wsn,wcn->sc", cot_skip, last_step, preferred_element_type=jnp.float32)
     grad_bskip = jnp.sum(cot_skip.astype(jnp.float32), axis=(0, 2))
 
-    def group_of(index):
-        return grad_parts[:, :, index * channel_count : (index + 1) * channel_count].reshape(
-            row_count, local_nodes
-        )
-
-    back2_fwd = group_of(2).astype(jnp.bfloat16)
-    back2_bwd = group_of(4).astype(jnp.bfloat16)
-
-    def fetch_rows(grad_fwd, grad_bwd):
-        return swap(pick_rows(grad_fwd, dst_placer), pick_rows(grad_bwd, dst_placer))
-
-    got_fwd, got_bwd = fetch_rows(back2_fwd, back2_bwd)
-    near1_fwd = place_rows(tile_backward(got_fwd, remote_fwd).astype(jnp.bfloat16), src_placer)
-    near1_bwd = place_rows(tile_backward(got_bwd, remote_bwd).astype(jnp.bfloat16), src_placer)
-    back1_fwd = (group_of(1) + near_transpose(back2_fwd, dense_fwd) + near1_fwd).astype(
-        jnp.bfloat16
-    )
-    back1_bwd = (group_of(3) + near_transpose(back2_bwd, dense_bwd) + near1_bwd).astype(
-        jnp.bfloat16
-    )
-    got_fwd, got_bwd = fetch_rows(back1_fwd, back1_bwd)
-    combined = (tile_backward(got_fwd, remote_fwd) + tile_backward(got_bwd, remote_bwd)).astype(
-        jnp.bfloat16
-    )
-    far_total = place_rows(combined, src_placer)
     skip_back = jnp.einsum("sc,wsn->wcn", w_skip, cot_skip, preferred_element_type=jnp.float32)
     direct = (
         grad_parts[:, :, :channel_count]

time: 233 us -> 265 us (1.14)
  waiting for transfers between devices: 61.9 us -> 106 us
  starting transfers between devices: 47.1 us -> 36.4 us
  blocking collectives: 14 us -> 11.3 us
    all_to_all x4 -> x2, waiting for transfers between devices: 45.8 us -> 89.9 us  [swap(): lax.all_to_all(jnp.concatenate(pieces, axis=1), 'node', split_axis=0, con...]
    all_to_all x4 -> x2, starting transfers between devices: 25.6 us -> 11.8 us  [swap(): lax.all_to_all(jnp.concatenate(pieces, axis=1), 'node', split_axis=0, con...]
    all_to_all x1, starting transfers between devices: 10.5 us -> 13.5 us  [exchange_sum(): part = lax.all_to_all(part, 'batch', 0, 0, tiled=True).sum(axis=0)]
    dot_general x4, matrix products: 2.96 us -> 5.69 us  [tile_products(): jnp.einsum('mn,qan->qma', values, spread_tiles, preferred_element_type=jn...]
    all_to_all x1, blocking collectives: 14 us -> 11.3 us  [exchange_sum(): lax.all_to_all(flat.reshape(node_count, padded // node_count), 'node', 0,...]
    concatenate x4 -> x2, other arithmetic: 6.29 us -> 4.6 us  [swap(): jnp.concatenate(pieces, axis=1)]
    unnamed x104 -> x88, local copies, waits for them, and re-layouts: 10.1 us -> 9.41 us
  transfers between devices with their start and end apart: 7 -> 5, of which waited for: 6 -> 4; matrix products, arithmetic and copies ran while one was open for 34% -> 20% of each run, Pallas kernels for 0% -> 0%
where the time goes in v4:
time: 265 us; the launch traced here: 263 us
  waiting for transfers between devices  106 us (40%)
  matrix products  46.2 us (17%)
  local copies, waits for them, and re-layouts  44.1 us (17%)
  starting transfers between devices  36.4 us (14%)
  other arithmetic  17.7 us (7%)
  blocking collectives  11.3 us (4%)
    all_to_all x2, waiting for transfers between devices, swap(): lax.all_to_all(jnp.concatenate(pieces, axis=1), 'node', split_axis=0, con...  89.9 us
    mul x9, local copies, waits for them, and re-layouts, spread_onehot(): placed = tile_vals[:, :, None, :] * chooser[:, None, :, None]  20.9 us
    dot_general x7, matrix products, place_rows(): jnp.einsum('sma,san->mn', pieces, placer, preferred_element_type=jnp.floa...  18.3 us
    all_to_all x1, starting transfers between devices, exchange_sum(): part = lax.all_to_all(part, 'batch', 0, 0, tiled=True).sum(axis=0)  13.5 us
    all_to_all x2, starting transfers between devices, swap(): lax.all_to_all(jnp.concatenate(pieces, axis=1), 'node', split_axis=0, con...  11.8 us
    all_to_all x1, blocking collectives, exchange_sum(): lax.all_to_all(flat.reshape(node_count, padded // node_count), 'node', 0,...  11.3 us
    unnamed x88, local copies, waits for them, and re-layouts  9.41 us
    all_to_all x1, waiting for transfers between devices, exchange_sum(): part = lax.all_to_all(part, 'batch', 0, 0, tiled=True).sum(axis=0)  8.85 us
  transfers between devices with their start and end apart: 5, of which 4 were waited for; matrix products, arithmetic and copies ran while one was open for 20% of the time, Pallas kernels for 0%

profile of v4, /device:TPU:1, one launch (start us, length us, event | category | flops | bytes accessed | tf_op | source)
XLA Modules:
  0.0 263.1 jit_solution(5036512923675069372)
XLA Ops:
  0.7 1.4 compare_convert_fusion
  2.0 7.6 %all-to-all-start = ((bf16[16,1,4]{2,1,0:T(2,128)(2,1)}), bf16[16,1,4]{2,1,0:T(2,128)(2,1)S(1)}, u32[]{:S(2)}, u32[]{:S(2)}) async-start(bf16[16,1,4]{2,1,0:T(2,128)(2,1)} %compare_convert_fusion), calls=%async_computation | async-start | bytes 16384 | tf_op jit(solution)/shard_map/all_to_all | solution.py:121
  9.6 1.1 fusion.207
  10.8 1.1 fusion.65
  11.9 0.9 constant_dynamic-update-slice_fusion.4
  13.4 1.5 copy-done.1
  14.9 0.8 fusion.206
  15.8 3.6 %broadcast_multiply_fusion.1 = (bf16[16,128,4,128]{3,2,1,0:T(4,128)(2,1)}, bf16[16,128,4,128]{3,2,1,0:T(4,128)(2,1)}) fusion(bf16[16,4]{1,0:T(8,128)(2,1)S(1)} %fusion.201, bf16[16,128,128]{2,1,0:T(8,128)(2,1)S(1)} %copy-done.4, bf16[16,128,128]{2,1,0:T(8,128)(2,1)S(1)} %copy-done.12), kind=kLoop, calls=%fused_computation.133 | loop fusion | flops 2097152 | bytes 5243008 | tf_op jit(solution)/shard_map/mul | solution.py:24
  19.4 4.1 %mul.184 = bf16[16,128,512]{2,1,0:T(8,128)(2,1)} reshape(bf16[16,128,4,128]{3,2,1,0:T(4,128)(2,1)} %get-tuple-element.115) | data formatting | bytes 4194304 | tf_op jit(solution)/shard_map/mul | solution.py:24
  23.5 4.1 %mul.181 = bf16[16,128,512]{2,1,0:T(8,128)(2,1)} reshape(bf16[16,128,4,128]{3,2,1,0:T(4,128)(2,1)} %get-tuple-element.114) | data formatting | bytes 4194304 | tf_op jit(solution)/shard_map/mul | solution.py:24
  27.6 2.5 fusion.45
  30.1 1.7 fusion.44
  32.8 1.8 fusion.52
  34.6 0.7 fusion.55
  35.8 2.3 pad_maximum_fusion
  38.1 6.9 %all-to-all-start.1 = ((bf16[16,1024,128]{1,2,0:T(8,128)(2,1)}), bf16[16,1024,128]{1,2,0:T(8,128)(2,1)}, u32[]{:S(2)}, u32[]{:S(2)}) async-start(bf16[16,1024,128]{1,2,0:T(8,128)(2,1)} %pad_maximum_fusion), calls=%async_computation.1 | async-start | bytes 8388608 | tf_op jit(solution)/shard_map/all_to_all | solution.py:125
  45.1 0.8 copy.107
  45.9 1.4 reshape.467
  47.4 1.8 multiply_reduce_fusion
  50.2 2.1 mul.182
  52.3 4.1 %mul.195 = bf16[16,128,512]{2,1,0:T(8,128)(2,1)} reshape(bf16[16,128,4,128]{3,2,1,0:T(4,128)(2,1)} %mul.182) | data formatting | bytes 4194304 | tf_op jit(solution)/shard_map/mul | solution.py:24
  56.4 2.1 mul.178
  58.5 4.1 %mul.190 = bf16[16,128,512]{2,1,0:T(8,128)(2,1)} reshape(bf16[16,128,4,128]{3,2,1,0:T(4,128)(2,1)} %mul.178) | data formatting | bytes 4194304 | tf_op jit(solution)/shard_map/mul | solution.py:24
  62.6 2.6 fusion.205
  65.2 40.8 %all-to-all-done.1 = bf16[16,1024,128]{1,2,0:T(8,128)(2,1)} async-done(((bf16[16,1024,128]{1,2,0:T(8,128)(2,1)}), bf16[16,1024,128]{1,2,0:T(8,128)(2,1)}, u32[]{:S(2)}, u32[]{:S(2)}) %all-to-all-start.1) | async-done | bytes 4194336 | tf_op jit(solution)/shard_map/all_to_all | solution.py:125
  105.9 3.2 %fusion.76 = f32[256,512]{1,0:T(8,128)} fusion(bf16[16,128,128]{2,1,0:T(8,128)(2,1)} %param.31, bf16[16,1024,128]{1,2,0:T(8,128)(2,1)} %all-to-all-done.1, bf16[16,512]{1,0:T(8,128)(2,1)S(1)} %bitcast.277, bf16[128,512]{1,0:T(8,128)(2,1)} %bitcast.257), kind=kOutput, calls=%fused_computation.62 | convolution fusion | flops 672661504 | bytes 2244608 | tf_op jit(solution)/shard_map/sma,san->mn/dot_general | solution.py:43
  109.2 1.6 fusion.108
  110.8 0.7 copy-done.24
  111.5 1.7 fusion.46
  113.3 3.1 %fusion.73 = f32[256,512]{1,0:T(8,128)} fusion(bf16[16,128,128]{2,1,0:T(8,128)(2,1)S(1)} %copy-done.4, bf16[16,1024,128]{1,2,0:T(8,128)(2,1)} %all-to-all-done.1, bf16[16,512]{1,0:T(8,128)(2,1)S(1)} %bitcast.278, bf16[128,512]{1,0:T(8,128)(2,1)} %bitcast.258), kind=kOutput, calls=%fused_computation.61 | convolution fusion | flops 672661504 | bytes 2244608 | tf_op jit(solution)/shard_map/sma,san->mn/dot_general | solution.py:43
  116.3 1.5 fusion.107
  117.9 0.7 fusion.49
  118.7 2.0 fusion.82
  121.0 2.1 fusion.85
  123.5 0.8 fusion.58
  124.3 0.9 copy-done.15
  125.2 0.8 fusion.61
  126.4 2.3 pad_maximum_fusion.1
  128.7 4.9 %all-to-all-start.2 = ((bf16[16,1024,128]{1,2,0:T(8,128)(2,1)}), bf16[16,1024,128]{1,2,0:T(8,128)(2,1)}, u32[]{:S(2)}, u32[]{:S(2)}) async-start(bf16[16,1024,128]{1,2,0:T(8,128)(2,1)} %pad_maximum_fusion.1), calls=%async_computation.2 | async-start | bytes 8388608 | tf_op jit(solution)/shard_map/all_to_all | solution.py:125
  133.9 0.7 copy.117
  134.6 1.0 reshape.445
  136.3 1.7 fusion.120
  138.0 1.7 constant_dynamic-update-slice_fusion.3
  139.7 2.2 convolution_add_fusion.1
  141.9 49.2 %all-to-all-done.2 = bf16[16,1024,128]{1,2,0:T(8,128)(2,1)} async-done(((bf16[16,1024,128]{1,2,0:T(8,128)(2,1)}), bf16[16,1024,128]{1,2,0:T(8,128)(2,1)}, u32[]{:S(2)}, u32[]{:S(2)}) %all-to-all-start.2) | async-done | bytes 4194336 | tf_op jit(solution)/shard_map/all_to_all | solution.py:125
  191.1 3.1 %fusion.126 = f32[16,256,128]{2,1,0:T(8,128)} fusion(bf16[16,128,128]{2,1,0:T(8,128)(2,1)S(1)} %copy-done.4, bf16[16,1024,128]{1,2,0:T(8,128)(2,1)} %all-to-all-done.2), kind=kOutput, calls=%fused_computation.99 | convolution fusion | flops 134217728 | bytes 3670016 | tf_op jit(solution)/shard_map/qma,qac->qmc/dot_general | solution.py:53
  194.2 4.0 %fusion.79 = f32[256,512]{1,0:T(8,128)} fusion(f32[16,256,128]{2,1,0:T(8,128)} %fusion.126, bf16[16,128,128]{2,1,0:T(8,128)(2,1)} %param.31, bf16[16,1024,128]{1,2,0:T(8,128)(2,1)} %all-to-all-done.2, bf16[16,512]{1,0:T(8,128)(2,1)} %bitcast.281, bf16[128,512]{1,0:T(8,128)(2,1)} %bitcast.259), kind=kOutput, calls=%fused_computation.63 | convolution fusion | flops 673185792 | bytes 4341760 | tf_op jit(solution)/shard_map/sma,san->mn/dot_general | solution.py:43
  198.2 1.4 fusion.109
  201.1 2.0 fusion.88
  203.4 2.0 fusion.91
  206.2 0.9 copy-done.3
  207.8 1.0 concatenate.51
  209.1 11.3 %all_to_all.37 = f32[16,1,3356]{2,1,0:T(1,128)S(1)} all-to-all(f32[16,1,3356]{2,1,0:T(1,128)S(1)} %all_to_all.27), channel_id=1, replica_groups=mesh['node'=16,'batch'=16] {'node'}, dimensions={0} | all-to-all | bytes 429568 | tf_op jit(solution)/shard_map/all_to_all | solution.py:64
  220.6 0.8 broadcast_in_dim.4
  221.4 13.5 %all-to-all-start.4 = ((f32[16,1,3356]{2,1,0:T(1,128)}), f32[16,1,3356]{2,1,0:T(1,128)S(1)}, u32[]{:S(2)}, u32[]{:S(2)}) async-start(f32[16,1,3356]{2,1,0:T(1,128)} %broadcast_in_dim.4), calls=%async_computation.4 | async-start | bytes 442368 | tf_op jit(solution)/shard_map/all_to_all | solution.py:68
  235.2 0.8 copy.120
  236.0 0.8 convert_element_type.233
  236.8 8.8 %all-to-all-done.4 = f32[16,1,3356]{2,1,0:T(1,128)S(1)} async-done(((f32[16,1,3356]{2,1,0:T(1,128)}), f32[16,1,3356]{2,1,0:T(1,128)S(1)}, u32[]{:S(2)}, u32[]{:S(2)}) %all-to-all-start.4) | async-done | bytes 214816 | tf_op jit(solution)/shard_map/all_to_all | solution.py:68
  245.8 0.8 broadcast_in_dim.5
  246.6 3.5 %all-to-all-start.5 = ((f32[16,1,3356]{2,1,0:T(1,128)}), f32[16,1,3356]{2,1,0:T(1,128)S(1)}, u32[]{:S(2)}, u32[]{:S(2)}) async-start(f32[16,1,3356]{2,1,0:T(1,128)} %broadcast_in_dim.5), calls=%async_computation.5 | async-start | bytes 442368 | tf_op jit(solution)/shard_map/all_to_all | solution.py:70
  250.2 1.1 fusion.110
  251.2 7.2 %all-to-all-done.5 = f32[16,1,3356]{2,1,0:T(1,128)S(1)} async-done(((f32[16,1,3356]{2,1,0:T(1,128)}), f32[16,1,3356]{2,1,0:T(1,128)S(1)}, u32[]{:S(2)}, u32[]{:S(2)}) %all-to-all-start.5) | async-done | bytes 214816 | tf_op jit(solution)/shard_map/all_to_all | solution.py:70
  261.7 0.7 mul.214
  262.4 0.7 copy.121
  (124 shorter events, 12.6 us)
Async XLA Ops:
  0.6 12.1 %copy-start = (bf16[64,320]{1,0:T(8,128)(2,1)S(1)}, bf16[64,320]{1,0:T(8,128)(2,1)}, u32[]{:S(2)}) copy-start(bf16[64,320]{1,0:T(8,128)(2,1)} %param.24) | copy-start | bytes 122884
  2.0 30.5 %all-to-all-start = ((bf16[16,1,4]{2,1,0:T(2,128)(2,1)}), bf16[16,1,4]{2,1,0:T(2,128)(2,1)S(1)}, u32[]{:S(2)}, u32[]{:S(2)}) async-start(bf16[16,1,4]{2,1,0:T(2,128)(2,1)} %compare_convert_fusion), calls=%async_computation | async-start | bytes 16384 | tf_op jit(solution)/shard_map/all_to_all | solution.py:121
  9.6 3.2 %copy-start.6 = (bf16[1,4,64,512]{3,2,1,0:T(8,128)(2,1)S(1)}, bf16[1,4,64,512]{3,2,1,0:T(8,128)(2,1)}, u32[]{:S(2)}) copy-start(bf16[1,4,64,512]{3,2,1,0:T(8,128)(2,1)} %param.34) | copy-start | bytes 786436
  10.7 1.1 copy-start.18
  10.7 1.1 copy-start.20
  12.8 2.9 %copy-start.38 = (s32[16]{0:T(128)S(1)}, s32[16]{0:T(128)}, u32[]{:S(2)}) copy-start(s32[16]{0:T(128)} %param.32) | copy-start | bytes 196
  12.8 3.0 %copy-start.4 = (bf16[16,128,128]{2,1,0:T(8,128)(2,1)S(1)}, bf16[16,128,128]{2,1,0:T(8,128)(2,1)}, u32[]{:S(2)}) copy-start(bf16[16,128,128]{2,1,0:T(8,128)(2,1)} %param.30) | copy-start | bytes 1572868
  12.8 3.0 %copy-start.12 = (bf16[16,128,128]{2,1,0:T(8,128)(2,1)S(1)}, bf16[16,128,128]{2,1,0:T(8,128)(2,1)}, u32[]{:S(2)}) copy-start(bf16[16,128,128]{2,1,0:T(8,128)(2,1)} %param.31) | copy-start | bytes 1572868
  13.4 1.6 copy-start.1
  27.6 2.5 copy-start.2
  32.7 1.9 copy-start.28
  32.8 88.2 %copy-start.33 = (bf16[2,8,4,128]{3,1,2,0:T(8,128)(2,1)}, bf16[2,8,4,128]{3,1,2,0:T(8,128)(2,1)S(1)}, u32[]{:S(2)}) copy-start(bf16[2,8,4,128]{3,1,2,0:T(8,128)(2,1)S(1)} %copy.180) | copy-start | bytes 49156
  34.6 1.2 copy-start.5
  38.1 6.9 %copy-start.26 = (bf16[512,384]{1,0:T(8,128)(2,1)S(1)}, bf16[512,384]{1,0:T(8,128)(2,1)}, u32[]{:S(2)}) copy-start(bf16[512,384]{1,0:T(8,128)(2,1)} %param.29) | copy-start | bytes 1179652
  38.1 67.8 %all-to-all-start.1 = ((bf16[16,1024,128]{1,2,0:T(8,128)(2,1)}), bf16[16,1024,128]{1,2,0:T(8,128)(2,1)}, u32[]{:S(2)}, u32[]{:S(2)}) async-start(bf16[16,1024,128]{1,2,0:T(8,128)(2,1)} %pad_maximum_fusion), calls=%async_computation.1 | async-start | bytes 8388608 | tf_op jit(solution)/shard_map/all_to_all | solution.py:125
  47.4 2.7 %copy-start.13 = (bf16[16,128,128]{2,1,0:T(8,128)(2,1)S(1)}, bf16[16,128,128]{2,1,0:T(8,128)(2,1)}, u32[]{:S(2)}) copy-start(bf16[16,128,128]{2,1,0:T(8,128)(2,1)} %param.31) | copy-start | bytes 1572868
  49.7 74.5 %copy-start.35 = (bf16[2,8,4,128]{3,1,2,0:T(8,128)(2,1)}, bf16[2,8,4,128]{3,1,2,0:T(8,128)(2,1)S(1)}, u32[]{:S(2)}) copy-start(bf16[2,8,4,128]{3,1,2,0:T(8,128)(2,1)S(1)} %copy.179) | copy-start | bytes 49156
  109.2 2.4 copy-start.29
  110.8 0.7 copy-start.24
  116.3 1.6 copy-start.30
  117.9 2.7 %copy-start.22 = (bf16[256,512]{1,0:T(8,128)(2,1)}, bf16[256,512]{1,0:T(8,128)(2,1)S(1)}, u32[]{:S(2)}) copy-start(bf16[256,512]{1,0:T(8,128)(2,1)S(1)} %fusion.107) | copy-start | bytes 786436
  121.0 3.3 %copy-start.10 = (bf16[256,512]{1,0:T(8,128)(2,1)}, bf16[256,512]{1,0:T(8,128)(2,1)S(1)}, u32[]{:S(2)}) copy-start(bf16[256,512]{1,0:T(8,128)(2,1)S(1)} %fusion.114) | copy-start | bytes 786436
  121.0 2.5 copy-start.14
  123.5 0.8 copy-start.8
  123.5 1.7 copy-start.15
  125.2 1.2 copy-start.23
  128.7 4.9 %copy-start.7 = (bf16[1,256,512]{2,1,0:T(8,128)(2,1)S(1)}, bf16[1,256,512]{2,1,0:T(8,128)(2,1)}, u32[]{:S(2)}) copy-start(bf16[1,256,512]{2,1,0:T(8,128)(2,1)} %param.35) | copy-start | bytes 786436
  128.7 7.6 %copy-start.32 = (bf16[256,64]{0,1:T(8,128)(2,1)S(1)}, bf16[256,64]{0,1:T(8,128)(2,1)}, u32[]{:S(2)}) copy-start(bf16[256,64]{0,1:T(8,128)(2,1)} %param.26) | copy-start | bytes 98308
  128.7 62.4 %all-to-all-start.2 = ((bf16[16,1024,128]{1,2,0:T(8,128)(2,1)}), bf16[16,1024,128]{1,2,0:T(8,128)(2,1)}, u32[]{:S(2)}, u32[]{:S(2)}) async-start(bf16[16,1024,128]{1,2,0:T(8,128)(2,1)} %pad_maximum_fusion.1), calls=%async_computation.2 | async-start | bytes 8388608 | tf_op jit(solution)/shard_map/all_to_all | solution.py:125
  194.2 4.0 %copy-start.16 = (f32[256,512]{1,0:T(8,128)S(1)}, f32[256,512]{1,0:T(8,128)}, u32[]{:S(2)}) copy-start(f32[256,512]{1,0:T(8,128)} %convolution_add_fusion.1) | copy-start | bytes 1572868
  194.2 4.0 %copy-start.25 = (bf16[256,512]{1,0:T(8,128)(2,1)S(1)}, bf16[256,512]{1,0:T(8,128)(2,1)}, u32[]{:S(2)}) copy-start(bf16[256,512]{1,0:T(8,128)(2,1)} %copy-done.24) | copy-start | bytes 786436
  198.2 1.7 copy-start.27
  199.6 1.0 copy-start.19
  199.6 1.0 copy-start.21
  199.9 1.2 copy-start.31
  199.9 1.2 copy-start.34
  200.9 2.2 copy-start.11
  203.0 2.3 copy-start.9
  205.7 1.3 copy-start.3
  206.2 1.6 copy-start.36
  207.1 27.8 %copy-start.37 = (f32[256]{0:T(256)S(1)}, f32[256]{0:T(256)}, u32[]{:S(2)}) copy-start(f32[256]{0:T(256)} %param.27) | copy-start | bytes 3076
  209.1 41.1 %copy-start.17 = (bf16[1,6,64,512]{3,2,1,0:T(8,128)(2,1)S(1)}, bf16[1,6,64,512]{3,2,1,0:T(8,128)(2,1)}, u32[]{:S(2)}) copy-start(bf16[1,6,64,512]{3,2,1,0:T(8,128)(2,1)} %param.21) | copy-start | bytes 1179652
  209.1 41.1 %copy-start.39 = (f32[64]{0:T(128)S(1)}, f32[64]{0:T(128)}, u32[]{:S(2)}) copy-start(f32[64]{0:T(128)} %param.25) | copy-start | bytes 772
  221.4 24.3 %all-to-all-start.4 = ((f32[16,1,3356]{2,1,0:T(1,128)}), f32[16,1,3356]{2,1,0:T(1,128)S(1)}, u32[]{:S(2)}, u32[]{:S(2)}) async-start(f32[16,1,3356]{2,1,0:T(1,128)} %broadcast_in_dim.4), calls=%async_computation.4 | async-start | bytes 442368 | tf_op jit(solution)/shard_map/all_to_all | solution.py:68
  246.6 11.8 %all-to-all-start.5 = ((f32[16,1,3356]{2,1,0:T(1,128)}), f32[16,1,3356]{2,1,0:T(1,128)S(1)}, u32[]{:S(2)}, u32[]{:S(2)}) async-start(f32[16,1,3356]{2,1,0:T(1,128)} %broadcast_in_dim.5), calls=%async_computation.5 | async-start | bytes 442368 | tf_op jit(solution)/shard_map/all_to_all | solution.py:70

commit v5 on v3

--- a/solution.py
+++ b/solution.py
@@ -33,12 +33,6 @@
     return jnp.einsum("mk,kn->mn", gradient, dense, preferred_element_type=jnp.float32)
 
 
-def tile_products(values, spread_tiles):
-    return jnp.einsum(
-        "mn,qan->qma", values, spread_tiles, preferred_element_type=jnp.float32
-    ).astype(jnp.bfloat16)
-
-
 def place_rows(pieces, placer):
     return jnp.einsum("sma,san->mn", pieces, placer, preferred_element_type=jnp.float32)
 
@@ -47,10 +41,6 @@
     return jnp.einsum(
         "mn,san->sma", values, placer, preferred_element_type=jnp.float32
     ).astype(jnp.bfloat16)
-
-
-def tile_backward(pieces, tile_vals):
-    return jnp.einsum("qma,qac->qmc", pieces, tile_vals, preferred_element_type=jnp.float32)
 
 
 def exchange_sum(pieces):
@@ -115,32 +105,43 @@
     eye_slots = jnp.broadcast_to(eye_tile, (own_src.shape[0], tile_width, tile_width))
     dense_fwd = dense_band(local_fwd, blocks, tile_width)
     dense_bwd = dense_band(local_bwd, blocks, tile_width)
-    spread_fwd = spread_onehot(own_src, remote_fwd)
-    spread_bwd = spread_onehot(own_src, remote_bwd)
     src_placer = spread_onehot(own_src, eye_slots)
     recv_dst = lax.all_to_all(own_dst, "node", split_axis=0, concat_axis=0, tiled=True)
     dst_placer = spread_onehot(recv_dst, eye_slots)
-
-    def swap(first, second):
-        got_both = lax.all_to_all(
-            jnp.concatenate([first, second], axis=1),
-            "node",
-            split_axis=0,
-            concat_axis=0,
-            tiled=True,
+    tiles_in = lax.all_to_all(
+        jnp.concatenate([remote_fwd, remote_bwd], axis=1),
+        "node",
+        split_axis=0,
+        concat_axis=0,
+        tiled=True,
+    )
+    tiles_fwd, tiles_bwd = tiles_in[:, :tile_width], tiles_in[:, tile_width:]
+
+    def swap(pieces):
+        got_all = lax.all_to_all(
+            jnp.concatenate(pieces, axis=1), "node", split_axis=0, concat_axis=0, tiled=True
         )
-        return got_both[:, :row_count], got_both[:, row_count:]
-
-    def push_hop(values_fwd, values_bwd):
-        got_fwd, got_bwd = swap(
-            tile_products(values_fwd, spread_fwd), tile_products(values_bwd, spread_bwd)
-        )
-        return place_rows(got_fwd, dst_placer), place_rows(got_bwd, dst_placer)
-
-    far_fwd, far_bwd = push_hop(flat_hidden, flat_hidden)
+        return [got_all[:, k * row_count : (k + 1) * row_count] for k in range(len(pieces))]
+
+    def far_terms(columns, tiles):
+        return jnp.einsum(
+            "smc,sac->sma", columns, tiles, preferred_element_type=jnp.float32
+        ).astype(jnp.bfloat16)
+
+    def row_terms(gradient, tiles):
+        wanted = pick_rows(gradient, dst_placer)
+        return jnp.einsum("sma,sac->smc", wanted, tiles, preferred_element_type=jnp.float32)
+
+    (columns,) = swap([pick_rows(flat_hidden, src_placer)])
+    far_fwd = place_rows(far_terms(columns, tiles_fwd), dst_placer)
+    far_bwd = place_rows(far_terms(columns, tiles_bwd), dst_placer)
     hop_fwd = (near_apply(flat_hidden, dense_fwd) + far_fwd).astype(jnp.bfloat16)
     hop_bwd = (near_apply(flat_hidden, dense_bwd) + far_bwd).astype(jnp.bfloat16)
-    far_fwd, far_bwd = push_hop(hop_fwd, hop_bwd)
+    columns_fwd, columns_bwd = swap(
+        [pick_rows(hop_fwd, src_placer), pick_rows(hop_bwd, src_placer)]
+    )
+    far_fwd = place_rows(far_terms(columns_fwd, tiles_fwd), dst_placer)
+    far_bwd = place_rows(far_terms(columns_bwd, tiles_bwd), dst_placer)
     two_fwd = (near_apply(hop_fwd, dense_fwd) + far_fwd).astype(jnp.bfloat16)
     two_bwd = (near_apply(hop_bwd, dense_bwd) + far_bwd).astype(jnp.bfloat16)
     stacked_parts = jnp.concatenate(
@@ -183,21 +184,22 @@
     back2_fwd = group_of(2).astype(jnp.bfloat16)
     back2_bwd = group_of(4).astype(jnp.bfloat16)
 
-    def fetch_rows(grad_fwd, grad_bwd):
-        return swap(pick_rows(grad_fwd, dst_placer), pick_rows(grad_bwd, dst_placer))
-
-    got_fwd, got_bwd = fetch_rows(back2_fwd, back2_bwd)
-    near1_fwd = place_rows(tile_backward(got_fwd, remote_fwd).astype(jnp.bfloat16), src_placer)
-    near1_bwd = place_rows(tile_backward(got_bwd, remote_bwd).astype(jnp.bfloat16), src_placer)
+    got_fwd, got_bwd = swap(
+        [
+            row_terms(back2_fwd, tiles_fwd).astype(jnp.bfloat16),
+            row_terms(back2_bwd, tiles_bwd).astype(jnp.bfloat16),
+        ]
+    )
+    near1_fwd = place_rows(got_fwd, src_placer)
+    near1_bwd = place_rows(got_bwd, src_placer)
     back1_fwd = (group_of(1) + near_transpose(back2_fwd, dense_fwd) + near1_fwd).astype(
         jnp.bfloat16
     )
     back1_bwd = (group_of(3) + near_transpose(back2_bwd, dense_bwd) + near1_bwd).astype(
         jnp.bfloat16
     )
-    got_fwd, got_bwd = fetch_rows(back1_fwd, back1_bwd)
-    combined = (tile_backward(got_fwd, remote_fwd) + tile_backward(got_bwd, remote_bwd)).astype(
-        jnp.bfloat16
+    (combined,) = swap(
+        [(row_terms(back1_fwd, tiles_fwd) + row_terms(back1_bwd, tiles_bwd)).astype(jnp.bfloat16)]
     )
     far_total = place_rows(combined, src_placer)
     skip_back = jnp.einsum("sc,wsn->wcn", w_skip, cot_skip, preferred_element_type=jnp.float32)

time: 233 us -> 208 us (0.89)
  waiting for transfers between devices: 61.9 us -> 40.4 us
  local copies, waits for them, and re-layouts: 43.4 us -> 22.7 us
  matrix products: 44 us -> 58.8 us
  starting transfers between devices: 47.1 us -> 54.6 us
  other arithmetic: 20 us -> 14.3 us
    all_to_all x4 -> x5, waiting for transfers between devices: 45.8 us -> 25.2 us  [the longest x4 13.5 us: swap(): lax.all_to_all(jnp.concatenate(pieces, axis=1), 'node', split_axis=0, con...]
    mul x9 -> x3, local copies, waits for them, and re-layouts: 19.7 us -> 0.27 us  [spread_onehot(): placed = tile_vals[:, :, None, :] * chooser[:, None, :, None]]
    dot_general x5 -> x4, matrix products: 6.02 us -> 14.6 us  [row_terms(): jnp.einsum('sma,sac->smc', wanted, tiles, preferred_element_type=jnp.floa...]
    all_to_all x4 -> x5, starting transfers between devices: 25.6 us -> 30.8 us  [the longest x4 24.1 us: swap(): lax.all_to_all(jnp.concatenate(pieces, axis=1), 'node', split_axis=0, con...]
    dot_general x4, matrix products: 1.36 us -> 6.55 us  [near_apply(): jnp.einsum('mn,kn->mk', values, dense, preferred_element_type=jnp.float32)]
    mul x1 -> x0, other arithmetic: 3.57 us -> none  [spread_onehot(): placed = tile_vals[:, :, None, :] * chooser[:, None, :, None]]
    dot_general x4 -> x3, matrix products: 4.99 us -> 6.2 us  [pick_rows(): jnp.einsum('mn,san->sma', values, placer, preferred_element_type=jnp.floa...]
    concatenate x4 -> x3, other arithmetic: 6.29 us -> 5.73 us  [the longest x2 4.67 us: swap(): jnp.concatenate(pieces, axis=1)]
  transfers between devices with their start and end apart: 7 -> 8, of which waited for: 6 -> 6; matrix products, arithmetic and copies ran while one was open for 34% -> 38% of each run, Pallas kernels for 0% -> 0%
where the time goes in v5:
time: 208 us; the launch traced here: 206 us
  matrix products  58.8 us (28%)
  starting transfers between devices  54.6 us (26%)
  waiting for transfers between devices  40.4 us (19%)
  local copies, waits for them, and re-layouts  22.7 us (11%)
  other arithmetic  14.3 us (7%)
  blocking collectives  13.7 us (7%)
    all_to_all x4, starting transfers between devices, swap(): lax.all_to_all(jnp.concatenate(pieces, axis=1), 'node', split_axis=0, con...  24.1 us
    dot_general x7, matrix products, place_rows(): jnp.einsum('sma,san->mn', pieces, placer, preferred_element_type=jnp.floa...  18.9 us
    dot_general x4, matrix products, row_terms(): jnp.einsum('sma,sac->smc', wanted, tiles, preferred_element_type=jnp.floa...  14.6 us
    all_to_all x1, blocking collectives, exchange_sum(): lax.all_to_all(flat.reshape(node_count, padded // node_count), 'node', 0,...  13.7 us
    all_to_all x4, waiting for transfers between devices, swap(): lax.all_to_all(jnp.concatenate(pieces, axis=1), 'node', split_axis=0, con...  13.5 us
    all_to_all x1, starting transfers between devices, exchange_sum(): part = lax.all_to_all(part, 'batch', 0, 0, tiled=True).sum(axis=0)  12.7 us
    all_to_all x1, waiting for transfers between devices, shards(): lax.all_to_all(jnp.concatenate([remote_fwd, remote_bwd], axis=1), 'node',...  11.7 us
    unnamed x84, local copies, waits for them, and re-layouts  10.4 us
  transfers between devices with their start and end apart: 8, of which 6 were waited for; matrix products, arithmetic and copies ran while one was open for 38% of the time, Pallas kernels for 0%

profile of v5, /device:TPU:1, one launch (start us, length us, event | category | flops | bytes accessed | tf_op | source)
XLA Modules:
  0.0 206.1 jit_solution(15607405805100040385)
XLA Ops:
  0.7 1.4 compare_convert_fusion
  2.0 7.6 %all-to-all-start.2 = ((bf16[16,1,4]{2,1,0:T(2,128)(2,1)}), bf16[16,1,4]{2,1,0:T(2,128)(2,1)S(1)}, u32[]{:S(2)}, u32[]{:S(2)}) async-start(bf16[16,1,4]{2,1,0:T(2,128)(2,1)} %compare_convert_fusion), calls=%async_computation.2 | async-start | bytes 16384 | tf_op jit(solution)/shard_map/all_to_all | solution.py:109
  10.4 1.5 convolution_bitcast_fusion.1
  11.9 1.5 copy-done.1
  13.4 0.9 fusion.229
  16.0 1.1 pad_maximum_fusion.2
  17.5 6.7 %all-to-all-start.1 = ((bf16[16,256,128]{2,1,0:T(8,128)(2,1)}), bf16[16,256,128]{2,1,0:T(8,128)(2,1)}, u32[]{:S(2)}, u32[]{:S(2)}) async-start(bf16[16,256,128]{2,1,0:T(8,128)(2,1)} %pad_maximum_fusion.2), calls=%async_computation.1 | async-start | bytes 2097152 | tf_op jit(solution)/shard_map/all_to_all | solution.py:111
  25.6 0.7 copy-done.2
  26.3 1.8 fusion.55
  28.0 11.7 %all-to-all-done.1 = bf16[16,256,128]{2,1,0:T(8,128)(2,1)} async-done(((bf16[16,256,128]{2,1,0:T(8,128)(2,1)}), bf16[16,256,128]{2,1,0:T(8,128)(2,1)}, u32[]{:S(2)}, u32[]{:S(2)}) %all-to-all-start.1) | async-done | bytes 1048608 | tf_op jit(solution)/shard_map/all_to_all | solution.py:111
  39.7 4.4 %all-to-all-start = ((bf16[16,256,128]{1,2,0:T(8,128)(2,1)}), bf16[16,256,128]{1,2,0:T(8,128)(2,1)}, u32[]{:S(2)}, u32[]{:S(2)}) async-start(bf16[16,256,128]{1,2,0:T(8,128)(2,1)} %fusion.55), calls=%async_computation | async-start | bytes 2097152 | tf_op jit(solution)/shard_map/all_to_all | solution.py:121
  44.2 2.6 %fusion.228 = (f32[1,4,64,512]{3,2,1,0:T(8,128)}, f32[1,4,64,512]{3,2,1,0:T(8,128)}, f32[1,4,64,512]{3,2,1,0:T(8,128)}) fusion(f32[1,4,320,512]{3,2,1,0:T(8,128)} %copy-done.1), kind=kLoop, calls=%fused_computation.217 | loop fusion | bytes 3145728 | tf_op jit(solution)/shard_map/slice | solution.py:207
  47.0 3.4 %convolution_convert_fusion = bf16[16,256,128]{2,1,0:T(8,128)(2,1)} fusion(bf16[256,512,1]{1,0,2:T(8,128)(2,1)} %bitcast.238, bf16[16,512]{1,0:T(8,128)(2,1)S(1)} %bitcast.265, bf16[128,512]{1,0:T(8,128)(2,1)} %bitcast.243, bf16[16,256,128]{2,1,0:T(8,128)(2,1)} %all-to-all-done.1), kind=kOutput, calls=%fused_computation.42 | convolution fusion | flops 673185792 | bytes 1982464 | tf_op jit(solution)/shard_map/sma,sac->smc/dot_general | solution.py:133
  50.4 3.4 %convolution_convert_fusion.1 = bf16[16,256,128]{2,1,0:T(8,128)(2,1)} fusion(bf16[256,512,1]{1,0,2:T(8,128)(2,1)} %bitcast.240, bf16[16,512]{1,0:T(8,128)(2,1)S(1)} %bitcast.266, bf16[128,512]{1,0:T(8,128)(2,1)} %bitcast.244, bf16[16,256,128]{2,1,0:T(8,128)(2,1)} %all-to-all-done.1), kind=kOutput, calls=%fused_computation.43 | convolution fusion | flops 673185792 | bytes 1982464 | tf_op jit(solution)/shard_map/sma,sac->smc/dot_general | solution.py:133
  53.8 3.1 %pad_maximum_fusion.1 = bf16[16,512,128]{2,1,0:T(8,128)(2,1)} fusion(bf16[16,256,128]{2,1,0:T(8,128)(2,1)} %convolution_convert_fusion, bf16[16,256,128]{2,1,0:T(8,128)(2,1)} %convolution_convert_fusion.1), kind=kLoop, calls=%fused_computation.30 | loop fusion | flops 4194304 | bytes 4194304 | tf_op jit(solution)/shard_map/concatenate | solution.py:122
  56.9 2.0 all-to-all-done
  58.8 4.8 %all-to-all-start.4 = ((bf16[16,512,128]{2,1,0:T(8,128)(2,1)}), bf16[16,512,128]{2,1,0:T(8,128)(2,1)}, u32[]{:S(2)}, u32[]{:S(2)}) async-start(bf16[16,512,128]{2,1,0:T(8,128)(2,1)} %pad_maximum_fusion.1), calls=%async_computation.4 | async-start | bytes 4194304 | tf_op jit(solution)/shard_map/all_to_all | solution.py:121
  63.7 1.8 fusion.123
  65.5 3.2 %fusion.79 = f32[256,512]{1,0:T(8,128)} fusion(bf16[16,256,128]{1,2,0:T(8,128)(2,1)} %all-to-all-done, bf16[16,512]{1,0:T(8,128)(2,1)S(1)} %bitcast.267, bf16[128,512]{1,0:T(8,128)(2,1)} %bitcast.245, bf16[16,256,128]{2,1,0:T(8,128)(2,1)} %all-to-all-done.1), kind=kOutput, calls=%fused_computation.63 | convolution fusion | flops 672661504 | bytes 2244608 | tf_op jit(solution)/shard_map/sma,san->mn/dot_general | solution.py:37
  68.7 1.5 fusion.119
  70.2 0.7 copy-done.5
  70.9 2.7 %fusion.49 = bf16[16,256,128]{1,2,0:T(8,128)(2,1)} fusion(bf16[16,512]{1,0:T(8,128)(2,1)S(1)} %bitcast.260, bf16[128,512]{1,0:T(8,128)(2,1)} %bitcast.246, bf16[256,512]{1,0:T(8,128)(2,1)S(1)} %fusion.119), kind=kOutput, calls=%fused_computation.48 | convolution fusion | flops 538443776 | bytes 1458176 | tf_op jit(solution)/shard_map/mn,san->sma/dot_general | solution.py:41
  73.6 3.2 %fusion.76 = f32[256,512]{1,0:T(8,128)} fusion(bf16[16,256,128]{1,2,0:T(8,128)(2,1)} %all-to-all-done, bf16[16,512]{1,0:T(8,128)(2,1)S(1)} %bitcast.268, bf16[128,512]{1,0:T(8,128)(2,1)} %bitcast.247, bf16[16,256,128]{2,1,0:T(8,128)(2,1)} %all-to-all-done.1), kind=kOutput, calls=%fused_computation.62 | convolution fusion | flops 672661504 | bytes 2244608 | tf_op jit(solution)/shard_map/sma,san->mn/dot_general | solution.py:37
  76.8 1.5 fusion.117
  79.0 1.7 fusion.52
  80.7 1.6 pad_maximum_fusion
  82.3 6.4 %all-to-all-done.4 = bf16[16,512,128]{2,1,0:T(8,128)(2,1)} async-done(((bf16[16,512,128]{2,1,0:T(8,128)(2,1)}), bf16[16,512,128]{2,1,0:T(8,128)(2,1)}, u32[]{:S(2)}, u32[]{:S(2)}) %all-to-all-start.4) | async-done | bytes 2097184 | tf_op jit(solution)/shard_map/all_to_all | solution.py:121
  88.6 7.3 %all-to-all-start.3 = ((bf16[16,512,128]{1,2,0:T(8,128)(2,1)}), bf16[16,512,128]{1,2,0:T(8,128)(2,1)}, u32[]{:S(2)}, u32[]{:S(2)}) async-start(bf16[16,512,128]{1,2,0:T(8,128)(2,1)} %pad_maximum_fusion), calls=%async_computation.3 | async-start | bytes 4194304 | tf_op jit(solution)/shard_map/all_to_all | solution.py:121
  95.9 1.2 convolution_bitcast_fusion.6
  97.1 0.8 copy.109
  97.9 1.6 reshape.401
  99.5 1.6 convert_reduce_fusion.2
  101.1 1.0 constant_dynamic-update-slice_fusion.3
  102.1 2.0 fusion.88
  104.1 2.0 fusion.91
  106.2 1.0 fusion.110
  107.3 1.0 fusion.111
  108.3 3.7 %fusion.59 = f32[16,256,128]{2,1,0:T(8,128)} fusion(bf16[16,512]{1,0:T(8,128)(2,1)S(1)} %bitcast.269, bf16[128,512]{1,0:T(8,128)(2,1)} %bitcast.250, bf16[16,256,128]{2,1,0:T(8,128)(2,1)} %all-to-all-done.1, bf16[256,512]{1,0:T(8,128)(2,1)} %fusion.110), kind=kOutput, calls=%fused_computation.53 | convolution fusion | flops 672661504 | bytes 3031040 | tf_op jit(solution)/shard_map/sma,sac->smc/dot_general | solution.py:133
  112.0 4.1 %add_convert_fusion = bf16[16,256,128]{2,1,0:T(8,128)(2,1)} fusion(f32[16,256,128]{2,1,0:T(8,128)} %fusion.59, bf16[16,512]{1,0:T(8,128)(2,1)S(1)} %bitcast.270, bf16[128,512]{1,0:T(8,128)(2,1)} %bitcast.251, bf16[16,256,128]{2,1,0:T(8,128)(2,1)} %all-to-all-done.1, bf16[256,512]{1,0:T(8,128)(2,1)} %fusion.111), kind=kOutput, calls=%fused_computation.31 | convolution fusion | flops 673710080 | bytes 4079616 | tf_op jit(solution)/shard_map/sma,sac->smc/dot_general | solution.py:133
  116.1 5.2 %all-to-all-done.3 = bf16[16,512,128]{1,2,0:T(8,128)(2,1)} async-done(((bf16[16,512,128]{1,2,0:T(8,128)(2,1)}), bf16[16,512,128]{1,2,0:T(8,128)(2,1)}, u32[]{:S(2)}, u32[]{:S(2)}) %all-to-all-start.3) | async-done | bytes 2097184 | tf_op jit(solution)/shard_map/all_to_all | solution.py:121
  121.3 7.5 %all-to-all-start.5 = ((bf16[16,256,128]{2,1,0:T(8,128)(2,1)}), bf16[16,256,128]{2,1,0:T(8,128)(2,1)}, u32[]{:S(2)}, u32[]{:S(2)}) async-start(bf16[16,256,128]{2,1,0:T(8,128)(2,1)} %add_convert_fusion), calls=%async_computation.5 | async-start | bytes 2097152 | tf_op jit(solution)/shard_map/all_to_all | solution.py:121
  128.9 3.2 %fusion.82 = f32[256,512]{1,0:T(8,128)} fusion(bf16[16,512,128]{1,2,0:T(8,128)(2,1)} %all-to-all-done.3, bf16[16,512]{1,0:T(8,128)(2,1)S(1)} %bitcast.271, bf16[128,512]{1,0:T(8,128)(2,1)} %bitcast.252, bf16[16,256,128]{2,1,0:T(8,128)(2,1)} %all-to-all-done.1), kind=kOutput, calls=%fused_computation.64 | convolution fusion | flops 672661504 | bytes 2244608 | tf_op jit(solution)/shard_map/sma,san->mn/dot_general | solution.py:37
  132.1 2.2 %fusion.118 = bf16[256,512]{1,0:T(8,128)(2,1)} fusion(f32[256,512]{1,0:T(8,128)} %fusion.82, bf16[256,512]{1,0:T(8,128)(2,1)} %copy-done.6, bf16[64,8,4,128]{3,2,1,0:T(4,128)(2,1)S(1)} %bitcast.221), kind=kOutput, calls=%fused_computation.90 | convolution fusion | flops 134479872 | bytes 1572864 | tf_op jit(solution)/shard_map/mn,kn->mk/dot_general | solution.py:29
  134.3 3.2 %fusion.85 = f32[256,512]{1,0:T(8,128)} fusion(bf16[16,512,128]{1,2,0:T(8,128)(2,1)} %all-to-all-done.3, bf16[16,512]{1,0:T(8,128)(2,1)S(1)} %bitcast.272, bf16[128,512]{1,0:T(8,128)(2,1)} %bitcast.253, bf16[16,256,128]{2,1,0:T(8,128)(2,1)} %all-to-all-done.1), kind=kOutput, calls=%fused_computation.65 | convolution fusion | flops 672661504 | bytes 2244608 | tf_op jit(solution)/shard_map/sma,san->mn/dot_general | solution.py:37
  137.5 1.0 constant_dynamic-update-slice_fusion.2
  138.5 1.0 constant_dynamic-update-slice_fusion.1
  139.5 1.5 fusion.120
  141.5 0.7 reshape.400
  142.2 2.2 %convolution_add_fusion.2 = f32[256,512]{1,0:T(8,128)} fusion(f32[256,512]{1,0:T(8,128)} %bitcast.232, bf16[256,512]{1,0:T(8,128)(2,1)} %fusion.110, bf16[64,8,4,128]{3,2,1,0:T(4,128)(2,1)S(1)} %bitcast.222), kind=kOutput, calls=%fused_computation.73 | convolution fusion | flops 134348800 | bytes 1835008 | tf_op jit(solution)/shard_map/mk,kn->mn/dot_general | solution.py:33
  144.5 2.0 fusion.94
  149.2 1.0 concatenate.55
  150.5 13.7 %all_to_all.52 = f32[16,1,3356]{2,1,0:T(1,128)S(1)} all-to-all(f32[16,1,3356]{2,1,0:T(1,128)S(1)} %all_to_all.39), channel_id=1, replica_groups=mesh['node'=16,'batch'=16] {'node'}, dimensions={0} | all-to-all | bytes 429568 | tf_op jit(solution)/shard_map/all_to_all | solution.py:54
  164.4 0.8 broadcast_in_dim.4
  165.2 12.7 %all-to-all-start.7 = ((f32[16,1,3356]{2,1,0:T(1,128)}), f32[16,1,3356]{2,1,0:T(1,128)S(1)}, u32[]{:S(2)}, u32[]{:S(2)}) async-start(f32[16,1,3356]{2,1,0:T(1,128)} %broadcast_in_dim.4), calls=%async_computation.7 | async-start | bytes 442368 | tf_op jit(solution)/shard_map/all_to_all | solution.py:58
  177.9 1.1 fusion.121
  179.0 0.8 copy.112
  179.8 8.8 %all-to-all-done.7 = f32[16,1,3356]{2,1,0:T(1,128)S(1)} async-done(((f32[16,1,3356]{2,1,0:T(1,128)}), f32[16,1,3356]{2,1,0:T(1,128)S(1)}, u32[]{:S(2)}, u32[]{:S(2)}) %all-to-all-start.7) | async-done | bytes 214816 | tf_op jit(solution)/shard_map/all_to_all | solution.py:58
  188.8 0.8 broadcast_in_dim.5
  189.6 3.5 %all-to-all-start.8 = ((f32[16,1,3356]{2,1,0:T(1,128)}), f32[16,1,3356]{2,1,0:T(1,128)S(1)}, u32[]{:S(2)}, u32[]{:S(2)}) async-start(f32[16,1,3356]{2,1,0:T(1,128)} %broadcast_in_dim.5), calls=%async_computation.8 | async-start | bytes 442368 | tf_op jit(solution)/shard_map/all_to_all | solution.py:60
  193.1 1.1 fusion.113
  194.2 0.8 convert_element_type.229
  195.0 6.4 %all-to-all-done.8 = f32[16,1,3356]{2,1,0:T(1,128)S(1)} async-done(((f32[16,1,3356]{2,1,0:T(1,128)}), f32[16,1,3356]{2,1,0:T(1,128)S(1)}, u32[]{:S(2)}, u32[]{:S(2)}) %all-to-all-start.8) | async-done | bytes 214816 | tf_op jit(solution)/shard_map/all_to_all | solution.py:60
  204.7 0.7 copy.113
  205.4 0.7 mul.151
  (118 shorter events, 12.0 us)
Async XLA Ops:
  0.6 9.7 %copy-start = (bf16[64,320]{1,0:T(8,128)(2,1)S(1)}, bf16[64,320]{1,0:T(8,128)(2,1)}, u32[]{:S(2)}) copy-start(bf16[64,320]{1,0:T(8,128)(2,1)} %param.24) | copy-start | bytes 122884
  2.0 15.4 %all-to-all-start.2 = ((bf16[16,1,4]{2,1,0:T(2,128)(2,1)}), bf16[16,1,4]{2,1,0:T(2,128)(2,1)S(1)}, u32[]{:S(2)}, u32[]{:S(2)}) async-start(bf16[16,1,4]{2,1,0:T(2,128)(2,1)} %compare_convert_fusion), calls=%async_computation.2 | async-start | bytes 16384 | tf_op jit(solution)/shard_map/all_to_all | solution.py:109
  9.7 4.6 %copy-start.36 = (s32[16]{0:T(128)S(1)}, s32[16]{0:T(128)}, u32[]{:S(2)}) copy-start(s32[16]{0:T(128)} %param.32) | copy-start | bytes 196
  9.7 4.7 %copy-start.22 = (bf16[512,384]{1,0:T(8,128)(2,1)S(1)}, bf16[512,384]{1,0:T(8,128)(2,1)}, u32[]{:S(2)}) copy-start(bf16[512,384]{1,0:T(8,128)(2,1)} %param.28) | copy-start | bytes 1179652
  11.9 1.5 copy-start.1
  13.4 1.3 copy-start.23
  14.4 89.7 %copy-start.32 = (bf16[2,8,4,128]{3,1,2,0:T(8,128)(2,1)}, bf16[2,8,4,128]{3,1,2,0:T(8,128)(2,1)S(1)}, u32[]{:S(2)}) copy-start(bf16[2,8,4,128]{3,1,2,0:T(8,128)(2,1)S(1)} %copy.172) | copy-start | bytes 49156
  14.8 1.2 copy-start.20
  14.8 1.2 copy-start.21
  17.0 7.2 %copy-start.10 = (bf16[1,6,64,512]{3,2,1,0:T(8,128)(2,1)S(1)}, bf16[1,6,64,512]{3,2,1,0:T(8,128)(2,1)}, u32[]{:S(2)}) copy-start(bf16[1,6,64,512]{3,2,1,0:T(8,128)(2,1)} %param.21) | copy-start | bytes 1179652
  17.0 8.0 %copy-start.26 = (bf16[128,128]{1,0:T(8,128)(2,1)S(1)}, bf16[128,128]{1,0:T(8,128)(2,1)}, u32[]{:S(2)}) copy-start(bf16[128,128]{1,0:T(8,128)(2,1)} %param.22) | copy-start | bytes 98308
  17.0 8.0 %copy-start.35 = (f32[128]{0:T(128)S(1)}, f32[128]{0:T(128)}, u32[]{:S(2)}) copy-start(f32[128]{0:T(128)} %param.23) | copy-start | bytes 1540
  17.5 22.3 %all-to-all-start.1 = ((bf16[16,256,128]{2,1,0:T(8,128)(2,1)}), bf16[16,256,128]{2,1,0:T(8,128)(2,1)}, u32[]{:S(2)}, u32[]{:S(2)}) async-start(bf16[16,256,128]{2,1,0:T(8,128)(2,1)} %pad_maximum_fusion.2), calls=%async_computation.1 | async-start | bytes 2097152 | tf_op jit(solution)/shard_map/all_to_all | solution.py:111
  24.2 2.1 %copy-start.28 = (bf16[16,8,4,128]{3,1,2,0:T(8,128)(2,1)S(1)}, bf16[16,8,4,128]{3,1,2,0:T(8,128)(2,1)}, u32[]{:S(2)}) copy-start(bf16[16,8,4,128]{3,1,2,0:T(8,128)(2,1)} %copy.170) | copy-start | bytes 393220
  24.2 0.7 copy-start.13
  24.3 0.8 copy-start.15
  25.6 0.7 copy-start.2
  39.7 19.1 %all-to-all-start = ((bf16[16,256,128]{1,2,0:T(8,128)(2,1)}), bf16[16,256,128]{1,2,0:T(8,128)(2,1)}, u32[]{:S(2)}, u32[]{:S(2)}) async-start(bf16[16,256,128]{1,2,0:T(8,128)(2,1)} %fusion.55), calls=%async_computation | async-start | bytes 2097152 | tf_op jit(solution)/shard_map/all_to_all | solution.py:121
  56.9 6.8 %copy-start.30 = (bf16[256,64]{0,1:T(8,128)(2,1)S(1)}, bf16[256,64]{0,1:T(8,128)(2,1)}, u32[]{:S(2)}) copy-start(bf16[256,64]{0,1:T(8,128)(2,1)} %param.26) | copy-start | bytes 98308
  58.8 29.8 %all-to-all-start.4 = ((bf16[16,512,128]{2,1,0:T(8,128)(2,1)}), bf16[16,512,128]{2,1,0:T(8,128)(2,1)}, u32[]{:S(2)}, u32[]{:S(2)}) async-start(bf16[16,512,128]{2,1,0:T(8,128)(2,1)} %pad_maximum_fusion.1), calls=%async_computation.4 | async-start | bytes 4194304 | tf_op jit(solution)/shard_map/all_to_all | solution.py:121
  70.2 0.7 copy-start.5
  78.3 0.7 copy-start.6
  79.0 1.7 copy-start.12
  88.6 32.7 %all-to-all-start.3 = ((bf16[16,512,128]{1,2,0:T(8,128)(2,1)}), bf16[16,512,128]{1,2,0:T(8,128)(2,1)}, u32[]{:S(2)}, u32[]{:S(2)}) async-start(bf16[16,512,128]{1,2,0:T(8,128)(2,1)} %pad_maximum_fusion), calls=%async_computation.3 | async-start | bytes 4194304 | tf_op jit(solution)/shard_map/all_to_all | solution.py:121
  102.1 2.0 copy-start.29
  104.1 2.1 copy-start.9
  104.1 2.1 copy-start.18
  106.2 1.1 copy-start.8
  106.2 1.1 copy-start.17
  121.3 23.1 %all-to-all-start.5 = ((bf16[16,256,128]{2,1,0:T(8,128)(2,1)}), bf16[16,256,128]{2,1,0:T(8,128)(2,1)}, u32[]{:S(2)}, u32[]{:S(2)}) async-start(bf16[16,256,128]{2,1,0:T(8,128)(2,1)} %add_convert_fusion), calls=%async_computation.5 | async-start | bytes 2097152 | tf_op jit(solution)/shard_map/all_to_all | solution.py:121
  137.5 3.5 %copy-start.3 = (bf16[1,4,64,512]{3,2,1,0:T(8,128)(2,1)S(1)}, bf16[1,4,64,512]{3,2,1,0:T(8,128)(2,1)}, u32[]{:S(2)}) copy-start(bf16[1,4,64,512]{3,2,1,0:T(8,128)(2,1)} %param.34) | copy-start | bytes 786436
  144.4 2.0 copy-start.7
  144.5 2.1 copy-start.19
  146.5 1.0 copy-start.14
  146.5 1.0 copy-start.16
  146.8 1.0 copy-start.27
  147.9 1.0 copy-start.4
  148.2 0.9 copy-start.24
  148.2 0.9 copy-start.25
  148.2 0.9 copy-start.33
  148.8 29.1 %copy-start.31 = (bf16[256,64]{0,1:T(8,128)(2,1)S(1)}, bf16[256,64]{0,1:T(8,128)(2,1)}, u32[]{:S(2)}) copy-start(bf16[256,64]{0,1:T(8,128)(2,1)} %param.26) | copy-start | bytes 98308
  148.8 29.1 %copy-start.34 = (f32[256]{0:T(256)S(1)}, f32[256]{0:T(256)}, u32[]{:S(2)}) copy-start(f32[256]{0:T(256)} %param.27) | copy-start | bytes 3076
  149.1 44.0 %copy-start.11 = (bf16[1,6,64,512]{3,2,1,0:T(8,128)(2,1)S(1)}, bf16[1,6,64,512]{3,2,1,0:T(8,128)(2,1)}, u32[]{:S(2)}) copy-start(bf16[1,6,64,512]{3,2,1,0:T(8,128)(2,1)} %param.21) | copy-start | bytes 1179652
  149.1 44.0 %copy-start.37 = (f32[64]{0:T(128)S(1)}, f32[64]{0:T(128)}, u32[]{:S(2)}) copy-start(f32[64]{0:T(128)} %param.25) | copy-start | bytes 772
  165.2 23.5 %all-to-all-start.7 = ((f32[16,1,3356]{2,1,0:T(1,128)}), f32[16,1,3356]{2,1,0:T(1,128)S(1)}, u32[]{:S(2)}, u32[]{:S(2)}) async-start(f32[16,1,3356]{2,1,0:T(1,128)} %broadcast_in_dim.4), calls=%async_computation.7 | async-start | bytes 442368 | tf_op jit(solution)/shard_map/all_to_all | solution.py:58
  189.6 11.8 %all-to-all-start.8 = ((f32[16,1,3356]{2,1,0:T(1,128)}), f32[16,1,3356]{2,1,0:T(1,128)S(1)}, u32[]{:S(2)}, u32[]{:S(2)}) async-start(f32[16,1,3356]{2,1,0:T(1,128)} %broadcast_in_dim.5), calls=%async_computation.8 | async-start | bytes 442368 | tf_op jit(solution)/shard_map/all_to_all | solution.py:60

commit v6 on v5

--- a/solution.py
+++ b/solution.py
@@ -116,6 +116,7 @@
         tiled=True,
     )
     tiles_fwd, tiles_bwd = tiles_in[:, :tile_width], tiles_in[:, tile_width:]
+    slot_count = own_src.shape[0]
 
     def swap(pieces):
         got_all = lax.all_to_all(
@@ -128,18 +129,52 @@
             "smc,sac->sma", columns, tiles, preferred_element_type=jnp.float32
         ).astype(jnp.bfloat16)
 
-    def row_terms(gradient, tiles):
-        wanted = pick_rows(gradient, dst_placer)
-        return jnp.einsum("sma,sac->smc", wanted, tiles, preferred_element_type=jnp.float32)
+    row_tiles = jnp.stack(
+        [
+            (tiles_fwd[:, None] * recv_dst[:, :, None, None]).reshape(
+                slot_count, local_nodes, tile_width
+            ),
+            (tiles_bwd[:, None] * recv_dst[:, :, None, None]).reshape(
+                slot_count, local_nodes, tile_width
+            ),
+        ]
+    )
+
+    def row_terms(gradient_fwd, gradient_bwd):
+        return jnp.einsum(
+            "dmn,dsnc->sdmc",
+            jnp.stack([gradient_fwd, gradient_bwd]),
+            row_tiles,
+            preferred_element_type=jnp.float32,
+        ).astype(jnp.bfloat16)
+
+    def row_terms_summed(gradient_fwd, gradient_bwd):
+        return jnp.einsum(
+            "dmn,dsnc->smc",
+            jnp.stack([gradient_fwd, gradient_bwd]),
+            row_tiles,
+            preferred_element_type=jnp.float32,
+        ).astype(jnp.bfloat16)
+
+    def exchange(send):
+        return lax.all_to_all(send, "node", split_axis=0, concat_axis=0, tiled=True)
 
     (columns,) = swap([pick_rows(flat_hidden, src_placer)])
     far_fwd = place_rows(far_terms(columns, tiles_fwd), dst_placer)
     far_bwd = place_rows(far_terms(columns, tiles_bwd), dst_placer)
     hop_fwd = (near_apply(flat_hidden, dense_fwd) + far_fwd).astype(jnp.bfloat16)
     hop_bwd = (near_apply(flat_hidden, dense_bwd) + far_bwd).astype(jnp.bfloat16)
-    columns_fwd, columns_bwd = swap(
-        [pick_rows(hop_fwd, src_placer), pick_rows(hop_bwd, src_placer)]
-    )
+    columns_both = exchange(
+        jnp.einsum(
+            "dmn,scn->sdmc",
+            jnp.stack([hop_fwd, hop_bwd]),
+            src_placer,
+            preferred_element_type=jnp.float32,
+        )
+        .astype(jnp.bfloat16)
+        .reshape(slot_count, 2 * row_count, tile_width)
+    )
+    columns_fwd, columns_bwd = columns_both[:, :row_count], columns_both[:, row_count:]
     far_fwd = place_rows(far_terms(columns_fwd, tiles_fwd), dst_placer)
     far_bwd = place_rows(far_terms(columns_bwd, tiles_bwd), dst_placer)
     two_fwd = (near_apply(hop_fwd, dense_fwd) + far_fwd).astype(jnp.bfloat16)
@@ -184,12 +219,10 @@
     back2_fwd = group_of(2).astype(jnp.bfloat16)
     back2_bwd = group_of(4).astype(jnp.bfloat16)
 
-    got_fwd, got_bwd = swap(
-        [
-            row_terms(back2_fwd, tiles_fwd).astype(jnp.bfloat16),
-            row_terms(back2_bwd, tiles_bwd).astype(jnp.bfloat16),
-        ]
-    )
+    got_both = exchange(
+        row_terms(back2_fwd, back2_bwd).reshape(slot_count, 2 * row_count, tile_width)
+    )
+    got_fwd, got_bwd = got_both[:, :row_count], got_both[:, row_count:]
     near1_fwd = place_rows(got_fwd, src_placer)
     near1_bwd = place_rows(got_bwd, src_placer)
     back1_fwd = (group_of(1) + near_transpose(back2_fwd, dense_fwd) + near1_fwd).astype(
@@ -198,9 +231,7 @@
     back1_bwd = (group_of(3) + near_transpose(back2_bwd, dense_bwd) + near1_bwd).astype(
         jnp.bfloat16
     )
-    (combined,) = swap(
-        [(row_terms(back1_fwd, tiles_fwd) + row_terms(back1_bwd, tiles_bwd)).astype(jnp.bfloat16)]
-    )
+    combined = exchange(row_terms_summed(back1_fwd, back1_bwd))
     far_total = place_rows(combined, src_placer)
     skip_back = jnp.einsum("sc,wsn->wcn", w_skip, cot_skip, preferred_element_type=jnp.float32)
     direct = (

time: 208 us -> 236 us (1.13)
  local copies, waits for them, and re-layouts: 22.7 us -> 60.2 us
  matrix products: 58.8 us -> 47 us
  waiting for transfers between devices: 40.4 us -> 47 us
  blocking collectives: 13.7 us -> 10.8 us
  starting transfers between devices: 54.6 us -> 51.9 us
    all_to_all x4 -> x1, starting transfers between devices: 24.1 us -> 4.43 us  [swap(): lax.all_to_all(jnp.concatenate(pieces, axis=1), 'node', split_axis=0, con...]
    all_to_all x0 -> x3, starting transfers between devices: none -> 17.7 us  [exchange(): return lax.all_to_all(send, 'node', split_axis=0, concat_axis=0, tiled=True)]
    mul x0 -> x4, local copies, waits for them, and re-layouts: none -> 14.7 us  [the longest x2 7.34 us: shards(): tiles_bwd[:, None] * recv_dst[:, :, None, None]]
    all_to_all x0 -> x3, waiting for transfers between devices: none -> 13.1 us  [exchange(): return lax.all_to_all(send, 'node', split_axis=0, concat_axis=0, tiled=True)]
    all_to_all x4 -> x1, waiting for transfers between devices: 13.5 us -> 4.7 us  [swap(): lax.all_to_all(jnp.concatenate(pieces, axis=1), 'node', split_axis=0, con...]
    convert_element_type x0 -> x2, local copies, waits for them, and re-layouts: none -> 7.86 us  [the longest x1 3.96 us: row_terms(): return jnp.einsum('dmn,dsnc->sdmc', jnp.stack([gradient_fwd, gradient_bwd...]
    mul x4, local copies, waits for them, and re-layouts: 0.37 us -> 7.1 us  [dense_band(): shaped * hits]
    dot_general x4 -> x3, matrix products: 14.6 us -> 8.53 us  [the longest x1 3.65 us: shards(): jnp.einsum('dmn,scn->sdmc', jnp.stack([hop_fwd, hop_bwd]), src_placer, pr...]
  transfers between devices with their start and end apart: 8 -> 8, of which waited for: 6 -> 7; matrix products, arithmetic and copies ran while one was open for 38% -> 32% of each run, Pallas kernels for 0% -> 0%
where the time goes in v6:
time: 236 us; the launch traced here: 234 us
  local copies, waits for them, and re-layouts  60.2 us (26%)
  starting transfers between devices  51.9 us (22%)
  waiting for transfers between devices  47 us (20%)
  matrix products  47 us (20%)
  other arithmetic  15.3 us (6%)
  blocking collectives  10.8 us (5%)
    dot_general x7, matrix products, place_rows(): jnp.einsum('sma,san->mn', pieces, placer, preferred_element_type=jnp.floa...  18.9 us
    all_to_all x3, starting transfers between devices, exchange(): return lax.all_to_all(send, 'node', split_axis=0, concat_axis=0, tiled=True)  17.7 us
    all_to_all x1, starting transfers between devices, exchange_sum(): part = lax.all_to_all(part, 'batch', 0, 0, tiled=True).sum(axis=0)  14.4 us
    unnamed x102, local copies, waits for them, and re-layouts  13.5 us
    all_to_all x3, waiting for transfers between devices, exchange(): return lax.all_to_all(send, 'node', split_axis=0, concat_axis=0, tiled=True)  13.1 us
    all_to_all x1, waiting for transfers between devices, shards(): lax.all_to_all(jnp.concatenate([remote_fwd, remote_bwd], axis=1), 'node',...  11.7 us
    all_to_all x1, blocking collectives, exchange_sum(): lax.all_to_all(flat.reshape(node_count, padded // node_count), 'node', 0,...  10.8 us
    all_to_all x1, waiting for transfers between devices, exchange_sum(): part = lax.all_to_all(part, 'batch', 0, 0, tiled=True).sum(axis=0)  8.8 us
  transfers between devices with their start and end apart: 8, of which 7 were waited for; matrix products, arithmetic and copies ran while one was open for 32% of the time, Pallas kernels for 0%

profile of v6, /device:TPU:1, one launch (start us, length us, event | category | flops | bytes accessed | tf_op | source)
XLA Modules:
  0.0 233.8 jit_solution(924740616638398925)
XLA Ops:
  0.7 1.4 compare_convert_fusion
  2.0 7.6 %all-to-all-start.2 = ((bf16[16,1,4]{2,1,0:T(2,128)(2,1)}), bf16[16,1,4]{2,1,0:T(2,128)(2,1)S(1)}, u32[]{:S(2)}, u32[]{:S(2)}) async-start(bf16[16,1,4]{2,1,0:T(2,128)(2,1)} %compare_convert_fusion), calls=%async_computation.2 | async-start | bytes 16384 | tf_op jit(solution)/shard_map/all_to_all | solution.py:109
  10.5 2.4 %pad_maximum_fusion.9 = bf16[16,256,128]{2,1,0:T(8,128)(2,1)} fusion(bf16[16,128,128]{2,1,0:T(8,128)(2,1)} %param.31, bf16[16,128,128]{2,1,0:T(8,128)(2,1)} %param.30), kind=kLoop, calls=%fused_computation.86 | loop fusion | flops 2097152 | bytes 2097152 | tf_op jit(solution)/shard_map/concatenate | solution.py:112
  13.5 2.4 %all-to-all-done.2 = bf16[16,1,4]{2,1,0:T(2,128)(2,1)S(1)} async-done(((bf16[16,1,4]{2,1,0:T(2,128)(2,1)}), bf16[16,1,4]{2,1,0:T(2,128)(2,1)S(1)}, u32[]{:S(2)}, u32[]{:S(2)}) %all-to-all-start.2) | async-done | bytes 160 | tf_op jit(solution)/shard_map/all_to_all | solution.py:109
  15.9 4.2 %all-to-all-start.1 = ((bf16[16,256,128]{2,1,0:T(8,128)(2,1)}), bf16[16,256,128]{2,1,0:T(8,128)(2,1)S(1)}, u32[]{:S(2)}, u32[]{:S(2)}) async-start(bf16[16,256,128]{2,1,0:T(8,128)(2,1)} %pad_maximum_fusion.9), calls=%async_computation.1 | async-start | bytes 2097152 | tf_op jit(solution)/shard_map/all_to_all | solution.py:111
  22.3 1.8 fusion.22
  24.0 11.7 %all-to-all-done.1 = bf16[16,256,128]{2,1,0:T(8,128)(2,1)S(1)} async-done(((bf16[16,256,128]{2,1,0:T(8,128)(2,1)}), bf16[16,256,128]{2,1,0:T(8,128)(2,1)S(1)}, u32[]{:S(2)}, u32[]{:S(2)}) %all-to-all-start.1) | async-done | bytes 1048608 | tf_op jit(solution)/shard_map/all_to_all | solution.py:111
  35.7 4.4 %all-to-all-start = ((bf16[16,256,128]{1,2,0:T(8,128)(2,1)}), bf16[16,256,128]{1,2,0:T(8,128)(2,1)}, u32[]{:S(2)}, u32[]{:S(2)}) async-start(bf16[16,256,128]{1,2,0:T(8,128)(2,1)} %fusion.22), calls=%async_computation | async-start | bytes 2097152 | tf_op jit(solution)/shard_map/all_to_all | solution.py:122
  40.1 2.1 reshape.480
  42.2 1.9 copy.96
  44.1 2.1 reshape.481
  46.1 1.1 copy.102
  47.3 1.7 multiply_reduce_fusion
  50.1 4.7 %all-to-all-done = bf16[16,256,128]{1,2,0:T(8,128)(2,1)} async-done(((bf16[16,256,128]{1,2,0:T(8,128)(2,1)}), bf16[16,256,128]{1,2,0:T(8,128)(2,1)}, u32[]{:S(2)}, u32[]{:S(2)}) %all-to-all-start) | async-done | bytes 1048608 | tf_op jit(solution)/shard_map/all_to_all | solution.py:122
  54.8 3.2 %fusion.35 = f32[256,512]{1,0:T(8,128)} fusion(bf16[16,256,128]{1,2,0:T(8,128)(2,1)} %all-to-all-done, bf16[16,512]{1,0:T(8,128)(2,1)S(1)} %bitcast.276, bf16[128,512]{1,0:T(8,128)(2,1)} %bitcast.267, bf16[16,256,128]{2,1,0:T(8,128)(2,1)} %copy-done.2), kind=kOutput, calls=%fused_computation.45 | convolution fusion | flops 672661504 | bytes 2244608 | tf_op jit(solution)/shard_map/sma,san->mn/dot_general | solution.py:37
  58.0 2.2 fusion.76
  60.2 3.2 %fusion.38 = f32[256,512]{1,0:T(8,128)} fusion(bf16[16,256,128]{1,2,0:T(8,128)(2,1)} %all-to-all-done, bf16[16,512]{1,0:T(8,128)(2,1)S(1)} %bitcast.277, bf16[128,512]{1,0:T(8,128)(2,1)} %bitcast.268, bf16[16,256,128]{2,1,0:T(8,128)(2,1)} %copy-done.2), kind=kOutput, calls=%fused_computation.46 | convolution fusion | flops 672661504 | bytes 2244608 | tf_op jit(solution)/shard_map/sma,san->mn/dot_general | solution.py:37
  63.4 1.5 fusion.78
  65.6 3.6 %convert_bitcast_fusion.1 = bf16[16,2,256,128]{2,3,1,0:T(8,128)(2,1)} fusion(bf16[16,512]{1,0:T(8,128)(2,1)S(1)} %bitcast.284, bf16[128,512]{1,0:T(8,128)(2,1)} %bitcast.269, bf16[1,256,512]{2,1,0:T(8,128)(2,1)S(1)} %bitcast.250, bf16[1,256,512]{2,1,0:T(8,128)(2,1)} %bitcast.252), kind=kOutput, calls=%fused_computation.24 | convolution fusion | flops 1080033280 | bytes 2768896 | tf_op jit(solution)/shard_map/dmn,scn->sdmc/dot_general | solution.py:168
  69.3 3.9 %copy.105 = bf16[16,2,256,128]{3,2,1,0:T(8,128)(2,1)} copy(bf16[16,2,256,128]{2,3,1,0:T(8,128)(2,1)} %convert_bitcast_fusion.1) | data formatting | bytes 4194304 | tf_op jit(solution)/shard_map/convert_element_type | solution.py:174
  73.2 4.6 %all-to-all-start.3 = ((bf16[16,512,128]{2,1,0:T(8,128)(2,1)}), bf16[16,512,128]{2,1,0:T(8,128)(2,1)}, u32[]{:S(2)}, u32[]{:S(2)}) async-start(bf16[16,512,128]{2,1,0:T(8,128)(2,1)} %bitcast.241), calls=%async_computation.3 | async-start | bytes 4194304 | tf_op jit(solution)/shard_map/all_to_all | solution.py:160
  77.8 1.6 convolution_bitcast_fusion.1
  79.4 1.5 copy-done.1
  80.9 0.9 fusion.169
  81.8 1.1 fusion.170
  82.9 2.1 copy.106
  85.0 2.1 copy.107
  87.0 3.2 %mul.184 = bf16[16,4,128,128]{2,1,3,0:T(4,128)(2,1)} broadcast(bf16[16,128,128]{1,2,0:T(8,128)(2,1)} %copy.107), dimensions={0,2,3} | broadcast | bytes 2621440 | tf_op jit(solution)/shard_map/mul | solution.py:137
  90.2 4.1 %mul.185 = bf16[1,16,512,128]{2,3,1,0:T(8,128)(2,1)} reshape(bf16[16,4,128,128]{2,1,3,0:T(4,128)(2,1)} %mul.184) | data formatting | bytes 4194304 | tf_op jit(solution)/shard_map/mul | solution.py:137
  94.4 3.2 %mul.180 = bf16[16,4,128,128]{2,1,3,0:T(4,128)(2,1)} broadcast(bf16[16,128,128]{1,2,0:T(8,128)(2,1)} %copy.106), dimensions={0,2,3} | broadcast | bytes 2621440 | tf_op jit(solution)/shard_map/mul | solution.py:134
  97.6 4.1 %mul.181 = bf16[1,16,512,128]{2,3,1,0:T(8,128)(2,1)} reshape(bf16[16,4,128,128]{2,1,3,0:T(4,128)(2,1)} %mul.180) | data formatting | bytes 4194304 | tf_op jit(solution)/shard_map/mul | solution.py:134
  101.7 2.6 %broadcast_multiply_fusion.1 = (bf16[1,16,512,128]{2,3,1,0:T(8,128)(2,1)S(1)}, bf16[1,16,512,128]{2,3,1,0:T(8,128)(2,1)S(1)}) fusion(bf16[1,16,512,128]{2,3,1,0:T(8,128)(2,1)} %mul.181, bf16[16,512]{1,0:T(8,128)(2,1)S(1)} %bitcast.278, bf16[1,16,512,128]{2,3,1,0:T(8,128)(2,1)} %mul.185), kind=kLoop, calls=%fused_computation.89 | loop fusion | flops 2097152 | bytes 8404992 | tf_op jit(solution)/shard_map/mul | solution.py:134
  104.3 1.4 copy-done.12
  106.4 2.6 %convert_bitcast_fusion = bf16[16,2,256,128]{2,3,0,1:T(8,128)(2,1)} fusion(bf16[1,16,512,128]{2,3,1,0:T(8,128)(2,1)S(1)} %get-tuple-element.117, bf16[1,16,512,128]{2,3,1,0:T(8,128)(2,1)S(1)} %get-tuple-element.116, bf16[1,256,512]{2,1,0:T(8,128)(2,1)S(1)} %bitcast.261, bf16[1,256,512]{2,1,0:T(8,128)(2,1)S(1)} %bitcast.263), kind=kOutput, calls=%fused_computation.23 | convolution fusion | flops 1077149696 | bytes 6815744 | tf_op jit(solution)/shard_map/dmn,dsnc->sdmc/dot_general | solution.py:144
  109.0 4.0 %copy.108 = bf16[16,2,256,128]{3,2,1,0:T(8,128)(2,1)} copy(bf16[16,2,256,128]{2,3,0,1:T(8,128)(2,1)} %convert_bitcast_fusion) | data formatting | bytes 4194304 | tf_op jit(solution)/shard_map/convert_element_type | solution.py:149
  112.9 6.4 %all-to-all-start.4 = ((bf16[16,512,128]{2,1,0:T(8,128)(2,1)}), bf16[16,512,128]{2,1,0:T(8,128)(2,1)}, u32[]{:S(2)}, u32[]{:S(2)}) async-start(bf16[16,512,128]{2,1,0:T(8,128)(2,1)} %bitcast.242), calls=%async_computation.4 | async-start | bytes 4194304 | tf_op jit(solution)/shard_map/all_to_all | solution.py:160
  119.3 1.2 convolution_bitcast_fusion.6
  121.3 1.6 reshape.459
  122.9 1.7 convert_reduce_fusion.2
  124.6 2.5 %fusion.168 = (f32[1,4,64,512]{3,2,1,0:T(8,128)S(1)}, f32[1,4,64,512]{3,2,1,0:T(8,128)}, f32[1,4,64,512]{3,2,1,0:T(8,128)}) fusion(f32[1,4,320,512]{3,2,1,0:T(8,128)} %copy-done.1), kind=kLoop, calls=%fused_computation.196 | loop fusion | bytes 3145728 | tf_op jit(solution)/shard_map/slice | solution.py:238
  127.1 1.1 fusion.82
  129.0 3.2 %fusion.41 = f32[256,512]{1,0:T(8,128)} fusion(bf16[16,512,128]{2,1,0:T(8,128)(2,1)} %all-to-all-done.3, bf16[16,512]{1,0:T(8,128)(2,1)S(1)} %bitcast.279, bf16[128,512]{1,0:T(8,128)(2,1)} %bitcast.270, bf16[16,256,128]{2,1,0:T(8,128)(2,1)} %copy-done.2), kind=kOutput, calls=%fused_computation.47 | convolution fusion | flops 672661504 | bytes 2244608 | tf_op jit(solution)/shard_map/sma,san->mn/dot_general | solution.py:37
  132.2 2.2 fusion.77
  134.4 9.8 %all-to-all-done.4 = bf16[16,512,128]{2,1,0:T(8,128)(2,1)} async-done(((bf16[16,512,128]{2,1,0:T(8,128)(2,1)}), bf16[16,512,128]{2,1,0:T(8,128)(2,1)}, u32[]{:S(2)}, u32[]{:S(2)}) %all-to-all-start.4) | async-done | bytes 2097184 | tf_op jit(solution)/shard_map/all_to_all | solution.py:160
  144.1 2.0 fusion.47
  147.1 2.1 fusion.50
  150.9 2.3 fusion.25
  153.2 6.7 %all-to-all-start.5 = ((bf16[16,256,128]{1,2,0:T(8,128)(2,1)}), bf16[16,256,128]{1,2,0:T(8,128)(2,1)}, u32[]{:S(2)}, u32[]{:S(2)}) async-start(bf16[16,256,128]{1,2,0:T(8,128)(2,1)} %fusion.25), calls=%async_computation.5 | async-start | bytes 2097152 | tf_op jit(solution)/shard_map/all_to_all | solution.py:160
  159.9 3.2 %fusion.44 = f32[256,512]{1,0:T(8,128)} fusion(bf16[16,512,128]{2,1,0:T(8,128)(2,1)} %all-to-all-done.3, bf16[16,512]{1,0:T(8,128)(2,1)S(1)} %bitcast.280, bf16[128,512]{1,0:T(8,128)(2,1)} %bitcast.272, bf16[16,256,128]{2,1,0:T(8,128)(2,1)} %copy-done.2), kind=kOutput, calls=%fused_computation.48 | convolution fusion | flops 672661504 | bytes 2244608 | tf_op jit(solution)/shard_map/sma,san->mn/dot_general | solution.py:37
  163.1 1.0 constant_dynamic-update-slice_fusion.2
  164.1 1.0 constant_dynamic-update-slice_fusion.1
  165.1 1.5 fusion.79
  167.8 2.2 convolution_add_fusion.2
  170.0 3.3 %all-to-all-done.5 = bf16[16,256,128]{1,2,0:T(8,128)(2,1)} async-done(((bf16[16,256,128]{1,2,0:T(8,128)(2,1)}), bf16[16,256,128]{1,2,0:T(8,128)(2,1)}, u32[]{:S(2)}, u32[]{:S(2)}) %all-to-all-start.5) | async-done | bytes 1048608 | tf_op jit(solution)/shard_map/all_to_all | solution.py:160
  173.3 2.0 fusion.53
  178.0 1.0 concatenate.47
  179.4 10.8 %all_to_all.52 = f32[16,1,3356]{2,1,0:T(1,128)S(1)} all-to-all(f32[16,1,3356]{2,1,0:T(1,128)S(1)} %all_to_all.39), channel_id=1, replica_groups=mesh['node'=16,'batch'=16] {'node'}, dimensions={0} | all-to-all | bytes 429568 | tf_op jit(solution)/shard_map/all_to_all | solution.py:54
  191.1 14.4 %all-to-all-start.7 = ((f32[16,1,3356]{2,1,0:T(1,128)}), f32[16,1,3356]{2,1,0:T(1,128)S(1)}, u32[]{:S(2)}, u32[]{:S(2)}) async-start(f32[16,1,3356]{2,1,0:T(1,128)} %broadcast_in_dim.4), calls=%async_computation.7 | async-start | bytes 442368 | tf_op jit(solution)/shard_map/all_to_all | solution.py:58
  205.6 1.1 fusion.80
  206.7 0.8 copy.114
  207.5 8.8 %all-to-all-done.7 = f32[16,1,3356]{2,1,0:T(1,128)S(1)} async-done(((f32[16,1,3356]{2,1,0:T(1,128)}), f32[16,1,3356]{2,1,0:T(1,128)S(1)}, u32[]{:S(2)}, u32[]{:S(2)}) %all-to-all-start.7) | async-done | bytes 214816 | tf_op jit(solution)/shard_map/all_to_all | solution.py:58
  217.3 3.5 %all-to-all-start.8 = ((f32[16,1,3356]{2,1,0:T(1,128)}), f32[16,1,3356]{2,1,0:T(1,128)S(1)}, u32[]{:S(2)}, u32[]{:S(2)}) async-start(f32[16,1,3356]{2,1,0:T(1,128)} %broadcast_in_dim.5), calls=%async_computation.8 | async-start | bytes 442368 | tf_op jit(solution)/shard_map/all_to_all | solution.py:60
  220.8 1.1 fusion.72
  222.7 6.4 %all-to-all-done.8 = f32[16,1,3356]{2,1,0:T(1,128)S(1)} async-done(((f32[16,1,3356]{2,1,0:T(1,128)}), f32[16,1,3356]{2,1,0:T(1,128)S(1)}, u32[]{:S(2)}, u32[]{:S(2)}) %all-to-all-start.8) | async-done | bytes 214816 | tf_op jit(solution)/shard_map/all_to_all | solution.py:60
  (141 shorter events, 21.6 us)
Async XLA Ops:
  0.6 77.2 %copy-start = (bf16[64,320]{1,0:T(8,128)(2,1)S(1)}, bf16[64,320]{1,0:T(8,128)(2,1)}, u32[]{:S(2)}) copy-start(bf16[64,320]{1,0:T(8,128)(2,1)} %param.24) | copy-start | bytes 122884
  2.0 13.9 %all-to-all-start.2 = ((bf16[16,1,4]{2,1,0:T(2,128)(2,1)}), bf16[16,1,4]{2,1,0:T(2,128)(2,1)S(1)}, u32[]{:S(2)}, u32[]{:S(2)}) async-start(bf16[16,1,4]{2,1,0:T(2,128)(2,1)} %compare_convert_fusion), calls=%async_computation.2 | async-start | bytes 16384 | tf_op jit(solution)/shard_map/all_to_all | solution.py:109
  10.4 54.5 %copy-start.41 = (bf16[2,8,4,128]{3,1,2,0:T(8,128)(2,1)}, bf16[2,8,4,128]{3,1,2,0:T(8,128)(2,1)S(1)}, u32[]{:S(2)}) copy-start(bf16[2,8,4,128]{3,1,2,0:T(8,128)(2,1)S(1)} %copy.172) | copy-start | bytes 49156
  10.5 9.8 %copy-start.18 = (bf16[1,6,64,512]{3,2,1,0:T(8,128)(2,1)S(1)}, bf16[1,6,64,512]{3,2,1,0:T(8,128)(2,1)}, u32[]{:S(2)}) copy-start(bf16[1,6,64,512]{3,2,1,0:T(8,128)(2,1)} %param.21) | copy-start | bytes 1179652
  12.8 8.2 %copy-start.33 = (bf16[128,128]{1,0:T(8,128)(2,1)S(1)}, bf16[128,128]{1,0:T(8,128)(2,1)}, u32[]{:S(2)}) copy-start(bf16[128,128]{1,0:T(8,128)(2,1)} %param.22) | copy-start | bytes 98308
  12.8 8.2 %copy-start.45 = (f32[128]{0:T(128)S(1)}, f32[128]{0:T(128)}, u32[]{:S(2)}) copy-start(f32[128]{0:T(128)} %param.23) | copy-start | bytes 1540
  15.9 19.7 %all-to-all-start.1 = ((bf16[16,256,128]{2,1,0:T(8,128)(2,1)}), bf16[16,256,128]{2,1,0:T(8,128)(2,1)S(1)}, u32[]{:S(2)}, u32[]{:S(2)}) async-start(bf16[16,256,128]{2,1,0:T(8,128)(2,1)} %pad_maximum_fusion.9), calls=%async_computation.1 | async-start | bytes 2097152 | tf_op jit(solution)/shard_map/all_to_all | solution.py:111
  20.2 2.1 copy-start.35
  20.3 0.7 copy-start.20
  20.3 0.8 copy-start.22
  21.6 0.7 copy-start.4
  35.7 10.4 %copy-start.2 = (bf16[16,256,128]{2,1,0:T(8,128)(2,1)}, bf16[16,256,128]{2,1,0:T(8,128)(2,1)S(1)}, u32[]{:S(2)}) copy-start(bf16[16,256,128]{2,1,0:T(8,128)(2,1)S(1)} %all-to-all-done.1) | copy-start | bytes 3145732
  35.7 19.1 %all-to-all-start = ((bf16[16,256,128]{1,2,0:T(8,128)(2,1)}), bf16[16,256,128]{1,2,0:T(8,128)(2,1)}, u32[]{:S(2)}, u32[]{:S(2)}) async-start(bf16[16,256,128]{1,2,0:T(8,128)(2,1)} %fusion.22), calls=%async_computation | async-start | bytes 2097152 | tf_op jit(solution)/shard_map/all_to_all | solution.py:122
  50.1 51.6 %copy-start.39 = (bf16[2,8,4,128]{3,1,2,0:T(8,128)(2,1)}, bf16[2,8,4,128]{3,1,2,0:T(8,128)(2,1)S(1)}, u32[]{:S(2)}) copy-start(bf16[2,8,4,128]{3,1,2,0:T(8,128)(2,1)S(1)} %copy.171) | copy-start | bytes 49156
  64.9 0.7 copy-start.8
  73.2 39.8 %all-to-all-start.3 = ((bf16[16,512,128]{2,1,0:T(8,128)(2,1)}), bf16[16,512,128]{2,1,0:T(8,128)(2,1)}, u32[]{:S(2)}, u32[]{:S(2)}) async-start(bf16[16,512,128]{2,1,0:T(8,128)(2,1)} %bitcast.241), calls=%async_computation.3 | async-start | bytes 4194304 | tf_op jit(solution)/shard_map/all_to_all | solution.py:160
  77.8 4.0 %copy-start.3 = (bf16[16,256,128]{2,1,0:T(8,128)(2,1)S(1)}, bf16[16,256,128]{2,1,0:T(8,128)(2,1)}, u32[]{:S(2)}) copy-start(bf16[16,256,128]{2,1,0:T(8,128)(2,1)} %copy-done.2) | copy-start | bytes 3145732
  79.4 1.5 copy-start.1
  101.7 4.6 %copy-start.25 = (bf16[1,4,64,512]{3,2,1,0:T(8,128)(2,1)S(1)}, bf16[1,4,64,512]{3,2,1,0:T(8,128)(2,1)}, u32[]{:S(2)}) copy-start(bf16[1,4,64,512]{3,2,1,0:T(8,128)(2,1)} %get-tuple-element.107) | copy-start | bytes 786436
  101.7 4.6 %copy-start.27 = (bf16[1,4,64,512]{3,2,1,0:T(8,128)(2,1)S(1)}, bf16[1,4,64,512]{3,2,1,0:T(8,128)(2,1)}, u32[]{:S(2)}) copy-start(bf16[1,4,64,512]{3,2,1,0:T(8,128)(2,1)} %get-tuple-element.106) | copy-start | bytes 786436
  104.3 1.4 copy-start.12
  104.3 2.1 copy-start.14
  112.9 31.2 %all-to-all-start.4 = ((bf16[16,512,128]{2,1,0:T(8,128)(2,1)}), bf16[16,512,128]{2,1,0:T(8,128)(2,1)}, u32[]{:S(2)}, u32[]{:S(2)}) async-start(bf16[16,512,128]{2,1,0:T(8,128)(2,1)} %bitcast.242), calls=%async_computation.4 | async-start | bytes 4194304 | tf_op jit(solution)/shard_map/all_to_all | solution.py:160
  119.3 7.8 %copy-start.37 = (bf16[256,64]{0,1:T(8,128)(2,1)S(1)}, bf16[256,64]{0,1:T(8,128)(2,1)}, u32[]{:S(2)}) copy-start(bf16[256,64]{0,1:T(8,128)(2,1)} %param.26) | copy-start | bytes 98308
  122.9 4.2 %copy-start.7 = (bf16[1,256,512]{2,1,0:T(8,128)(2,1)S(1)}, bf16[1,256,512]{2,1,0:T(8,128)(2,1)}, u32[]{:S(2)}) copy-start(bf16[1,256,512]{2,1,0:T(8,128)(2,1)} %param.35) | copy-start | bytes 786436
  122.9 6.1 %copy-start.9 = (bf16[256,512]{1,0:T(8,128)(2,1)S(1)}, bf16[256,512]{1,0:T(8,128)(2,1)}, u32[]{:S(2)}) copy-start(bf16[256,512]{1,0:T(8,128)(2,1)} %fusion.76) | copy-start | bytes 786436
  124.6 4.4 %copy-start.40 = (bf16[2,8,4,128]{3,1,2,0:T(8,128)(2,1)S(1)}, bf16[2,8,4,128]{3,1,2,0:T(8,128)(2,1)}, u32[]{:S(2)}) copy-start(bf16[2,8,4,128]{3,1,2,0:T(8,128)(2,1)} %copy-done.39) | copy-start | bytes 49156
  128.2 0.8 copy-start.11
  129.0 15.1 %copy-start.42 = (bf16[2,8,4,128]{3,1,2,0:T(8,128)(2,1)S(1)}, bf16[2,8,4,128]{3,1,2,0:T(8,128)(2,1)}, u32[]{:S(2)}) copy-start(bf16[2,8,4,128]{3,1,2,0:T(8,128)(2,1)} %copy-done.41) | copy-start | bytes 49156
  144.1 2.0 copy-start.17
  144.1 2.0 copy-start.28
  146.2 0.9 copy-start.36
  147.1 2.5 %copy-start.24 = (bf16[256,512]{1,0:T(8,128)(2,1)}, bf16[256,512]{1,0:T(8,128)(2,1)S(1)}, u32[]{:S(2)}) copy-start(bf16[256,512]{1,0:T(8,128)(2,1)S(1)} %fusion.69) | copy-start | bytes 786436
  147.1 2.1 copy-start.16
  147.1 2.1 copy-start.26
  147.1 3.2 %copy-start.15 = (bf16[1,16,512,128]{2,3,1,0:T(8,128)(2,1)S(1)}, bf16[1,16,512,128]{2,3,1,0:T(8,128)(2,1)}, u32[]{:S(2)}) copy-start(bf16[1,16,512,128]{2,3,1,0:T(8,128)(2,1)} %copy-done.14) | copy-start | bytes 6291460
  149.2 1.7 copy-start.13
  149.5 0.7 copy-start.29
  153.2 20.2 %all-to-all-start.5 = ((bf16[16,256,128]{1,2,0:T(8,128)(2,1)}), bf16[16,256,128]{1,2,0:T(8,128)(2,1)}, u32[]{:S(2)}, u32[]{:S(2)}) async-start(bf16[16,256,128]{1,2,0:T(8,128)(2,1)} %fusion.25), calls=%async_computation.5 | async-start | bytes 2097152 | tf_op jit(solution)/shard_map/all_to_all | solution.py:160
  163.1 3.5 %copy-start.5 = (bf16[1,4,64,512]{3,2,1,0:T(8,128)(2,1)S(1)}, bf16[1,4,64,512]{3,2,1,0:T(8,128)(2,1)}, u32[]{:S(2)}) copy-start(bf16[1,4,64,512]{3,2,1,0:T(8,128)(2,1)} %param.34) | copy-start | bytes 786436
  170.0 5.3 %copy-start.10 = (f32[256,512]{1,0:T(8,128)S(1)}, f32[256,512]{1,0:T(8,128)}, u32[]{:S(2)}) copy-start(f32[256,512]{1,0:T(8,128)} %convolution_add_fusion.2) | copy-start | bytes 1572868
  173.3 2.0 copy-start.30
  175.4 1.0 copy-start.21
  175.4 1.0 copy-start.23
  175.7 1.0 copy-start.34
  176.7 1.0 copy-start.6
  177.1 0.9 copy-start.31
  177.1 0.9 copy-start.32
  177.1 0.9 copy-start.43
  177.7 27.9 %copy-start.38 = (bf16[256,64]{0,1:T(8,128)(2,1)S(1)}, bf16[256,64]{0,1:T(8,128)(2,1)}, u32[]{:S(2)}) copy-start(bf16[256,64]{0,1:T(8,128)(2,1)} %param.26) | copy-start | bytes 98308
  177.7 27.9 %copy-start.44 = (f32[256]{0:T(256)S(1)}, f32[256]{0:T(256)}, u32[]{:S(2)}) copy-start(f32[256]{0:T(256)} %param.27) | copy-start | bytes 3076
  178.0 42.8 %copy-start.19 = (bf16[1,6,64,512]{3,2,1,0:T(8,128)(2,1)S(1)}, bf16[1,6,64,512]{3,2,1,0:T(8,128)(2,1)}, u32[]{:S(2)}) copy-start(bf16[1,6,64,512]{3,2,1,0:T(8,128)(2,1)} %param.21) | copy-start | bytes 1179652
  178.0 42.8 %copy-start.46 = (f32[64]{0:T(128)S(1)}, f32[64]{0:T(128)}, u32[]{:S(2)}) copy-start(f32[64]{0:T(128)} %param.25) | copy-start | bytes 772
  191.1 25.2 %all-to-all-start.7 = ((f32[16,1,3356]{2,1,0:T(1,128)}), f32[16,1,3356]{2,1,0:T(1,128)S(1)}, u32[]{:S(2)}, u32[]{:S(2)}) async-start(f32[16,1,3356]{2,1,0:T(1,128)} %broadcast_in_dim.4), calls=%async_computation.7 | async-start | bytes 442368 | tf_op jit(solution)/shard_map/all_to_all | solution.py:58
  217.3 11.8 %all-to-all-start.8 = ((f32[16,1,3356]{2,1,0:T(1,128)}), f32[16,1,3356]{2,1,0:T(1,128)S(1)}, u32[]{:S(2)}, u32[]{:S(2)}) async-start(f32[16,1,3356]{2,1,0:T(1,128)} %broadcast_in_dim.5), calls=%async_computation.8 | async-start | bytes 442368 | tf_op jit(solution)/shard_map/all_to_all | solution.py:60

commit v7 on v5

--- a/solution.py
+++ b/solution.py
@@ -106,16 +106,18 @@
     dense_fwd = dense_band(local_fwd, blocks, tile_width)
     dense_bwd = dense_band(local_bwd, blocks, tile_width)
     src_placer = spread_onehot(own_src, eye_slots)
-    recv_dst = lax.all_to_all(own_dst, "node", split_axis=0, concat_axis=0, tiled=True)
-    dst_placer = spread_onehot(recv_dst, eye_slots)
+    dst_rows = jnp.zeros((own_dst.shape[0], 8, tile_width), jnp.bfloat16)
+    dst_rows = dst_rows.at[:, 0, :blocks].set(own_dst)
     tiles_in = lax.all_to_all(
-        jnp.concatenate([remote_fwd, remote_bwd], axis=1),
+        jnp.concatenate([remote_fwd, remote_bwd, dst_rows], axis=1),
         "node",
         split_axis=0,
         concat_axis=0,
         tiled=True,
     )
-    tiles_fwd, tiles_bwd = tiles_in[:, :tile_width], tiles_in[:, tile_width:]
+    recv_dst = tiles_in[:, 2 * tile_width, :blocks]
+    dst_placer = spread_onehot(recv_dst, eye_slots)
+    tiles_fwd, tiles_bwd = tiles_in[:, :tile_width], tiles_in[:, tile_width : 2 * tile_width]
 
     def swap(pieces):
         got_all = lax.all_to_all(

time: 208 us -> 201 us (0.966)
  starting transfers between devices: 54.6 us -> 48.4 us
    all_to_all x2 -> x1, starting transfers between devices: 14.3 us -> 7.75 us  [shards(): lax.all_to_all(jnp.concatenate([remote_fwd, remote_bwd, dst_rows], axis=1...]
    all_to_all x2 -> x1, waiting for transfers between devices: 11.7 us -> 8.74 us  [shards(): lax.all_to_all(jnp.concatenate([remote_fwd, remote_bwd, dst_rows], axis=1...]
    unnamed x84 -> x80, local copies, waits for them, and re-layouts: 10.4 us -> 8.44 us
  transfers between devices with their start and end apart: 8 -> 7, of which waited for: 6 -> 6; matrix products, arithmetic and copies ran while one was open for 38% -> 38% of each run, Pallas kernels for 0% -> 0%
where the time goes in v7:
time: 201 us; the launch traced here: 199 us
  matrix products  58.5 us (29%)
  starting transfers between devices  48.4 us (24%)
  waiting for transfers between devices  38.8 us (19%)
  local copies, waits for them, and re-layouts  23.1 us (11%)
  other arithmetic  15 us (7%)
  blocking collectives  13.8 us (7%)
    all_to_all x4, starting transfers between devices, swap(): lax.all_to_all(jnp.concatenate(pieces, axis=1), 'node', split_axis=0, con...  25 us
    dot_general x7, matrix products, place_rows(): jnp.einsum('sma,san->mn', pieces, placer, preferred_element_type=jnp.floa...  18.9 us
    all_to_all x4, waiting for transfers between devices, swap(): lax.all_to_all(jnp.concatenate(pieces, axis=1), 'node', split_axis=0, con...  14.8 us
    dot_general x4, matrix products, row_terms(): jnp.einsum('sma,sac->smc', wanted, tiles, preferred_element_type=jnp.floa...  14.6 us
    all_to_all x1, blocking collectives, exchange_sum(): lax.all_to_all(flat.reshape(node_count, padded // node_count), 'node', 0,...  13.8 us
    all_to_all x1, starting transfers between devices, exchange_sum(): part = lax.all_to_all(part, 'batch', 0, 0, tiled=True).sum(axis=0)  12.1 us
    all_to_all x1, waiting for transfers between devices, exchange_sum(): part = lax.all_to_all(part, 'batch', 0, 0, tiled=True).sum(axis=0)  8.8 us
    all_to_all x1, waiting for transfers between devices, shards(): lax.all_to_all(jnp.concatenate([remote_fwd, remote_bwd, dst_rows], axis=1...  8.74 us
  transfers between devices with their start and end apart: 7, of which 6 were waited for; matrix products, arithmetic and copies ran while one was open for 38% of the time, Pallas kernels for 0%

profile of v7, /device:TPU:1, one launch (start us, length us, event | category | flops | bytes accessed | tf_op | source)
XLA Modules:
  0.0 199.1 jit_solution(12859732272397817553)
XLA Ops:
  0.7 0.8 iota_compare_fusion.1
  1.5 2.3 %pad_maximum_fusion.2 = bf16[16,264,128]{2,1,0:T(8,128)(2,1)} fusion(bf16[16,8,128]{2,1,0:T(8,128)(2,1)S(1)} %pad_convert_fusion, bf16[16,128,128]{2,1,0:T(8,128)(2,1)} %param.33, bf16[16,128,128]{2,1,0:T(8,128)(2,1)} %param.32), kind=kLoop, calls=%fused_computation.99 | loop fusion | flops 3244032 | bytes 2162688 | tf_op jit(solution)/shard_map/concatenate | solution.py:112
  3.8 7.7 %all-to-all-start.1 = ((bf16[16,264,128]{2,1,0:T(8,128)(2,1)}), bf16[16,264,128]{2,1,0:T(8,128)(2,1)}, u32[]{:S(2)}, u32[]{:S(2)}) async-start(bf16[16,264,128]{2,1,0:T(8,128)(2,1)} %pad_maximum_fusion.2), calls=%async_computation.1 | async-start | bytes 2162688 | tf_op jit(solution)/shard_map/all_to_all | solution.py:111
  15.1 0.9 fusion.229
  16.8 0.7 copy-done.2
  17.5 1.8 fusion.55
  19.3 8.7 %all-to-all-done.1 = bf16[16,264,128]{2,1,0:T(8,128)(2,1)} async-done(((bf16[16,264,128]{2,1,0:T(8,128)(2,1)}), bf16[16,264,128]{2,1,0:T(8,128)(2,1)}, u32[]{:S(2)}, u32[]{:S(2)}) %all-to-all-start.1) | async-done | bytes 1081376 | tf_op jit(solution)/shard_map/all_to_all | solution.py:111
  28.0 4.8 %all-to-all-start = ((bf16[16,256,128]{1,2,0:T(8,128)(2,1)}), bf16[16,256,128]{1,2,0:T(8,128)(2,1)}, u32[]{:S(2)}, u32[]{:S(2)}) async-start(bf16[16,256,128]{1,2,0:T(8,128)(2,1)} %fusion.55), calls=%async_computation | async-start | bytes 2097152 | tf_op jit(solution)/shard_map/all_to_all | solution.py:123
  32.8 2.5 %fusion.228 = (f32[1,4,64,512]{3,2,1,0:T(8,128)}, f32[1,4,64,512]{3,2,1,0:T(8,128)}, f32[1,4,64,512]{3,2,1,0:T(8,128)}) fusion(f32[1,4,320,512]{3,2,1,0:T(8,128)} %copy-done.1), kind=kLoop, calls=%fused_computation.218 | loop fusion | bytes 3145728 | tf_op jit(solution)/shard_map/slice | solution.py:209
  35.3 0.8 slice.216
  36.4 3.4 %convolution_convert_fusion = bf16[16,256,128]{2,1,0:T(8,128)(2,1)} fusion(bf16[256,512,1]{1,0,2:T(8,128)(2,1)} %bitcast.238, bf16[16,512]{1,0:T(8,128)(2,1)S(1)} %bitcast.265, bf16[128,512]{1,0:T(8,128)(2,1)} %bitcast.243, bf16[16,264,128]{2,1,0:T(8,128)(2,1)} %all-to-all-done.1), kind=kOutput, calls=%fused_computation.42 | convolution fusion | flops 673185792 | bytes 1982464 | tf_op jit(solution)/shard_map/sma,sac->smc/dot_general | solution.py:135
  39.8 3.4 %convolution_convert_fusion.1 = bf16[16,256,128]{2,1,0:T(8,128)(2,1)} fusion(bf16[256,512,1]{1,0,2:T(8,128)(2,1)} %bitcast.240, bf16[16,512]{1,0:T(8,128)(2,1)S(1)} %bitcast.266, bf16[128,512]{1,0:T(8,128)(2,1)} %bitcast.244, bf16[16,264,128]{2,1,0:T(8,128)(2,1)} %all-to-all-done.1), kind=kOutput, calls=%fused_computation.43 | convolution fusion | flops 673185792 | bytes 1982464 | tf_op jit(solution)/shard_map/sma,sac->smc/dot_general | solution.py:135
  43.1 3.1 %pad_maximum_fusion.1 = bf16[16,512,128]{2,1,0:T(8,128)(2,1)} fusion(bf16[16,256,128]{2,1,0:T(8,128)(2,1)} %convolution_convert_fusion, bf16[16,256,128]{2,1,0:T(8,128)(2,1)} %convolution_convert_fusion.1), kind=kLoop, calls=%fused_computation.30 | loop fusion | flops 4194304 | bytes 4194304 | tf_op jit(solution)/shard_map/concatenate | solution.py:124
  46.2 1.6 all-to-all-done
  47.8 5.2 %all-to-all-start.3 = ((bf16[16,512,128]{2,1,0:T(8,128)(2,1)}), bf16[16,512,128]{2,1,0:T(8,128)(2,1)}, u32[]{:S(2)}, u32[]{:S(2)}) async-start(bf16[16,512,128]{2,1,0:T(8,128)(2,1)} %pad_maximum_fusion.1), calls=%async_computation.3 | async-start | bytes 4194304 | tf_op jit(solution)/shard_map/all_to_all | solution.py:123
  53.0 1.8 fusion.123
  54.8 3.3 %fusion.79 = f32[256,512]{1,0:T(8,128)} fusion(bf16[16,256,128]{1,2,0:T(8,128)(2,1)} %all-to-all-done, bf16[16,512]{1,0:T(8,128)(2,1)S(1)} %bitcast.267, bf16[128,512]{1,0:T(8,128)(2,1)} %bitcast.245, bf16[16,264,128]{2,1,0:T(8,128)(2,1)} %all-to-all-done.1), kind=kOutput, calls=%fused_computation.63 | convolution fusion | flops 672661504 | bytes 2244608 | tf_op jit(solution)/shard_map/sma,san->mn/dot_general | solution.py:37
  58.1 1.5 fusion.119
  59.6 0.7 copy-done.6
  60.3 2.7 %fusion.49 = bf16[16,256,128]{1,2,0:T(8,128)(2,1)} fusion(bf16[16,512]{1,0:T(8,128)(2,1)S(1)} %bitcast.260, bf16[128,512]{1,0:T(8,128)(2,1)} %bitcast.246, bf16[256,512]{1,0:T(8,128)(2,1)S(1)} %fusion.119), kind=kOutput, calls=%fused_computation.48 | convolution fusion | flops 538443776 | bytes 1458176 | tf_op jit(solution)/shard_map/mn,san->sma/dot_general | solution.py:41
  63.0 3.2 %fusion.76 = f32[256,512]{1,0:T(8,128)} fusion(bf16[16,256,128]{1,2,0:T(8,128)(2,1)} %all-to-all-done, bf16[16,512]{1,0:T(8,128)(2,1)S(1)} %bitcast.268, bf16[128,512]{1,0:T(8,128)(2,1)} %bitcast.247, bf16[16,264,128]{2,1,0:T(8,128)(2,1)} %all-to-all-done.1), kind=kOutput, calls=%fused_computation.62 | convolution fusion | flops 672661504 | bytes 2244608 | tf_op jit(solution)/shard_map/sma,san->mn/dot_general | solution.py:37
  66.2 1.5 fusion.117
  67.7 0.7 copy-done.7
  68.4 1.7 fusion.52
  70.1 1.6 pad_maximum_fusion
  71.7 7.0 %all-to-all-done.3 = bf16[16,512,128]{2,1,0:T(8,128)(2,1)} async-done(((bf16[16,512,128]{2,1,0:T(8,128)(2,1)}), bf16[16,512,128]{2,1,0:T(8,128)(2,1)}, u32[]{:S(2)}, u32[]{:S(2)}) %all-to-all-start.3) | async-done | bytes 2097184 | tf_op jit(solution)/shard_map/all_to_all | solution.py:123
  78.6 7.8 %all-to-all-start.2 = ((bf16[16,512,128]{1,2,0:T(8,128)(2,1)}), bf16[16,512,128]{1,2,0:T(8,128)(2,1)}, u32[]{:S(2)}, u32[]{:S(2)}) async-start(bf16[16,512,128]{1,2,0:T(8,128)(2,1)} %pad_maximum_fusion), calls=%async_computation.2 | async-start | bytes 4194304 | tf_op jit(solution)/shard_map/all_to_all | solution.py:123
  86.4 1.2 convolution_bitcast_fusion.6
  87.6 0.8 copy.111
  88.4 1.6 reshape.423
  90.0 1.6 convert_reduce_fusion.2
  91.6 1.0 constant_dynamic-update-slice_fusion.3
  92.6 2.0 fusion.88
  94.6 2.0 %fusion.91 = f32[256,512]{1,0:T(8,128)S(1)} fusion(bf16[16,512,128]{2,1,0:T(8,128)(2,1)} %all-to-all-done.3, bf16[16,512]{1,0:T(8,128)(2,1)S(1)} %bitcast.263, bf16[128,512]{1,0:T(8,128)(2,1)S(1)} %bitcast.256), kind=kOutput, calls=%fused_computation.67 | convolution fusion | flops 537919488 | bytes 1720320 | tf_op jit(solution)/shard_map/sma,san->mn/dot_general | solution.py:37
  96.7 1.0 fusion.110
  97.8 1.0 fusion.111
  98.8 3.7 %fusion.59 = f32[16,256,128]{2,1,0:T(8,128)} fusion(bf16[16,512]{1,0:T(8,128)(2,1)S(1)} %bitcast.269, bf16[128,512]{1,0:T(8,128)(2,1)} %bitcast.250, bf16[16,264,128]{2,1,0:T(8,128)(2,1)} %all-to-all-done.1, bf16[256,512]{1,0:T(8,128)(2,1)} %fusion.110), kind=kOutput, calls=%fused_computation.53 | convolution fusion | flops 672661504 | bytes 3031040 | tf_op jit(solution)/shard_map/sma,sac->smc/dot_general | solution.py:135
  102.5 4.1 %add_convert_fusion = bf16[16,256,128]{2,1,0:T(8,128)(2,1)} fusion(f32[16,256,128]{2,1,0:T(8,128)} %fusion.59, bf16[16,512]{1,0:T(8,128)(2,1)S(1)} %bitcast.270, bf16[128,512]{1,0:T(8,128)(2,1)} %bitcast.251, bf16[16,264,128]{2,1,0:T(8,128)(2,1)} %all-to-all-done.1, bf16[256,512]{1,0:T(8,128)(2,1)} %fusion.111), kind=kOutput, calls=%fused_computation.31 | convolution fusion | flops 673710080 | bytes 4079616 | tf_op jit(solution)/shard_map/sma,sac->smc/dot_general | solution.py:135
  106.6 6.3 %all-to-all-done.2 = bf16[16,512,128]{1,2,0:T(8,128)(2,1)} async-done(((bf16[16,512,128]{1,2,0:T(8,128)(2,1)}), bf16[16,512,128]{1,2,0:T(8,128)(2,1)}, u32[]{:S(2)}, u32[]{:S(2)}) %all-to-all-start.2) | async-done | bytes 2097184 | tf_op jit(solution)/shard_map/all_to_all | solution.py:123
  112.9 7.3 %all-to-all-start.4 = ((bf16[16,256,128]{2,1,0:T(8,128)(2,1)}), bf16[16,256,128]{2,1,0:T(8,128)(2,1)}, u32[]{:S(2)}, u32[]{:S(2)}) async-start(bf16[16,256,128]{2,1,0:T(8,128)(2,1)} %add_convert_fusion), calls=%async_computation.4 | async-start | bytes 2097152 | tf_op jit(solution)/shard_map/all_to_all | solution.py:123
  120.2 3.2 %fusion.82 = f32[256,512]{1,0:T(8,128)} fusion(bf16[16,512,128]{1,2,0:T(8,128)(2,1)} %all-to-all-done.2, bf16[16,512]{1,0:T(8,128)(2,1)S(1)} %bitcast.271, bf16[128,512]{1,0:T(8,128)(2,1)} %bitcast.252, bf16[16,264,128]{2,1,0:T(8,128)(2,1)} %all-to-all-done.1), kind=kOutput, calls=%fused_computation.64 | convolution fusion | flops 672661504 | bytes 2244608 | tf_op jit(solution)/shard_map/sma,san->mn/dot_general | solution.py:37
  123.4 2.2 %fusion.118 = bf16[256,512]{1,0:T(8,128)(2,1)} fusion(f32[256,512]{1,0:T(8,128)} %fusion.82, bf16[256,512]{1,0:T(8,128)(2,1)} %copy-done.7, bf16[64,8,4,128]{3,2,1,0:T(4,128)(2,1)S(1)} %bitcast.221), kind=kOutput, calls=%fused_computation.90 | convolution fusion | flops 134479872 | bytes 1572864 | tf_op jit(solution)/shard_map/mn,kn->mk/dot_general | solution.py:29
  125.6 3.2 %fusion.85 = f32[256,512]{1,0:T(8,128)} fusion(bf16[16,512,128]{1,2,0:T(8,128)(2,1)} %all-to-all-done.2, bf16[16,512]{1,0:T(8,128)(2,1)S(1)} %bitcast.272, bf16[128,512]{1,0:T(8,128)(2,1)} %bitcast.253, bf16[16,264,128]{2,1,0:T(8,128)(2,1)} %all-to-all-done.1), kind=kOutput, calls=%fused_computation.65 | convolution fusion | flops 672661504 | bytes 2244608 | tf_op jit(solution)/shard_map/sma,san->mn/dot_general | solution.py:37
  128.8 1.0 constant_dynamic-update-slice_fusion.2
  129.8 1.0 constant_dynamic-update-slice_fusion.1
  130.8 1.5 fusion.120
  132.8 0.7 reshape.422
  133.5 2.2 %convolution_add_fusion.2 = f32[256,512]{1,0:T(8,128)} fusion(f32[256,512]{1,0:T(8,128)} %bitcast.232, bf16[256,512]{1,0:T(8,128)(2,1)} %fusion.110, bf16[64,8,4,128]{3,2,1,0:T(4,128)(2,1)S(1)} %bitcast.222), kind=kOutput, calls=%fused_computation.73 | convolution fusion | flops 134348800 | bytes 1835008 | tf_op jit(solution)/shard_map/mk,kn->mn/dot_general | solution.py:33
  135.7 2.0 %fusion.94 = f32[256,512]{1,0:T(8,128)S(1)} fusion(bf16[16,256,128]{2,1,0:T(8,128)(2,1)} %all-to-all-done.4, bf16[16,512]{1,0:T(8,128)(2,1)} %bitcast.264, bf16[128,512]{1,0:T(8,128)(2,1)} %bitcast.254), kind=kOutput, calls=%fused_computation.68 | convolution fusion | flops 537919488 | bytes 1720320 | tf_op jit(solution)/shard_map/sma,san->mn/dot_general | solution.py:37
  138.8 0.9 convolution_bitcast_fusion
  141.1 2.6 %concatenate.57 = f32[53696]{0:T(1024)S(1)} concatenate(f32[16384]{0:T(1024)} %convolution_bitcast_fusion, f32[128]{0:T(128)S(1)} %convert_reduce_fusion, f32[20480]{0:T(1024)S(1)} %copy-done.23, f32[64]{0:T(128)S(1)} %get-tuple-element.124, f32[16384]{0:T(1024)} %reshape.423, f32[256]{0:T(256)S(1)} %copy-done.31), dimensions={0} | concatenate | bytes 429568 | tf_op jit(solution)/shard_map/concatenate | solution.py:48
  143.9 13.8 %all_to_all.46 = f32[16,1,3356]{2,1,0:T(1,128)S(1)} all-to-all(f32[16,1,3356]{2,1,0:T(1,128)S(1)} %all_to_all.34), channel_id=1, replica_groups=mesh['node'=16,'batch'=16] {'node'}, dimensions={0} | all-to-all | bytes 429568 | tf_op jit(solution)/shard_map/all_to_all | solution.py:54
  157.9 0.8 broadcast_in_dim.4
  158.7 12.1 %all-to-all-start.6 = ((f32[16,1,3356]{2,1,0:T(1,128)}), f32[16,1,3356]{2,1,0:T(1,128)S(1)}, u32[]{:S(2)}, u32[]{:S(2)}) async-start(f32[16,1,3356]{2,1,0:T(1,128)} %broadcast_in_dim.4), calls=%async_computation.6 | async-start | bytes 442368 | tf_op jit(solution)/shard_map/all_to_all | solution.py:58
  170.9 1.1 fusion.121
  172.0 0.8 copy.114
  172.8 8.8 %all-to-all-done.6 = f32[16,1,3356]{2,1,0:T(1,128)S(1)} async-done(((f32[16,1,3356]{2,1,0:T(1,128)}), f32[16,1,3356]{2,1,0:T(1,128)S(1)}, u32[]{:S(2)}, u32[]{:S(2)}) %all-to-all-start.6) | async-done | bytes 214816 | tf_op jit(solution)/shard_map/all_to_all | solution.py:58
  181.8 0.8 broadcast_in_dim.5
  182.6 3.5 %all-to-all-start.7 = ((f32[16,1,3356]{2,1,0:T(1,128)}), f32[16,1,3356]{2,1,0:T(1,128)S(1)}, u32[]{:S(2)}, u32[]{:S(2)}) async-start(f32[16,1,3356]{2,1,0:T(1,128)} %broadcast_in_dim.5), calls=%async_computation.7 | async-start | bytes 442368 | tf_op jit(solution)/shard_map/all_to_all | solution.py:60
  186.1 1.1 fusion.113
  187.2 0.8 convert_element_type.224
  188.0 6.4 %all-to-all-done.7 = f32[16,1,3356]{2,1,0:T(1,128)S(1)} async-done(((f32[16,1,3356]{2,1,0:T(1,128)}), f32[16,1,3356]{2,1,0:T(1,128)S(1)}, u32[]{:S(2)}, u32[]{:S(2)}) %all-to-all-start.7) | async-done | bytes 214816 | tf_op jit(solution)/shard_map/all_to_all | solution.py:60
  197.6 0.7 copy.115
  198.3 0.7 mul.151
  (114 shorter events, 11.1 us)
Async XLA Ops:
  0.6 13.9 %copy-start = (bf16[64,320]{1,0:T(8,128)(2,1)S(1)}, bf16[64,320]{1,0:T(8,128)(2,1)}, u32[]{:S(2)}) copy-start(bf16[64,320]{1,0:T(8,128)(2,1)} %param.26) | copy-start | bytes 122884
  1.4 10.9 %copy-start.34 = (s32[16]{0:T(128)S(1)}, s32[16]{0:T(128)}, u32[]{:S(2)}) copy-start(s32[16]{0:T(128)} %param.34) | copy-start | bytes 196
  1.4 11.0 %copy-start.21 = (bf16[512,384]{1,0:T(8,128)(2,1)S(1)}, bf16[512,384]{1,0:T(8,128)(2,1)}, u32[]{:S(2)}) copy-start(bf16[512,384]{1,0:T(8,128)(2,1)} %param.31) | copy-start | bytes 1179652
  3.8 8.9 %copy-start.22 = (bf16[512,384]{1,0:T(8,128)(2,1)S(1)}, bf16[512,384]{1,0:T(8,128)(2,1)}, u32[]{:S(2)}) copy-start(bf16[512,384]{1,0:T(8,128)(2,1)} %param.30) | copy-start | bytes 1179652
  3.8 24.2 %all-to-all-start.1 = ((bf16[16,264,128]{2,1,0:T(8,128)(2,1)}), bf16[16,264,128]{2,1,0:T(8,128)(2,1)}, u32[]{:S(2)}, u32[]{:S(2)}) async-start(bf16[16,264,128]{2,1,0:T(8,128)(2,1)} %pad_maximum_fusion.2), calls=%async_computation.1 | async-start | bytes 2162688 | tf_op jit(solution)/shard_map/all_to_all | solution.py:111
  12.5 82.1 %copy-start.30 = (bf16[2,8,4,128]{3,1,2,0:T(8,128)(2,1)}, bf16[2,8,4,128]{3,1,2,0:T(8,128)(2,1)S(1)}, u32[]{:S(2)}) copy-start(bf16[2,8,4,128]{3,1,2,0:T(8,128)(2,1)S(1)} %copy.174) | copy-start | bytes 49156
  12.9 1.5 copy-start.11
  12.9 1.6 copy-start.3
  14.5 1.5 copy-start.14
  14.5 1.5 copy-start.16
  14.5 1.5 copy-start.24
  14.5 1.5 copy-start.33
  15.1 1.7 copy-start.1
  15.1 2.4 %copy-start.26 = (bf16[16,8,4,128]{3,1,2,0:T(8,128)(2,1)S(1)}, bf16[16,8,4,128]{3,1,2,0:T(8,128)(2,1)}, u32[]{:S(2)}) copy-start(bf16[16,8,4,128]{3,1,2,0:T(8,128)(2,1)} %copy.172) | copy-start | bytes 393220
  16.8 0.7 copy-start.2
  28.0 19.8 %all-to-all-start = ((bf16[16,256,128]{1,2,0:T(8,128)(2,1)}), bf16[16,256,128]{1,2,0:T(8,128)(2,1)}, u32[]{:S(2)}, u32[]{:S(2)}) async-start(bf16[16,256,128]{1,2,0:T(8,128)(2,1)} %fusion.55), calls=%async_computation | async-start | bytes 2097152 | tf_op jit(solution)/shard_map/all_to_all | solution.py:123
  46.2 6.8 %copy-start.28 = (bf16[256,64]{0,1:T(8,128)(2,1)S(1)}, bf16[256,64]{0,1:T(8,128)(2,1)}, u32[]{:S(2)}) copy-start(bf16[256,64]{0,1:T(8,128)(2,1)} %param.28) | copy-start | bytes 98308
  47.8 30.8 %all-to-all-start.3 = ((bf16[16,512,128]{2,1,0:T(8,128)(2,1)}), bf16[16,512,128]{2,1,0:T(8,128)(2,1)}, u32[]{:S(2)}, u32[]{:S(2)}) async-start(bf16[16,512,128]{2,1,0:T(8,128)(2,1)} %pad_maximum_fusion.1), calls=%async_computation.3 | async-start | bytes 4194304 | tf_op jit(solution)/shard_map/all_to_all | solution.py:123
  59.6 0.7 copy-start.6
  67.7 0.7 copy-start.7
  68.4 1.7 copy-start.13
  78.6 34.3 %all-to-all-start.2 = ((bf16[16,512,128]{1,2,0:T(8,128)(2,1)}), bf16[16,512,128]{1,2,0:T(8,128)(2,1)}, u32[]{:S(2)}, u32[]{:S(2)}) async-start(bf16[16,512,128]{1,2,0:T(8,128)(2,1)} %pad_maximum_fusion), calls=%async_computation.2 | async-start | bytes 4194304 | tf_op jit(solution)/shard_map/all_to_all | solution.py:123
  92.6 2.0 %copy-start.27 = (bf16[16,8,4,128]{3,1,2,0:T(8,128)(2,1)S(1)}, bf16[16,8,4,128]{3,1,2,0:T(8,128)(2,1)}, u32[]{:S(2)}) copy-start(bf16[16,8,4,128]{3,1,2,0:T(8,128)(2,1)} %copy.172) | copy-start | bytes 393220
  94.6 2.1 %copy-start.10 = (f32[1,4,64,512]{3,2,1,0:T(8,128)S(1)}, f32[1,4,64,512]{3,2,1,0:T(8,128)}, u32[]{:S(2)}) copy-start(f32[1,4,64,512]{3,2,1,0:T(8,128)} %get-tuple-element.117) | copy-start | bytes 1572868
  94.6 2.1 %copy-start.19 = (bf16[1,4,64,512]{3,2,1,0:T(8,128)(2,1)S(1)}, bf16[1,4,64,512]{3,2,1,0:T(8,128)(2,1)}, u32[]{:S(2)}) copy-start(bf16[1,4,64,512]{3,2,1,0:T(8,128)(2,1)} %get-tuple-element.118) | copy-start | bytes 786436
  96.7 1.1 copy-start.9
  96.7 1.1 copy-start.18
  112.9 22.8 %all-to-all-start.4 = ((bf16[16,256,128]{2,1,0:T(8,128)(2,1)}), bf16[16,256,128]{2,1,0:T(8,128)(2,1)}, u32[]{:S(2)}, u32[]{:S(2)}) async-start(bf16[16,256,128]{2,1,0:T(8,128)(2,1)} %add_convert_fusion), calls=%async_computation.4 | async-start | bytes 2097152 | tf_op jit(solution)/shard_map/all_to_all | solution.py:123
  128.8 3.5 %copy-start.4 = (bf16[1,4,64,512]{3,2,1,0:T(8,128)(2,1)S(1)}, bf16[1,4,64,512]{3,2,1,0:T(8,128)(2,1)}, u32[]{:S(2)}) copy-start(bf16[1,4,64,512]{3,2,1,0:T(8,128)(2,1)} %param.36) | copy-start | bytes 786436
  135.7 2.0 %copy-start.8 = (f32[256,512]{1,0:T(8,128)S(1)}, f32[256,512]{1,0:T(8,128)}, u32[]{:S(2)}) copy-start(f32[256,512]{1,0:T(8,128)} %convolution_add_fusion.2) | copy-start | bytes 1572868
  135.7 2.1 %copy-start.20 = (bf16[256,512]{1,0:T(8,128)(2,1)S(1)}, bf16[256,512]{1,0:T(8,128)(2,1)}, u32[]{:S(2)}) copy-start(bf16[256,512]{1,0:T(8,128)(2,1)} %fusion.111) | copy-start | bytes 786436
  137.8 1.0 copy-start.15
  137.8 1.0 copy-start.17
  138.1 1.6 copy-start.25
  139.8 1.0 copy-start.5
  140.1 0.9 copy-start.23
  140.1 0.9 copy-start.31
  140.7 30.1 %copy-start.32 = (f32[256]{0:T(256)S(1)}, f32[256]{0:T(256)}, u32[]{:S(2)}) copy-start(f32[256]{0:T(256)} %param.29) | copy-start | bytes 3076
  141.0 29.9 %copy-start.29 = (bf16[256,64]{0,1:T(8,128)(2,1)S(1)}, bf16[256,64]{0,1:T(8,128)(2,1)}, u32[]{:S(2)}) copy-start(bf16[256,64]{0,1:T(8,128)(2,1)} %param.28) | copy-start | bytes 98308
  141.0 45.1 %copy-start.12 = (bf16[1,6,64,512]{3,2,1,0:T(8,128)(2,1)S(1)}, bf16[1,6,64,512]{3,2,1,0:T(8,128)(2,1)}, u32[]{:S(2)}) copy-start(bf16[1,6,64,512]{3,2,1,0:T(8,128)(2,1)} %param.23) | copy-start | bytes 1179652
  141.0 45.1 %copy-start.35 = (f32[64]{0:T(128)S(1)}, f32[64]{0:T(128)}, u32[]{:S(2)}) copy-start(f32[64]{0:T(128)} %param.27) | copy-start | bytes 772
  158.7 22.9 %all-to-all-start.6 = ((f32[16,1,3356]{2,1,0:T(1,128)}), f32[16,1,3356]{2,1,0:T(1,128)S(1)}, u32[]{:S(2)}, u32[]{:S(2)}) async-start(f32[16,1,3356]{2,1,0:T(1,128)} %broadcast_in_dim.4), calls=%async_computation.6 | async-start | bytes 442368 | tf_op jit(solution)/shard_map/all_to_all | solution.py:58
  182.6 11.8 %all-to-all-start.7 = ((f32[16,1,3356]{2,1,0:T(1,128)}), f32[16,1,3356]{2,1,0:T(1,128)S(1)}, u32[]{:S(2)}, u32[]{:S(2)}) async-start(f32[16,1,3356]{2,1,0:T(1,128)} %broadcast_in_dim.5), calls=%async_computation.7 | async-start | bytes 442368 | tf_op jit(solution)/shard_map/all_to_all | solution.py:60

commit v8 on v7

--- a/solution.py
+++ b/solution.py
@@ -33,14 +33,20 @@
     return jnp.einsum("mk,kn->mn", gradient, dense, preferred_element_type=jnp.float32)
 
 
-def place_rows(pieces, placer):
-    return jnp.einsum("sma,san->mn", pieces, placer, preferred_element_type=jnp.float32)
-
-
-def pick_rows(values, placer):
-    return jnp.einsum(
-        "mn,san->sma", values, placer, preferred_element_type=jnp.float32
-    ).astype(jnp.bfloat16)
+def place_rows(pieces, chooser):
+    slots, rows, tile_width = pieces.shape
+    weighted = pieces.astype(jnp.float32)[:, :, None, :] * chooser.astype(jnp.float32)[
+        :, None, :, None
+    ]
+    return weighted.sum(axis=0).reshape(rows, chooser.shape[1] * tile_width)
+
+
+def pick_rows(values, chooser):
+    rows = values.shape[0]
+    blocks = chooser.shape[1]
+    shaped = values.reshape(rows, blocks, values.shape[1] // blocks).astype(jnp.float32)
+    weighted = shaped[None] * chooser.astype(jnp.float32)[:, None, :, None]
+    return weighted.sum(axis=2).astype(jnp.bfloat16)
 
 
 def exchange_sum(pieces):
@@ -101,11 +107,8 @@
     gate_val = jax.nn.sigmoid(pre_act[:, :, channel_count:])
     hidden = (filtered * gate_val).astype(jnp.bfloat16)
     flat_hidden = hidden.reshape(row_count, local_nodes)
-    eye_tile = jnp.eye(tile_width, dtype=jnp.bfloat16)
-    eye_slots = jnp.broadcast_to(eye_tile, (own_src.shape[0], tile_width, tile_width))
     dense_fwd = dense_band(local_fwd, blocks, tile_width)
     dense_bwd = dense_band(local_bwd, blocks, tile_width)
-    src_placer = spread_onehot(own_src, eye_slots)
     dst_rows = jnp.zeros((own_dst.shape[0], 8, tile_width), jnp.bfloat16)
     dst_rows = dst_rows.at[:, 0, :blocks].set(own_dst)
     tiles_in = lax.all_to_all(
@@ -116,7 +119,6 @@
         tiled=True,
     )
     recv_dst = tiles_in[:, 2 * tile_width, :blocks]
-    dst_placer = spread_onehot(recv_dst, eye_slots)
     tiles_fwd, tiles_bwd = tiles_in[:, :tile_width], tiles_in[:, tile_width : 2 * tile_width]
 
     def swap(pieces):
@@ -131,19 +133,19 @@
         ).astype(jnp.bfloat16)
 
     def row_terms(gradient, tiles):
-        wanted = pick_rows(gradient, dst_placer)
+        wanted = pick_rows(gradient, recv_dst)
         return jnp.einsum("sma,sac->smc", wanted, tiles, preferred_element_type=jnp.float32)
 
-    (columns,) = swap([pick_rows(flat_hidden, src_placer)])
-    far_fwd = place_rows(far_terms(columns, tiles_fwd), dst_placer)
-    far_bwd = place_rows(far_terms(columns, tiles_bwd), dst_placer)
+    (columns,) = swap([pick_rows(flat_hidden, own_src)])
+    far_fwd = place_rows(far_terms(columns, tiles_fwd), recv_dst)
+    far_bwd = place_rows(far_terms(columns, tiles_bwd), recv_dst)
     hop_fwd = (near_apply(flat_hidden, dense_fwd) + far_fwd).astype(jnp.bfloat16)
     hop_bwd = (near_apply(flat_hidden, dense_bwd) + far_bwd).astype(jnp.bfloat16)
     columns_fwd, columns_bwd = swap(
-        [pick_rows(hop_fwd, src_placer), pick_rows(hop_bwd, src_placer)]
-    )
-    far_fwd = place_rows(far_terms(columns_fwd, tiles_fwd), dst_placer)
-    far_bwd = place_rows(far_terms(columns_bwd, tiles_bwd), dst_placer)
+        [pick_rows(hop_fwd, own_src), pick_rows(hop_bwd, own_src)]
+    )
+    far_fwd = place_rows(far_terms(columns_fwd, tiles_fwd), recv_dst)
+    far_bwd = place_rows(far_terms(columns_bwd, tiles_bwd), recv_dst)
     two_fwd = (near_apply(hop_fwd, dense_fwd) + far_fwd).astype(jnp.bfloat16)
     two_bwd = (near_apply(hop_bwd, dense_bwd) + far_bwd).astype(jnp.bfloat16)
     stacked_parts = jnp.concatenate(
@@ -192,8 +194,8 @@
             row_terms(back2_bwd, tiles_bwd).astype(jnp.bfloat16),
         ]
     )
-    near1_fwd = place_rows(got_fwd, src_placer)
-    near1_bwd = place_rows(got_bwd, src_placer)
+    near1_fwd = place_rows(got_fwd, own_src)
+    near1_bwd = place_rows(got_bwd, own_src)
     back1_fwd = (group_of(1) + near_transpose(back2_fwd, dense_fwd) + near1_fwd).astype(
         jnp.bfloat16
     )
@@ -203,7 +205,7 @@
     (combined,) = swap(
         [(row_terms(back1_fwd, tiles_fwd) + row_terms(back1_bwd, tiles_bwd)).astype(jnp.bfloat16)]
     )
-    far_total = place_rows(combined, src_placer)
+    far_total = place_rows(combined, own_src)
     skip_back = jnp.einsum("sc,wsn->wcn", w_skip, cot_skip, preferred_element_type=jnp.float32)
     direct = (
         grad_parts[:, :, :channel_count]

time: 201 us -> 218 us (1.085)
  waiting for transfers between devices: 38.8 us -> 80.5 us
  matrix products: 58.5 us -> 19.6 us
  other arithmetic: 15 us -> 37.3 us
  starting transfers between devices: 48.4 us -> 43.2 us
  local copies, waits for them, and re-layouts: 23.1 us -> 20.3 us
    all_to_all x4, waiting for transfers between devices: 14.8 us -> 52.6 us  [swap(): lax.all_to_all(jnp.concatenate(pieces, axis=1), 'node', split_axis=0, con...]
    dot_general x10 -> x4, matrix products: 25.1 us -> 4.18 us  [far_terms(): jnp.einsum('smc,sac->sma', columns, tiles, preferred_element_type=jnp.flo...]
    reduce_sum x0 -> x5, other arithmetic: none -> 14.1 us  [the longest x3 8.44 us: place_rows(): return weighted.sum(axis=0).reshape(rows, chooser.shape[1] * tile_width)]
    dot_general x4, matrix products: 14.6 us -> 2.71 us  [row_terms(): jnp.einsum('sma,sac->smc', wanted, tiles, preferred_element_type=jnp.floa...]
    all_to_all x1, waiting for transfers between devices: 8.74 us -> 13.8 us  [shards(): lax.all_to_all(jnp.concatenate([remote_fwd, remote_bwd, dst_rows], axis=1...]
    convert_element_type x2 -> x7, other arithmetic: 0.09 us -> 5.05 us  [the longest x3 2.75 us: pick_rows(): values.reshape(rows, blocks, values.shape[1] // blocks).astype(jnp.float32)]
    dot_general x4, matrix products: 6.55 us -> 2.45 us  [near_apply(): jnp.einsum('mn,kn->mk', values, dense, preferred_element_type=jnp.float32)]
    all_to_all x4, starting transfers between devices: 25 us -> 21.1 us  [swap(): lax.all_to_all(jnp.concatenate(pieces, axis=1), 'node', split_axis=0, con...]
  transfers between devices with their start and end apart: 7 -> 7, of which waited for: 6 -> 7; matrix products, arithmetic and copies ran while one was open for 38% -> 14% of each run, Pallas kernels for 0% -> 0%
where the time goes in v8:
time: 218 us; the launch traced here: 217 us
  waiting for transfers between devices  80.5 us (37%)
  starting transfers between devices  43.2 us (20%)
  other arithmetic  37.3 us (17%)
  local copies, waits for them, and re-layouts  20.3 us (9%)
  matrix products  19.6 us (9%)
  blocking collectives  14.4 us (7%)
    all_to_all x4, waiting for transfers between devices, swap(): lax.all_to_all(jnp.concatenate(pieces, axis=1), 'node', split_axis=0, con...  52.6 us
    all_to_all x4, starting transfers between devices, swap(): lax.all_to_all(jnp.concatenate(pieces, axis=1), 'node', split_axis=0, con...  21.1 us
    all_to_all x1, blocking collectives, exchange_sum(): lax.all_to_all(flat.reshape(node_count, padded // node_count), 'node', 0,...  14.4 us
    all_to_all x1, waiting for transfers between devices, shards(): lax.all_to_all(jnp.concatenate([remote_fwd, remote_bwd, dst_rows], axis=1...  13.8 us
    all_to_all x1, starting transfers between devices, exchange_sum(): part = lax.all_to_all(part, 'batch', 0, 0, tiled=True).sum(axis=0)  11 us
    unnamed x106, local copies, waits for them, and re-layouts  8.99 us
    reduce_sum x3, other arithmetic, place_rows(): return weighted.sum(axis=0).reshape(rows, chooser.shape[1] * tile_width)  8.44 us
    all_to_all x1, starting transfers between devices, shards(): lax.all_to_all(jnp.concatenate([remote_fwd, remote_bwd, dst_rows], axis=1...  7.57 us
  transfers between devices with their start and end apart: 7, of which 7 were waited for; matrix products, arithmetic and copies ran while one was open for 14% of the time, Pallas kernels for 0%

profile of v8, /device:TPU:1, one launch (start us, length us, event | category | flops | bytes accessed | tf_op | source)
XLA Modules:
  0.0 216.8 jit_solution(17069223051428476819)
XLA Ops:
  0.7 0.8 iota_compare_fusion
  1.4 2.3 %pad_maximum_fusion.2 = bf16[16,264,128]{2,1,0:T(8,128)(2,1)} fusion(bf16[16,8,128]{2,1,0:T(8,128)(2,1)S(1)} %pad_convert_fusion, bf16[16,128,128]{2,1,0:T(8,128)(2,1)} %param.33, bf16[16,128,128]{2,1,0:T(8,128)(2,1)} %param.32), kind=kLoop, calls=%fused_computation.71 | loop fusion | flops 3244032 | bytes 2162688 | tf_op jit(solution)/shard_map/concatenate | solution.py:115
  3.8 7.6 %all-to-all-start.1 = ((bf16[16,264,128]{2,1,0:T(8,128)(2,1)}), bf16[16,264,128]{2,1,0:T(8,128)(2,1)S(1)}, u32[]{:S(2)}, u32[]{:S(2)}) async-start(bf16[16,264,128]{2,1,0:T(8,128)(2,1)} %pad_maximum_fusion.2), calls=%async_computation.1 | async-start | bytes 2162688 | tf_op jit(solution)/shard_map/all_to_all | solution.py:114
  11.4 0.5 convolution_bitcast_fusion.1
  11.9 1.5 copy-done.3
  14.0 13.8 %all-to-all-done.1 = bf16[16,264,128]{2,1,0:T(8,128)(2,1)S(1)} async-done(((bf16[16,264,128]{2,1,0:T(8,128)(2,1)}), bf16[16,264,128]{2,1,0:T(8,128)(2,1)S(1)}, u32[]{:S(2)}, u32[]{:S(2)}) %all-to-all-start.1) | async-done | bytes 1081376 | tf_op jit(solution)/shard_map/all_to_all | solution.py:114
  28.0 1.4 multiply_reduce_fusion.6
  30.2 1.5 pad_maximum_fusion.1
  31.8 4.9 %all-to-all-start.3 = ((bf16[16,512,128]{2,1,0:T(8,128)(2,1)}), bf16[16,512,128]{2,1,0:T(8,128)(2,1)}, u32[]{:S(2)}, u32[]{:S(2)}) async-start(bf16[16,512,128]{2,1,0:T(8,128)(2,1)} %pad_maximum_fusion.1), calls=%async_computation.3 | async-start | bytes 4194304 | tf_op jit(solution)/shard_map/all_to_all | solution.py:125
  37.2 0.7 multiply_reduce_fusion.14
  38.7 0.7 copy-done.31
  39.9 1.0 copy-done.1
  40.9 0.9 constant_dynamic-update-slice_fusion.4
  42.1 21.1 %all-to-all-done.3 = bf16[16,512,128]{2,1,0:T(8,128)(2,1)} async-done(((bf16[16,512,128]{2,1,0:T(8,128)(2,1)}), bf16[16,512,128]{2,1,0:T(8,128)(2,1)}, u32[]{:S(2)}, u32[]{:S(2)}) %all-to-all-start.3) | async-done | bytes 2097184 | tf_op jit(solution)/shard_map/all_to_all | solution.py:125
  63.3 2.0 slice_convert_fusion.1
  65.3 3.6 %multiply_reduce_fusion.3 = (f32[256,4,128]{2,0,1:T(8,128)}, f32[256,4,128]{2,0,1:T(8,128)}, bf16[16,256,128]{2,1,0:T(8,128)(2,1)}) fusion(f32[16,256,128]{2,1,0:T(8,128)S(1)} %get-tuple-element.153, f32[16,4]{1,0:T(8,128)S(1)} %fusion.95, f32[16,256,128]{2,1,0:T(8,128)S(1)} %get-tuple-element.152, f32[256,4,128]{2,0,1:T(8,128)S(1)} %copy.166), kind=kLoop, calls=%fused_computation.3 | loop fusion | flops 11796480 | bytes 6816000 | tf_op jit(solution)/shard_map/reduce_sum | solution.py:41
  68.9 7.1 %all-to-all-start = ((bf16[16,256,128]{2,1,0:T(8,128)(2,1)}), bf16[16,256,128]{2,1,0:T(8,128)(2,1)S(1)}, u32[]{:S(2)}, u32[]{:S(2)}) async-start(bf16[16,256,128]{2,1,0:T(8,128)(2,1)} %get-tuple-element.138), calls=%async_computation | async-start | bytes 2097152 | tf_op jit(solution)/shard_map/all_to_all | solution.py:125
  76.1 2.5 %fusion.99 = (f32[1,4,64,512]{3,2,1,0:T(8,128)}, f32[1,4,64,512]{3,2,1,0:T(8,128)S(1)}, f32[1,4,64,512]{3,2,1,0:T(8,128)S(1)}) fusion(f32[1,4,320,512]{3,2,1,0:T(8,128)} %copy-done.3), kind=kLoop, calls=%fused_computation.168 | loop fusion | bytes 3145728 | tf_op jit(solution)/shard_map/slice | solution.py:211
  79.6 0.7 copy-done.19
  80.3 1.0 copy_bitcast_fusion
  81.4 10.2 %all-to-all-done = bf16[16,256,128]{2,1,0:T(8,128)(2,1)S(1)} async-done(((bf16[16,256,128]{2,1,0:T(8,128)(2,1)}), bf16[16,256,128]{2,1,0:T(8,128)(2,1)S(1)}, u32[]{:S(2)}, u32[]{:S(2)}) %all-to-all-start) | async-done | bytes 1048608 | tf_op jit(solution)/shard_map/all_to_all | solution.py:125
  92.5 0.6 copy-done.22
  93.2 4.2 %multiply_reduce_fusion.1 = (bf16[16,256,128]{2,1,0:T(8,128)(2,1)S(1)}, f32[256,4,128]{2,0,1:T(8,128)}, bf16[16,256,128]{2,1,0:T(8,128)(2,1)S(1)}, f32[256,4,128]{2,0,1:T(8,128)}) fusion(f32[256,4,128]{2,0,1:T(8,128)S(1)} %copy-done.22, f32[16,4]{1,0:T(8,128)S(1)} %copy.168, f32[16,256,128]{2,1,0:T(8,128)S(1)} %fusion.2, f32[256,4,128]{2,0,1:T(8,128)S(1)} %copy-done.23, ...), kind=kLoop, calls=%fused_computation.1 | loop fusion | flops 15466496 | bytes 8388864 | tf_op jit(solution)/shard_map/reduce_sum | solution.py:49
  97.9 1.4 add_convert_fusion
  99.3 4.3 %all-to-all-start.4 = ((bf16[16,256,128]{2,1,0:T(8,128)(2,1)}), bf16[16,256,128]{2,1,0:T(8,128)(2,1)S(1)}, u32[]{:S(2)}, u32[]{:S(2)}) async-start(bf16[16,256,128]{2,1,0:T(8,128)(2,1)} %add_convert_fusion), calls=%async_computation.4 | async-start | bytes 2097152 | tf_op jit(solution)/shard_map/all_to_all | solution.py:125
  103.7 1.4 fusion.33
  105.2 0.9 copy_bitcast_fusion.3
  106.4 0.7 copy-done.6
  107.1 0.8 copy_bitcast_fusion.2
  107.9 10.7 %all-to-all-done.4 = bf16[16,256,128]{2,1,0:T(8,128)(2,1)S(1)} async-done(((bf16[16,256,128]{2,1,0:T(8,128)(2,1)}), bf16[16,256,128]{2,1,0:T(8,128)(2,1)S(1)}, u32[]{:S(2)}, u32[]{:S(2)}) %all-to-all-start.4) | async-done | bytes 1048608 | tf_op jit(solution)/shard_map/all_to_all | solution.py:125
  118.8 0.8 copy-done.24
  119.8 3.3 %multiply_reduce_fusion = (f32[256,4,128]{2,0,1:T(8,128)}, bf16[16,256,128]{2,1,0:T(8,128)(2,1)S(1)}, bf16[16,256,128]{2,1,0:T(8,128)(2,1)S(1)}) fusion(f32[16,256,128]{2,1,0:T(8,128)S(1)} %convert_element_type.351, f32[16,4]{1,0:T(8,128)S(1)} %fusion.95, f32[256,4,128]{2,0,1:T(8,128)S(1)} %copy-done.24, f32[256,4,128]{2,0,1:T(8,128)S(1)} %copy-done.25), kind=kLoop, calls=%fused_computation | loop fusion | flops 11403264 | bytes 5767424 | tf_op jit(solution)/shard_map/reduce_sum | solution.py:41
  123.0 1.6 pad_maximum_fusion
  124.6 4.7 %all-to-all-start.2 = ((bf16[16,512,128]{2,1,0:T(8,128)(2,1)}), bf16[16,512,128]{2,1,0:T(8,128)(2,1)}, u32[]{:S(2)}, u32[]{:S(2)}) async-start(bf16[16,512,128]{2,1,0:T(8,128)(2,1)} %pad_maximum_fusion), calls=%async_computation.2 | async-start | bytes 4194304 | tf_op jit(solution)/shard_map/all_to_all | solution.py:125
  129.3 1.3 convolution_bitcast_fusion.6
  130.6 0.8 copy.186
  131.4 1.0 reshape.518
  132.4 1.7 convert_reduce_fusion.2
  134.1 1.8 fusion.39
  135.9 1.5 convolution_add_fusion.2
  138.7 1.0 scatter-add.11
  139.7 0.7 convert_reduce_fusion
  140.3 0.9 convolution_bitcast_fusion
  141.3 2.6 %convert_reduce_fusion.1 = (f32[64]{0:T(128)}, f32[1,6,64,512]{3,2,1,0:T(8,128)}) fusion(bf16[1,4,64,512]{3,2,1,0:T(8,128)(2,1)S(1)} %copy-done.12, f32[1,6,64,512]{3,2,1,0:T(8,128)} %scatter-add.11, f32[1,4,128,512]{3,2,1,0:T(8,128)S(1)} %convolution_bitcast_fusion.3), kind=kLoop, calls=%fused_computation.84 | loop fusion | flops 524224 | bytes 1835520 | tf_op jit(solution)/shard_map/reduce_sum | solution.py:179
  143.8 10.6 %all-to-all-done.2 = bf16[16,512,128]{2,1,0:T(8,128)(2,1)} async-done(((bf16[16,512,128]{2,1,0:T(8,128)(2,1)}), bf16[16,512,128]{2,1,0:T(8,128)(2,1)}, u32[]{:S(2)}, u32[]{:S(2)}) %all-to-all-start.2) | async-done | bytes 2097184 | tf_op jit(solution)/shard_map/all_to_all | solution.py:125
  154.4 1.7 fusion
  156.1 1.7 fusion.1
  157.8 1.5 multiply_reduce_fusion.7
  160.9 1.0 concatenate.57
  162.3 14.4 %all_to_all.46 = f32[16,1,3356]{2,1,0:T(1,128)S(1)} all-to-all(f32[16,1,3356]{2,1,0:T(1,128)S(1)} %all_to_all.34), channel_id=1, replica_groups=mesh['node'=16,'batch'=16] {'node'}, dimensions={0} | all-to-all | bytes 429568 | tf_op jit(solution)/shard_map/all_to_all | solution.py:60
  176.8 0.8 broadcast_in_dim.4
  177.6 11.0 %all-to-all-start.6 = ((f32[16,1,3356]{2,1,0:T(1,128)}), f32[16,1,3356]{2,1,0:T(1,128)S(1)}, u32[]{:S(2)}, u32[]{:S(2)}) async-start(f32[16,1,3356]{2,1,0:T(1,128)} %broadcast_in_dim.4), calls=%async_computation.6 | async-start | bytes 442368 | tf_op jit(solution)/shard_map/all_to_all | solution.py:64
  188.6 1.1 fusion.37
  189.7 0.8 copy.189
  190.6 1.9 convert_element_type.356
  192.5 6.9 %all-to-all-done.6 = f32[16,1,3356]{2,1,0:T(1,128)S(1)} async-done(((f32[16,1,3356]{2,1,0:T(1,128)}), f32[16,1,3356]{2,1,0:T(1,128)S(1)}, u32[]{:S(2)}, u32[]{:S(2)}) %all-to-all-start.6) | async-done | bytes 214816 | tf_op jit(solution)/shard_map/all_to_all | solution.py:64
  199.5 0.8 broadcast_in_dim.5
  200.3 3.5 %all-to-all-start.7 = ((f32[16,1,3356]{2,1,0:T(1,128)}), f32[16,1,3356]{2,1,0:T(1,128)S(1)}, u32[]{:S(2)}, u32[]{:S(2)}) async-start(f32[16,1,3356]{2,1,0:T(1,128)} %broadcast_in_dim.5), calls=%async_computation.7 | async-start | bytes 442368 | tf_op jit(solution)/shard_map/all_to_all | solution.py:66
  203.9 1.1 fusion.29
  205.0 7.2 %all-to-all-done.7 = f32[16,1,3356]{2,1,0:T(1,128)S(1)} async-done(((f32[16,1,3356]{2,1,0:T(1,128)}), f32[16,1,3356]{2,1,0:T(1,128)S(1)}, u32[]{:S(2)}, u32[]{:S(2)}) %all-to-all-start.7) | async-done | bytes 214816 | tf_op jit(solution)/shard_map/all_to_all | solution.py:66
  213.9 0.6 slice_multiply_fusion.3
  214.5 0.6 fusion.88
  215.4 0.7 mul.302
  216.1 0.7 copy.190
  (146 shorter events, 11.9 us)
Async XLA Ops:
  0.6 10.7 %copy-start = (bf16[64,320]{1,0:T(8,128)(2,1)S(1)}, bf16[64,320]{1,0:T(8,128)(2,1)}, u32[]{:S(2)}) copy-start(bf16[64,320]{1,0:T(8,128)(2,1)} %param.26) | copy-start | bytes 122884
  1.4 9.9 %copy-start.11 = (bf16[1,4,64,512]{3,2,1,0:T(8,128)(2,1)S(1)}, bf16[1,4,64,512]{3,2,1,0:T(8,128)(2,1)}, u32[]{:S(2)}) copy-start(bf16[1,4,64,512]{3,2,1,0:T(8,128)(2,1)} %param.36) | copy-start | bytes 786436
  3.8 24.0 %all-to-all-start.1 = ((bf16[16,264,128]{2,1,0:T(8,128)(2,1)}), bf16[16,264,128]{2,1,0:T(8,128)(2,1)S(1)}, u32[]{:S(2)}, u32[]{:S(2)}) async-start(bf16[16,264,128]{2,1,0:T(8,128)(2,1)} %pad_maximum_fusion.2), calls=%async_computation.1 | async-start | bytes 2162688 | tf_op jit(solution)/shard_map/all_to_all | solution.py:114
  11.9 1.5 copy-start.3
  13.5 15.8 %copy-start.14 = (bf16[1,4,64,512]{3,2,1,0:T(8,128)(2,1)}, bf16[1,4,64,512]{3,2,1,0:T(8,128)(2,1)S(1)}, u32[]{:S(2)}) copy-start(bf16[1,4,64,512]{3,2,1,0:T(8,128)(2,1)S(1)} %get-tuple-element.151) | copy-start | bytes 786436
  13.5 15.8 %copy-start.16 = (bf16[1,4,64,512]{3,2,1,0:T(8,128)(2,1)}, bf16[1,4,64,512]{3,2,1,0:T(8,128)(2,1)S(1)}, u32[]{:S(2)}) copy-start(bf16[1,4,64,512]{3,2,1,0:T(8,128)(2,1)S(1)} %get-tuple-element.150) | copy-start | bytes 786436
  28.0 64.5 %copy-start.37 = (f32[16,4]{1,0:T(8,128)}, f32[16,4]{1,0:T(8,128)S(1)}, u32[]{:S(2)}) copy-start(f32[16,4]{1,0:T(8,128)S(1)} %copy.168) | copy-start | bytes 772
  31.8 4.9 %copy-start.35 = (bf16[512,384]{1,0:T(8,128)(2,1)S(1)}, bf16[512,384]{1,0:T(8,128)(2,1)}, u32[]{:S(2)}) copy-start(bf16[512,384]{1,0:T(8,128)(2,1)} %param.30) | copy-start | bytes 1179652
  31.8 5.1 %copy-start.36 = (bf16[512,384]{1,0:T(8,128)(2,1)S(1)}, bf16[512,384]{1,0:T(8,128)(2,1)}, u32[]{:S(2)}) copy-start(bf16[512,384]{1,0:T(8,128)(2,1)} %param.31) | copy-start | bytes 1179652
  31.8 31.5 %all-to-all-start.3 = ((bf16[16,512,128]{2,1,0:T(8,128)(2,1)}), bf16[16,512,128]{2,1,0:T(8,128)(2,1)}, u32[]{:S(2)}, u32[]{:S(2)}) async-start(bf16[16,512,128]{2,1,0:T(8,128)(2,1)} %pad_maximum_fusion.1), calls=%async_computation.3 | async-start | bytes 4194304 | tf_op jit(solution)/shard_map/all_to_all | solution.py:125
  37.1 1.6 copy-start.29
  37.1 2.4 %copy-start.39 = (bf16[128,128]{1,0:T(8,128)(2,1)S(1)}, bf16[128,128]{1,0:T(8,128)(2,1)}, u32[]{:S(2)}) copy-start(bf16[128,128]{1,0:T(8,128)(2,1)} %param.24) | copy-start | bytes 98308
  37.2 2.4 %copy-start.47 = (f32[128]{0:T(128)S(1)}, f32[128]{0:T(128)}, u32[]{:S(2)}) copy-start(f32[128]{0:T(128)} %param.25) | copy-start | bytes 1540
  38.7 0.7 copy-start.31
  38.7 0.8 copy-start.33
  39.8 1.1 copy-start.1
  40.9 1.2 copy-start.48
  41.8 64.2 %copy-start.5 = (bf16[1,4,64,512]{3,2,1,0:T(8,128)(2,1)}, bf16[1,4,64,512]{3,2,1,0:T(8,128)(2,1)S(1)}, u32[]{:S(2)}) copy-start(bf16[1,4,64,512]{3,2,1,0:T(8,128)(2,1)S(1)} %get-tuple-element.146) | copy-start | bytes 786436
  68.9 22.7 %all-to-all-start = ((bf16[16,256,128]{2,1,0:T(8,128)(2,1)}), bf16[16,256,128]{2,1,0:T(8,128)(2,1)S(1)}, u32[]{:S(2)}, u32[]{:S(2)}) async-start(bf16[16,256,128]{2,1,0:T(8,128)(2,1)} %get-tuple-element.138), calls=%async_computation | async-start | bytes 2097152 | tf_op jit(solution)/shard_map/all_to_all | solution.py:125
  76.1 2.5 %copy-start.17 = (bf16[1,4,64,512]{3,2,1,0:T(8,128)(2,1)S(1)}, bf16[1,4,64,512]{3,2,1,0:T(8,128)(2,1)}, u32[]{:S(2)}) copy-start(bf16[1,4,64,512]{3,2,1,0:T(8,128)(2,1)} %copy-done.16) | copy-start | bytes 786436
  76.1 2.5 %copy-start.28 = (f32[256,4,128]{2,0,1:T(8,128)S(1)}, f32[256,4,128]{2,0,1:T(8,128)}, u32[]{:S(2)}) copy-start(f32[256,4,128]{2,0,1:T(8,128)} %get-tuple-element.137) | copy-start | bytes 1572868
  76.1 2.8 %copy-start.15 = (bf16[1,4,64,512]{3,2,1,0:T(8,128)(2,1)S(1)}, bf16[1,4,64,512]{3,2,1,0:T(8,128)(2,1)}, u32[]{:S(2)}) copy-start(bf16[1,4,64,512]{3,2,1,0:T(8,128)(2,1)} %copy-done.14) | copy-start | bytes 786436
  76.1 2.8 %copy-start.27 = (f32[256,4,128]{2,0,1:T(8,128)S(1)}, f32[256,4,128]{2,0,1:T(8,128)}, u32[]{:S(2)}) copy-start(f32[256,4,128]{2,0,1:T(8,128)} %get-tuple-element.136) | copy-start | bytes 1572868
  78.9 0.7 copy-start.18
  79.6 0.7 copy-start.19
  92.0 1.0 copy-start.22
  92.0 1.2 copy-start.23
  99.3 19.3 %all-to-all-start.4 = ((bf16[16,256,128]{2,1,0:T(8,128)(2,1)}), bf16[16,256,128]{2,1,0:T(8,128)(2,1)S(1)}, u32[]{:S(2)}, u32[]{:S(2)}) async-start(bf16[16,256,128]{2,1,0:T(8,128)(2,1)} %add_convert_fusion), calls=%async_computation.4 | async-start | bytes 2097152 | tf_op jit(solution)/shard_map/all_to_all | solution.py:125
  103.7 2.3 %copy-start.21 = (f32[256,4,128]{2,0,1:T(8,128)S(1)}, f32[256,4,128]{2,0,1:T(8,128)}, u32[]{:S(2)}) copy-start(f32[256,4,128]{2,0,1:T(8,128)} %get-tuple-element.133) | copy-start | bytes 1572868
  105.1 0.9 copy-start.8
  106.4 0.7 copy-start.6
  118.6 1.0 copy-start.24
  118.6 1.2 copy-start.25
  124.6 29.8 %all-to-all-start.2 = ((bf16[16,512,128]{2,1,0:T(8,128)(2,1)}), bf16[16,512,128]{2,1,0:T(8,128)(2,1)}, u32[]{:S(2)}, u32[]{:S(2)}) async-start(bf16[16,512,128]{2,1,0:T(8,128)(2,1)} %pad_maximum_fusion), calls=%async_computation.2 | async-start | bytes 4194304 | tf_op jit(solution)/shard_map/all_to_all | solution.py:125
  129.3 8.1 %copy-start.4 = (bf16[1,4,320,512]{3,2,1,0:T(8,128)(2,1)S(1)}, bf16[1,4,320,512]{3,2,1,0:T(8,128)(2,1)}, u32[]{:S(2)}) copy-start(bf16[1,4,320,512]{3,2,1,0:T(8,128)(2,1)} %get-tuple-element.145) | copy-start | bytes 3932164
  132.4 5.1 %copy-start.9 = (bf16[256,512]{1,0:T(8,128)(2,1)S(1)}, bf16[256,512]{1,0:T(8,128)(2,1)}, u32[]{:S(2)}) copy-start(bf16[256,512]{1,0:T(8,128)(2,1)} %copy-done.8) | copy-start | bytes 786436
  132.4 5.1 %copy-start.20 = (bf16[256,512]{1,0:T(8,128)(2,1)S(1)}, bf16[256,512]{1,0:T(8,128)(2,1)}, u32[]{:S(2)}) copy-start(bf16[256,512]{1,0:T(8,128)(2,1)} %copy-done.19) | copy-start | bytes 786436
  132.4 5.1 %copy-start.26 = (f32[256,4,128]{2,0,1:T(8,128)S(1)}, f32[256,4,128]{2,0,1:T(8,128)}, u32[]{:S(2)}) copy-start(f32[256,4,128]{2,0,1:T(8,128)} %get-tuple-element.129) | copy-start | bytes 1572868
  135.9 1.9 copy-start.2
  137.5 0.8 copy-start.40
  138.3 2.1 copy-start.32
  138.3 2.1 copy-start.34
  138.7 2.6 %copy-start.12 = (bf16[1,4,64,512]{3,2,1,0:T(8,128)(2,1)S(1)}, bf16[1,4,64,512]{3,2,1,0:T(8,128)(2,1)}, u32[]{:S(2)}) copy-start(bf16[1,4,64,512]{3,2,1,0:T(8,128)(2,1)} %param.36) | copy-start | bytes 786436
  156.0 1.7 copy-start.38
  157.7 1.6 copy-start.10
  157.7 1.9 copy-start.7
  159.3 1.0 copy-start.13
  160.0 0.9 copy-start.42
  160.0 0.9 copy-start.43
  160.1 0.8 copy-start.44
  160.1 0.8 copy-start.45
  160.3 28.3 %copy-start.41 = (bf16[256,64]{0,1:T(8,128)(2,1)S(1)}, bf16[256,64]{0,1:T(8,128)(2,1)}, u32[]{:S(2)}) copy-start(bf16[256,64]{0,1:T(8,128)(2,1)} %param.28) | copy-start | bytes 98308
  160.3 28.3 %copy-start.46 = (f32[256]{0:T(256)S(1)}, f32[256]{0:T(256)}, u32[]{:S(2)}) copy-start(f32[256]{0:T(256)} %param.29) | copy-start | bytes 3076
  162.3 41.6 %copy-start.30 = (bf16[1,6,64,512]{3,2,1,0:T(8,128)(2,1)S(1)}, bf16[1,6,64,512]{3,2,1,0:T(8,128)(2,1)}, u32[]{:S(2)}) copy-start(bf16[1,6,64,512]{3,2,1,0:T(8,128)(2,1)} %param.23) | copy-start | bytes 1179652
  162.3 41.6 %copy-start.49 = (f32[64]{0:T(128)S(1)}, f32[64]{0:T(128)}, u32[]{:S(2)}) copy-start(f32[64]{0:T(128)} %param.27) | copy-start | bytes 772
  177.6 21.8 %all-to-all-start.6 = ((f32[16,1,3356]{2,1,0:T(1,128)}), f32[16,1,3356]{2,1,0:T(1,128)S(1)}, u32[]{:S(2)}, u32[]{:S(2)}) async-start(f32[16,1,3356]{2,1,0:T(1,128)} %broadcast_in_dim.4), calls=%async_computation.6 | async-start | bytes 442368 | tf_op jit(solution)/shard_map/all_to_all | solution.py:64
  200.3 11.8 %all-to-all-start.7 = ((f32[16,1,3356]{2,1,0:T(1,128)}), f32[16,1,3356]{2,1,0:T(1,128)S(1)}, u32[]{:S(2)}, u32[]{:S(2)}) async-start(f32[16,1,3356]{2,1,0:T(1,128)} %broadcast_in_dim.5), calls=%async_computation.7 | async-start | bytes 442368 | tf_op jit(solution)/shard_map/all_to_all | solution.py:66

commit v9 on v7

--- a/solution.py
+++ b/solution.py
@@ -109,12 +109,15 @@
     dst_rows = jnp.zeros((own_dst.shape[0], 8, tile_width), jnp.bfloat16)
     dst_rows = dst_rows.at[:, 0, :blocks].set(own_dst)
     tiles_in = lax.all_to_all(
-        jnp.concatenate([remote_fwd, remote_bwd, dst_rows], axis=1),
+        jnp.concatenate(
+            [remote_fwd, remote_bwd, dst_rows, pick_rows(flat_hidden, src_placer)], axis=1
+        ),
         "node",
         split_axis=0,
         concat_axis=0,
         tiled=True,
     )
+    columns = tiles_in[:, 2 * tile_width + 8 :]
     recv_dst = tiles_in[:, 2 * tile_width, :blocks]
     dst_placer = spread_onehot(recv_dst, eye_slots)
     tiles_fwd, tiles_bwd = tiles_in[:, :tile_width], tiles_in[:, tile_width : 2 * tile_width]
@@ -134,7 +137,6 @@
         wanted = pick_rows(gradient, dst_placer)
         return jnp.einsum("sma,sac->smc", wanted, tiles, preferred_element_type=jnp.float32)
 
-    (columns,) = swap([pick_rows(flat_hidden, src_placer)])
     far_fwd = place_rows(far_terms(columns, tiles_fwd), dst_placer)
     far_bwd = place_rows(far_terms(columns, tiles_bwd), dst_placer)
     hop_fwd = (near_apply(flat_hidden, dense_fwd) + far_fwd).astype(jnp.bfloat16)

time: 201 us -> 226 us (1.12)
  waiting for transfers between devices: 38.8 us -> 83.6 us
  matrix products: 58.5 us -> 47.3 us
  starting transfers between devices: 48.4 us -> 40 us
  local copies, waits for them, and re-layouts: 23.1 us -> 25.6 us
    all_to_all x4 -> x3, waiting for transfers between devices: 14.8 us -> 38 us  [swap(): lax.all_to_all(jnp.concatenate(pieces, axis=1), 'node', split_axis=0, con...]
    all_to_all x1, waiting for transfers between devices: 8.74 us -> 29.6 us  [shards(): lax.all_to_all(jnp.concatenate([remote_fwd, remote_bwd, dst_rows, pick_ro...]
    all_to_all x4 -> x3, starting transfers between devices: 25 us -> 17.5 us  [swap(): lax.all_to_all(jnp.concatenate(pieces, axis=1), 'node', split_axis=0, con...]
    dot_general x3, matrix products: 6.21 us -> 2.22 us  [pick_rows(): jnp.einsum('mn,san->sma', values, placer, preferred_element_type=jnp.floa...]
    concatenate x0 -> x1, local copies, waits for them, and re-layouts: none -> 2.57 us  [shards(): jnp.concatenate([remote_fwd, remote_bwd, dst_rows, pick_rows(flat_hidden,...]
    unnamed x80 -> x104, local copies, waits for them, and re-layouts: 8.44 us -> 10.7 us
  transfers between devices with their start and end apart: 7 -> 6, of which waited for: 6 -> 6; matrix products, arithmetic and copies ran while one was open for 38% -> 15% of each run, Pallas kernels for 0% -> 0%
where the time goes in v9:
time: 226 us; the launch traced here: 225 us
  waiting for transfers between devices  83.6 us (37%)
  matrix products  47.3 us (21%)
  starting transfers between devices  40 us (18%)
  local copies, waits for them, and re-layouts  25.6 us (11%)
  other arithmetic  15 us (7%)
  blocking collectives  12.1 us (5%)
    all_to_all x3, waiting for transfers between devices, swap(): lax.all_to_all(jnp.concatenate(pieces, axis=1), 'node', split_axis=0, con...  38 us
    all_to_all x1, waiting for transfers between devices, shards(): lax.all_to_all(jnp.concatenate([remote_fwd, remote_bwd, dst_rows, pick_ro...  29.6 us
    dot_general x7, matrix products, place_rows(): jnp.einsum('sma,san->mn', pieces, placer, preferred_element_type=jnp.floa...  18 us
    all_to_all x3, starting transfers between devices, swap(): lax.all_to_all(jnp.concatenate(pieces, axis=1), 'node', split_axis=0, con...  17.5 us
    dot_general x4, matrix products, row_terms(): jnp.einsum('sma,sac->smc', wanted, tiles, preferred_element_type=jnp.floa...  13.6 us
    all_to_all x1, blocking collectives, exchange_sum(): lax.all_to_all(flat.reshape(node_count, padded // node_count), 'node', 0,...  12.1 us
    all_to_all x1, starting transfers between devices, exchange_sum(): part = lax.all_to_all(part, 'batch', 0, 0, tiled=True).sum(axis=0)  11.3 us
    unnamed x104, local copies, waits for them, and re-layouts  10.7 us
  transfers between devices with their start and end apart: 6, of which 6 were waited for; matrix products, arithmetic and copies ran while one was open for 15% of the time, Pallas kernels for 0%

profile of v9, /device:TPU:1, one launch (start us, length us, event | category | flops | bytes accessed | tf_op | source)
XLA Modules:
  0.0 225.1 jit_solution(10043331197799463153)
XLA Ops:
  0.7 0.8 fusion.228
  1.5 0.7 iota_compare_fusion.1
  2.5 0.9 pad_convert_fusion
  3.4 2.0 copy.108
  5.4 1.1 copy.109
  6.5 0.7 copy-done.21
  7.6 1.0 copy-done.1
  8.6 0.9 constant_dynamic-update-slice_fusion.4
  9.5 0.7 fusion.55
  10.9 1.3 pad_maximum_fusion
  12.2 2.6 %copy.110 = bf16[16,520,128]{2,1,0:T(8,128)(2,1)} copy(bf16[16,520,128]{1,2,0:T(8,128)(2,1)S(1)} %pad_maximum_fusion) | data formatting | bytes 4259840 | tf_op jit(solution)/shard_map/concatenate | solution.py:112
  14.8 7.7 %all-to-all-start = ((bf16[16,520,128]{2,1,0:T(8,128)(2,1)}), bf16[16,520,128]{2,1,0:T(8,128)(2,1)}, u32[]{:S(2)}, u32[]{:S(2)}) async-start(bf16[16,520,128]{2,1,0:T(8,128)(2,1)} %copy.110), calls=%async_computation | async-start | bytes 4259840 | tf_op jit(solution)/shard_map/all_to_all | solution.py:111
  23.0 0.7 multiply_reduce_fusion
  24.5 29.6 %all-to-all-done = bf16[16,520,128]{2,1,0:T(8,128)(2,1)} async-done(((bf16[16,520,128]{2,1,0:T(8,128)(2,1)}), bf16[16,520,128]{2,1,0:T(8,128)(2,1)}, u32[]{:S(2)}, u32[]{:S(2)}) %all-to-all-start) | async-done | bytes 2129952 | tf_op jit(solution)/shard_map/all_to_all | solution.py:111
  54.0 0.8 slice.221
  55.1 2.3 %fusion.76 = f32[256,512]{1,0:T(8,128)S(1)} fusion(bf16[16,512]{1,0:T(8,128)(2,1)S(1)} %bitcast.263, bf16[128,512]{1,0:T(8,128)(2,1)S(1)} %bitcast.242, bf16[16,520,128]{2,1,0:T(8,128)(2,1)} %all-to-all-done), kind=kOutput, calls=%fused_computation.63 | convolution fusion | flops 672661504 | bytes 2244608 | tf_op jit(solution)/shard_map/sma,san->mn/dot_general | solution.py:37
  57.8 0.7 fusion.52
  58.6 3.1 %fusion.79 = f32[256,512]{1,0:T(8,128)} fusion(bf16[16,512]{1,0:T(8,128)(2,1)S(1)} %bitcast.264, bf16[128,512]{1,0:T(8,128)(2,1)S(1)} %bitcast.244, bf16[16,520,128]{2,1,0:T(8,128)(2,1)} %all-to-all-done), kind=kOutput, calls=%fused_computation.64 | convolution fusion | flops 672661504 | bytes 2244608 | tf_op jit(solution)/shard_map/sma,san->mn/dot_general | solution.py:37
  61.7 1.4 fusion.119
  63.1 0.7 fusion.49
  63.8 1.6 pad_maximum_fusion.1
  65.4 4.6 %all-to-all-start.1 = ((bf16[16,512,128]{1,2,0:T(8,128)(2,1)}), bf16[16,512,128]{1,2,0:T(8,128)(2,1)}, u32[]{:S(2)}, u32[]{:S(2)}) async-start(bf16[16,512,128]{1,2,0:T(8,128)(2,1)} %pad_maximum_fusion.1), calls=%async_computation.1 | async-start | bytes 4194304 | tf_op jit(solution)/shard_map/all_to_all | solution.py:126
  70.6 1.5 copy-done.3
  72.1 2.5 %convolution_convert_fusion = bf16[16,256,128]{2,1,0:T(8,128)(2,1)S(1)} fusion(bf16[256,512,1]{1,0,2:T(8,128)(2,1)S(1)} %bitcast.236, bf16[16,512]{1,0:T(8,128)(2,1)S(1)} %bitcast.265, bf16[128,512]{1,0:T(8,128)(2,1)} %bitcast.246, bf16[16,520,128]{2,1,0:T(8,128)(2,1)} %all-to-all-done), kind=kOutput, calls=%fused_computation.43 | convolution fusion | flops 673185792 | bytes 1982464 | tf_op jit(solution)/shard_map/sma,sac->smc/dot_general | solution.py:138
  74.6 3.3 %convolution_convert_fusion.1 = bf16[16,256,128]{2,1,0:T(8,128)(2,1)} fusion(bf16[256,512,1]{1,0,2:T(8,128)(2,1)S(1)} %bitcast.238, bf16[16,512]{1,0:T(8,128)(2,1)S(1)} %bitcast.266, bf16[128,512]{1,0:T(8,128)(2,1)} %bitcast.247, bf16[16,520,128]{2,1,0:T(8,128)(2,1)} %all-to-all-done), kind=kOutput, calls=%fused_computation.44 | convolution fusion | flops 673185792 | bytes 1982464 | tf_op jit(solution)/shard_map/sma,sac->smc/dot_general | solution.py:138
  77.9 2.7 %pad_maximum_fusion.2 = bf16[16,512,128]{2,1,0:T(8,128)(2,1)} fusion(bf16[16,256,128]{2,1,0:T(8,128)(2,1)S(1)} %convolution_convert_fusion, bf16[16,256,128]{2,1,0:T(8,128)(2,1)} %convolution_convert_fusion.1), kind=kLoop, calls=%fused_computation.31 | loop fusion | flops 4194304 | bytes 4194304 | tf_op jit(solution)/shard_map/concatenate | solution.py:127
  80.6 17.5 %all-to-all-done.1 = bf16[16,512,128]{1,2,0:T(8,128)(2,1)} async-done(((bf16[16,512,128]{1,2,0:T(8,128)(2,1)}), bf16[16,512,128]{1,2,0:T(8,128)(2,1)}, u32[]{:S(2)}, u32[]{:S(2)}) %all-to-all-start.1) | async-done | bytes 2097184 | tf_op jit(solution)/shard_map/all_to_all | solution.py:126
  98.1 5.7 %all-to-all-start.2 = ((bf16[16,512,128]{2,1,0:T(8,128)(2,1)}), bf16[16,512,128]{2,1,0:T(8,128)(2,1)}, u32[]{:S(2)}, u32[]{:S(2)}) async-start(bf16[16,512,128]{2,1,0:T(8,128)(2,1)} %pad_maximum_fusion.2), calls=%async_computation.2 | async-start | bytes 4194304 | tf_op jit(solution)/shard_map/all_to_all | solution.py:126
  104.1 0.8 copy.123
  104.9 1.7 reshape.423
  106.6 0.7 convert_reduce_fusion.2
  107.3 2.5 %fusion.232 = (f32[1,4,64,512]{3,2,1,0:T(8,128)S(1)}, f32[1,4,64,512]{3,2,1,0:T(8,128)}, f32[1,4,64,512]{3,2,1,0:T(8,128)}) fusion(f32[1,4,320,512]{3,2,1,0:T(8,128)} %copy-done.3), kind=kLoop, calls=%fused_computation.220 | loop fusion | bytes 3145728 | tf_op jit(solution)/shard_map/slice | solution.py:211
  109.8 1.1 fusion.123
  110.8 0.8 copy-done.14
  111.7 3.2 %fusion.82 = f32[256,512]{1,0:T(8,128)} fusion(bf16[16,512,128]{1,2,0:T(8,128)(2,1)} %all-to-all-done.1, bf16[16,512]{1,0:T(8,128)(2,1)S(1)} %bitcast.267, bf16[128,512]{1,0:T(8,128)(2,1)} %bitcast.248, bf16[16,520,128]{2,1,0:T(8,128)(2,1)} %all-to-all-done), kind=kOutput, calls=%fused_computation.65 | convolution fusion | flops 672661504 | bytes 2244608 | tf_op jit(solution)/shard_map/sma,san->mn/dot_general | solution.py:37
  114.9 2.1 fusion.118
  117.0 13.5 %all-to-all-done.2 = bf16[16,512,128]{2,1,0:T(8,128)(2,1)} async-done(((bf16[16,512,128]{2,1,0:T(8,128)(2,1)}), bf16[16,512,128]{2,1,0:T(8,128)(2,1)}, u32[]{:S(2)}, u32[]{:S(2)}) %all-to-all-start.2) | async-done | bytes 2097184 | tf_op jit(solution)/shard_map/all_to_all | solution.py:126
  130.5 2.0 fusion.88
  133.4 2.1 fusion.91
  135.5 1.0 fusion.111
  136.5 3.7 %fusion.59 = f32[16,256,128]{2,1,0:T(8,128)} fusion(bf16[16,512]{1,0:T(8,128)(2,1)S(1)} %bitcast.268, bf16[128,512]{1,0:T(8,128)(2,1)} %bitcast.250, bf16[16,520,128]{2,1,0:T(8,128)(2,1)} %all-to-all-done, bf16[256,512]{1,0:T(8,128)(2,1)S(1)} %fusion.110), kind=kOutput, calls=%fused_computation.54 | convolution fusion | flops 672661504 | bytes 3031040 | tf_op jit(solution)/shard_map/sma,sac->smc/dot_general | solution.py:138
  140.2 4.1 %add_convert_fusion = bf16[16,256,128]{2,1,0:T(8,128)(2,1)} fusion(f32[16,256,128]{2,1,0:T(8,128)} %fusion.59, bf16[16,512]{1,0:T(8,128)(2,1)S(1)} %bitcast.269, bf16[128,512]{1,0:T(8,128)(2,1)} %bitcast.251, bf16[16,520,128]{2,1,0:T(8,128)(2,1)} %all-to-all-done, bf16[256,512]{1,0:T(8,128)(2,1)} %fusion.111), kind=kOutput, calls=%fused_computation.32 | convolution fusion | flops 673710080 | bytes 4079616 | tf_op jit(solution)/shard_map/sma,sac->smc/dot_general | solution.py:138
  144.3 7.2 %all-to-all-start.3 = ((bf16[16,256,128]{2,1,0:T(8,128)(2,1)}), bf16[16,256,128]{2,1,0:T(8,128)(2,1)}, u32[]{:S(2)}, u32[]{:S(2)}) async-start(bf16[16,256,128]{2,1,0:T(8,128)(2,1)} %add_convert_fusion), calls=%async_computation.3 | async-start | bytes 2097152 | tf_op jit(solution)/shard_map/all_to_all | solution.py:126
  151.5 3.2 %fusion.85 = f32[256,512]{1,0:T(8,128)} fusion(bf16[16,512,128]{1,2,0:T(8,128)(2,1)} %all-to-all-done.1, bf16[16,512]{1,0:T(8,128)(2,1)S(1)} %bitcast.270, bf16[128,512]{1,0:T(8,128)(2,1)} %bitcast.252, bf16[16,520,128]{2,1,0:T(8,128)(2,1)} %all-to-all-done), kind=kOutput, calls=%fused_computation.66 | convolution fusion | flops 672661504 | bytes 2244608 | tf_op jit(solution)/shard_map/sma,san->mn/dot_general | solution.py:37
  154.8 1.4 fusion.120
  156.7 0.7 reshape.422
  157.5 2.1 convolution_add_fusion.2
  159.5 7.1 %all-to-all-done.3 = bf16[16,256,128]{2,1,0:T(8,128)(2,1)} async-done(((bf16[16,256,128]{2,1,0:T(8,128)(2,1)}), bf16[16,256,128]{2,1,0:T(8,128)(2,1)}, u32[]{:S(2)}, u32[]{:S(2)}) %all-to-all-start.3) | async-done | bytes 1048608 | tf_op jit(solution)/shard_map/all_to_all | solution.py:126
  166.6 2.0 fusion.94
  171.2 1.0 concatenate.57
  172.6 12.1 %all_to_all.41 = f32[16,1,3356]{2,1,0:T(1,128)S(1)} all-to-all(f32[16,1,3356]{2,1,0:T(1,128)S(1)} %all_to_all.30), channel_id=1, replica_groups=mesh['node'=16,'batch'=16] {'node'}, dimensions={0} | all-to-all | bytes 429568 | tf_op jit(solution)/shard_map/all_to_all | solution.py:54
  184.8 0.8 broadcast_in_dim.4
  185.6 11.3 %all-to-all-start.5 = ((f32[16,1,3356]{2,1,0:T(1,128)}), f32[16,1,3356]{2,1,0:T(1,128)S(1)}, u32[]{:S(2)}, u32[]{:S(2)}) async-start(f32[16,1,3356]{2,1,0:T(1,128)} %broadcast_in_dim.4), calls=%async_computation.5 | async-start | bytes 442368 | tf_op jit(solution)/shard_map/all_to_all | solution.py:58
  197.1 0.8 copy.126
  198.0 9.6 %all-to-all-done.5 = f32[16,1,3356]{2,1,0:T(1,128)S(1)} async-done(((f32[16,1,3356]{2,1,0:T(1,128)}), f32[16,1,3356]{2,1,0:T(1,128)S(1)}, u32[]{:S(2)}, u32[]{:S(2)}) %all-to-all-start.5) | async-done | bytes 214816 | tf_op jit(solution)/shard_map/all_to_all | solution.py:58
  207.8 0.8 broadcast_in_dim.5
  208.6 3.5 %all-to-all-start.6 = ((f32[16,1,3356]{2,1,0:T(1,128)}), f32[16,1,3356]{2,1,0:T(1,128)S(1)}, u32[]{:S(2)}, u32[]{:S(2)}) async-start(f32[16,1,3356]{2,1,0:T(1,128)} %broadcast_in_dim.5), calls=%async_computation.6 | async-start | bytes 442368 | tf_op jit(solution)/shard_map/all_to_all | solution.py:60
  212.1 1.1 fusion.113
  213.2 0.8 convert_element_type.224
  214.0 6.4 %all-to-all-done.6 = f32[16,1,3356]{2,1,0:T(1,128)S(1)} async-done(((f32[16,1,3356]{2,1,0:T(1,128)}), f32[16,1,3356]{2,1,0:T(1,128)S(1)}, u32[]{:S(2)}, u32[]{:S(2)}) %all-to-all-start.6) | async-done | bytes 214816 | tf_op jit(solution)/shard_map/all_to_all | solution.py:60
  222.1 0.6 slice_multiply_fusion.3
  222.8 0.6 fusion.221
  223.6 0.7 mul.151
  224.4 0.7 copy.127
  (137 shorter events, 10.6 us)
Async XLA Ops:
  0.6 69.3 %copy-start = (bf16[64,320]{1,0:T(8,128)(2,1)S(1)}, bf16[64,320]{1,0:T(8,128)(2,1)}, u32[]{:S(2)}) copy-start(bf16[64,320]{1,0:T(8,128)(2,1)} %param.26) | copy-start | bytes 122884
  0.7 4.7 %copy-start.31 = (bf16[16,128,128]{2,1,0:T(8,128)(2,1)S(1)}, bf16[16,128,128]{2,1,0:T(8,128)(2,1)}, u32[]{:S(2)}) copy-start(bf16[16,128,128]{2,1,0:T(8,128)(2,1)} %param.33) | copy-start | bytes 1572868
  0.7 5.8 %copy-start.18 = (bf16[1,6,64,512]{3,2,1,0:T(8,128)(2,1)S(1)}, bf16[1,6,64,512]{3,2,1,0:T(8,128)(2,1)}, u32[]{:S(2)}) copy-start(bf16[1,6,64,512]{3,2,1,0:T(8,128)(2,1)} %param.23) | copy-start | bytes 1179652
  0.7 6.6 %copy-start.36 = (bf16[128,128]{1,0:T(8,128)(2,1)S(1)}, bf16[128,128]{1,0:T(8,128)(2,1)}, u32[]{:S(2)}) copy-start(bf16[128,128]{1,0:T(8,128)(2,1)} %param.24) | copy-start | bytes 98308
  0.7 6.6 %copy-start.45 = (f32[128]{0:T(128)S(1)}, f32[128]{0:T(128)}, u32[]{:S(2)}) copy-start(f32[128]{0:T(128)} %param.25) | copy-start | bytes 1540
  2.4 130.5 %copy-start.42 = (bf16[2,8,4,128]{3,1,2,0:T(8,128)(2,1)}, bf16[2,8,4,128]{3,1,2,0:T(8,128)(2,1)S(1)}, u32[]{:S(2)}) copy-start(bf16[2,8,4,128]{3,1,2,0:T(8,128)(2,1)S(1)} %copy.184) | copy-start | bytes 49156
  2.5 60.6 %copy-start.38 = (bf16[16,8,4,128]{3,1,2,0:T(8,128)(2,1)}, bf16[16,8,4,128]{3,1,2,0:T(8,128)(2,1)S(1)}, u32[]{:S(2)}) copy-start(bf16[16,8,4,128]{3,1,2,0:T(8,128)(2,1)S(1)} %copy.182) | copy-start | bytes 393220
  6.5 0.7 copy-start.21
  6.5 0.8 copy-start.23
  7.6 1.0 copy-start.1
  9.5 1.0 copy-start.10
  9.5 1.2 copy-start.11
  9.5 1.4 copy-start.12
  14.8 7.8 %copy-start.32 = (bf16[512,384]{1,0:T(8,128)(2,1)S(1)}, bf16[512,384]{1,0:T(8,128)(2,1)}, u32[]{:S(2)}) copy-start(bf16[512,384]{1,0:T(8,128)(2,1)} %param.30) | copy-start | bytes 1179652
  14.8 8.0 %copy-start.33 = (bf16[512,384]{1,0:T(8,128)(2,1)S(1)}, bf16[512,384]{1,0:T(8,128)(2,1)}, u32[]{:S(2)}) copy-start(bf16[512,384]{1,0:T(8,128)(2,1)} %param.31) | copy-start | bytes 1179652
  14.8 39.3 %all-to-all-start = ((bf16[16,520,128]{2,1,0:T(8,128)(2,1)}), bf16[16,520,128]{2,1,0:T(8,128)(2,1)}, u32[]{:S(2)}, u32[]{:S(2)}) async-start(bf16[16,520,128]{2,1,0:T(8,128)(2,1)} %copy.110), calls=%async_computation | async-start | bytes 4259840 | tf_op jit(solution)/shard_map/all_to_all | solution.py:111
  57.8 3.9 %copy-start.7 = (bf16[256,512]{1,0:T(8,128)(2,1)}, bf16[256,512]{1,0:T(8,128)(2,1)S(1)}, u32[]{:S(2)}) copy-start(bf16[256,512]{1,0:T(8,128)(2,1)S(1)} %fusion.117) | copy-start | bytes 786436
  65.4 4.6 %copy-start.5 = (bf16[1,4,64,512]{3,2,1,0:T(8,128)(2,1)S(1)}, bf16[1,4,64,512]{3,2,1,0:T(8,128)(2,1)}, u32[]{:S(2)}) copy-start(bf16[1,4,64,512]{3,2,1,0:T(8,128)(2,1)} %param.36) | copy-start | bytes 786436
  65.4 32.7 %all-to-all-start.1 = ((bf16[16,512,128]{1,2,0:T(8,128)(2,1)}), bf16[16,512,128]{1,2,0:T(8,128)(2,1)}, u32[]{:S(2)}, u32[]{:S(2)}) async-start(bf16[16,512,128]{1,2,0:T(8,128)(2,1)} %pad_maximum_fusion.1), calls=%async_computation.1 | async-start | bytes 4194304 | tf_op jit(solution)/shard_map/all_to_all | solution.py:126
  70.6 1.5 copy-start.3
  72.1 2.5 %copy-start.26 = (bf16[1,4,64,512]{3,2,1,0:T(8,128)(2,1)}, bf16[1,4,64,512]{3,2,1,0:T(8,128)(2,1)S(1)}, u32[]{:S(2)}) copy-start(bf16[1,4,64,512]{3,2,1,0:T(8,128)(2,1)S(1)} %get-tuple-element.119) | copy-start | bytes 786436
  72.1 2.5 %copy-start.28 = (bf16[1,4,64,512]{3,2,1,0:T(8,128)(2,1)}, bf16[1,4,64,512]{3,2,1,0:T(8,128)(2,1)S(1)}, u32[]{:S(2)}) copy-start(bf16[1,4,64,512]{3,2,1,0:T(8,128)(2,1)S(1)} %get-tuple-element.118) | copy-start | bytes 786436
  80.6 23.2 %copy-start.6 = (bf16[1,256,512]{2,1,0:T(8,128)(2,1)S(1)}, bf16[1,256,512]{2,1,0:T(8,128)(2,1)}, u32[]{:S(2)}) copy-start(bf16[1,256,512]{2,1,0:T(8,128)(2,1)} %param.37) | copy-start | bytes 786436
  98.1 32.3 %all-to-all-start.2 = ((bf16[16,512,128]{2,1,0:T(8,128)(2,1)}), bf16[16,512,128]{2,1,0:T(8,128)(2,1)}, u32[]{:S(2)}, u32[]{:S(2)}) async-start(bf16[16,512,128]{2,1,0:T(8,128)(2,1)} %pad_maximum_fusion.2), calls=%async_computation.2 | async-start | bytes 4194304 | tf_op jit(solution)/shard_map/all_to_all | solution.py:126
  103.9 5.9 %copy-start.40 = (bf16[256,64]{0,1:T(8,128)(2,1)S(1)}, bf16[256,64]{0,1:T(8,128)(2,1)}, u32[]{:S(2)}) copy-start(bf16[256,64]{0,1:T(8,128)(2,1)} %param.28) | copy-start | bytes 98308
  104.9 6.8 %copy-start.4 = (bf16[1,4,320,512]{3,2,1,0:T(8,128)(2,1)S(1)}, bf16[1,4,320,512]{3,2,1,0:T(8,128)(2,1)}, u32[]{:S(2)}) copy-start(bf16[1,4,320,512]{3,2,1,0:T(8,128)(2,1)} %get-tuple-element.113) | copy-start | bytes 3932164
  106.6 5.0 %copy-start.8 = (bf16[256,512]{1,0:T(8,128)(2,1)S(1)}, bf16[256,512]{1,0:T(8,128)(2,1)}, u32[]{:S(2)}) copy-start(bf16[256,512]{1,0:T(8,128)(2,1)} %copy-done.7) | copy-start | bytes 786436
  110.8 0.8 copy-start.14
  111.7 3.3 %copy-start.9 = (bf16[256,512]{1,0:T(8,128)(2,1)S(1)}, bf16[256,512]{1,0:T(8,128)(2,1)}, u32[]{:S(2)}) copy-start(bf16[256,512]{1,0:T(8,128)(2,1)} %copy-done.7) | copy-start | bytes 786436
  130.5 2.0 copy-start.17
  130.5 2.0 copy-start.29
  132.5 0.9 copy-start.39
  133.4 3.1 %copy-start.25 = (bf16[256,512]{1,0:T(8,128)(2,1)}, bf16[256,512]{1,0:T(8,128)(2,1)S(1)}, u32[]{:S(2)}) copy-start(bf16[256,512]{1,0:T(8,128)(2,1)S(1)} %fusion.110) | copy-start | bytes 786436
  133.4 2.1 copy-start.16
  133.4 2.1 copy-start.27
  144.3 22.3 %all-to-all-start.3 = ((bf16[16,256,128]{2,1,0:T(8,128)(2,1)}), bf16[16,256,128]{2,1,0:T(8,128)(2,1)}, u32[]{:S(2)}, u32[]{:S(2)}) async-start(bf16[16,256,128]{2,1,0:T(8,128)(2,1)} %add_convert_fusion), calls=%async_computation.3 | async-start | bytes 2097152 | tf_op jit(solution)/shard_map/all_to_all | solution.py:126
  151.5 3.3 %copy-start.20 = (bf16[256,512]{1,0:T(8,128)(2,1)S(1)}, bf16[256,512]{1,0:T(8,128)(2,1)}, u32[]{:S(2)}) copy-start(bf16[256,512]{1,0:T(8,128)(2,1)} %fusion.118) | copy-start | bytes 786436
  156.2 1.3 copy-start.15
  159.5 9.4 %copy-start.2 = (f32[1,4,128,512]{3,2,1,0:T(8,128)S(1)}, f32[1,4,128,512]{3,2,1,0:T(8,128)}, u32[]{:S(2)}) copy-start(f32[1,4,128,512]{3,2,1,0:T(8,128)} %copy-done.1) | copy-start | bytes 3145732
  166.6 2.0 copy-start.13
  166.6 2.0 copy-start.30
  168.6 1.0 copy-start.22
  168.7 1.0 copy-start.24
  169.0 1.0 copy-start.37
  170.3 0.9 copy-start.34
  170.3 0.9 copy-start.35
  170.4 0.9 copy-start.43
  170.5 26.4 %copy-start.41 = (bf16[256,64]{0,1:T(8,128)(2,1)S(1)}, bf16[256,64]{0,1:T(8,128)(2,1)}, u32[]{:S(2)}) copy-start(bf16[256,64]{0,1:T(8,128)(2,1)} %param.28) | copy-start | bytes 98308
  170.5 26.4 %copy-start.44 = (f32[256]{0:T(256)S(1)}, f32[256]{0:T(256)}, u32[]{:S(2)}) copy-start(f32[256]{0:T(256)} %param.29) | copy-start | bytes 3076
  170.8 41.3 %copy-start.19 = (bf16[1,6,64,512]{3,2,1,0:T(8,128)(2,1)S(1)}, bf16[1,6,64,512]{3,2,1,0:T(8,128)(2,1)}, u32[]{:S(2)}) copy-start(bf16[1,6,64,512]{3,2,1,0:T(8,128)(2,1)} %param.23) | copy-start | bytes 1179652
  170.8 41.3 %copy-start.46 = (f32[64]{0:T(128)S(1)}, f32[64]{0:T(128)}, u32[]{:S(2)}) copy-start(f32[64]{0:T(128)} %param.27) | copy-start | bytes 772
  185.6 22.1 %all-to-all-start.5 = ((f32[16,1,3356]{2,1,0:T(1,128)}), f32[16,1,3356]{2,1,0:T(1,128)S(1)}, u32[]{:S(2)}, u32[]{:S(2)}) async-start(f32[16,1,3356]{2,1,0:T(1,128)} %broadcast_in_dim.4), calls=%async_computation.5 | async-start | bytes 442368 | tf_op jit(solution)/shard_map/all_to_all | solution.py:58
  208.6 11.8 %all-to-all-start.6 = ((f32[16,1,3356]{2,1,0:T(1,128)}), f32[16,1,3356]{2,1,0:T(1,128)S(1)}, u32[]{:S(2)}, u32[]{:S(2)}) async-start(f32[16,1,3356]{2,1,0:T(1,128)} %broadcast_in_dim.5), calls=%async_computation.6 | async-start | bytes 442368 | tf_op jit(solution)/shard_map/all_to_all | solution.py:60

commit v10 on v7

--- a/solution.py
+++ b/solution.py
@@ -37,10 +37,12 @@
     return jnp.einsum("sma,san->mn", pieces, placer, preferred_element_type=jnp.float32)
 
 
-def pick_rows(values, placer):
-    return jnp.einsum(
-        "mn,san->sma", values, placer, preferred_element_type=jnp.float32
-    ).astype(jnp.bfloat16)
+def pick_rows(values, chooser):
+    rows = values.shape[0]
+    blocks = chooser.shape[1]
+    shaped = values.reshape(rows, blocks, values.shape[1] // blocks).astype(jnp.float32)
+    weighted = shaped[None] * chooser.astype(jnp.float32)[:, None, :, None]
+    return weighted.sum(axis=2).astype(jnp.bfloat16)
 
 
 def exchange_sum(pieces):
@@ -131,16 +133,16 @@
         ).astype(jnp.bfloat16)
 
     def row_terms(gradient, tiles):
-        wanted = pick_rows(gradient, dst_placer)
+        wanted = pick_rows(gradient, recv_dst)
         return jnp.einsum("sma,sac->smc", wanted, tiles, preferred_element_type=jnp.float32)
 
-    (columns,) = swap([pick_rows(flat_hidden, src_placer)])
+    (columns,) = swap([pick_rows(flat_hidden, own_src)])
     far_fwd = place_rows(far_terms(columns, tiles_fwd), dst_placer)
     far_bwd = place_rows(far_terms(columns, tiles_bwd), dst_placer)
     hop_fwd = (near_apply(flat_hidden, dense_fwd) + far_fwd).astype(jnp.bfloat16)
     hop_bwd = (near_apply(flat_hidden, dense_bwd) + far_bwd).astype(jnp.bfloat16)
     columns_fwd, columns_bwd = swap(
-        [pick_rows(hop_fwd, src_placer), pick_rows(hop_bwd, src_placer)]
+        [pick_rows(hop_fwd, own_src), pick_rows(hop_bwd, own_src)]
     )
     far_fwd = place_rows(far_terms(columns_fwd, tiles_fwd), dst_placer)
     far_bwd = place_rows(far_terms(columns_bwd, tiles_bwd), dst_placer)

time: 201 us -> 216 us (1.075)
  matrix products: 58.5 us -> 37.6 us
  local copies, waits for them, and re-layouts: 23.1 us -> 38.6 us
  other arithmetic: 15 us -> 26.6 us
  waiting for transfers between devices: 38.8 us -> 46.2 us
    all_to_all x4, waiting for transfers between devices: 14.8 us -> 30.1 us  [swap(): lax.all_to_all(jnp.concatenate(pieces, axis=1), 'node', split_axis=0, con...]
    dot_general x4, matrix products: 14.6 us -> 2.72 us  [row_terms(): jnp.einsum('sma,sac->smc', wanted, tiles, preferred_element_type=jnp.floa...]
    all_to_all x1, waiting for transfers between devices: 8.74 us -> 0.01 us  [shards(): lax.all_to_all(jnp.concatenate([remote_fwd, remote_bwd, dst_rows], axis=1...]
    reduce_sum x0 -> x4, other arithmetic: none -> 8.55 us  [pick_rows(): return weighted.sum(axis=2).astype(jnp.bfloat16)]
    convert_element_type x0 -> x7, local copies, waits for them, and re-layouts: none -> 6.29 us  [the longest x6 4.94 us: pick_rows(): values.reshape(rows, blocks, values.shape[1] // blocks).astype(jnp.float32)]
    dot_general x3 -> x0, matrix products: 6.21 us -> none  [pick_rows(): jnp.einsum('mn,san->sma', values, placer, preferred_element_type=jnp.floa...]
    unnamed x80 -> x84, local copies, waits for them, and re-layouts: 8.44 us -> 12.1 us
    convert_element_type x0 -> x3, other arithmetic: none -> 2.44 us  [the longest x1 1.26 us: pick_rows(): weighted = shaped[None] * chooser.astype(jnp.float32)[:, None, :, None]]
  transfers between devices with their start and end apart: 7 -> 7, of which waited for: 6 -> 5; matrix products, arithmetic and copies ran while one was open for 38% -> 37% of each run, Pallas kernels for 0% -> 0%
where the time goes in v10:
time: 216 us; the launch traced here: 214 us
  starting transfers between devices  50 us (23%)
  waiting for transfers between devices  46.2 us (21%)
  local copies, waits for them, and re-layouts  38.6 us (18%)
  matrix products  37.6 us (17%)
  other arithmetic  26.6 us (12%)
  blocking collectives  13.7 us (6%)
    all_to_all x4, waiting for transfers between devices, swap(): lax.all_to_all(jnp.concatenate(pieces, axis=1), 'node', split_axis=0, con...  30.1 us
    all_to_all x4, starting transfers between devices, swap(): lax.all_to_all(jnp.concatenate(pieces, axis=1), 'node', split_axis=0, con...  26.6 us
    dot_general x7, matrix products, place_rows(): jnp.einsum('sma,san->mn', pieces, placer, preferred_element_type=jnp.floa...  18 us
    all_to_all x1, blocking collectives, exchange_sum(): lax.all_to_all(flat.reshape(node_count, padded // node_count), 'node', 0,...  13.7 us
    all_to_all x1, starting transfers between devices, exchange_sum(): part = lax.all_to_all(part, 'batch', 0, 0, tiled=True).sum(axis=0)  12.3 us
    unnamed x84, local copies, waits for them, and re-layouts  12.1 us
    all_to_all x1, waiting for transfers between devices, exchange_sum(): part = lax.all_to_all(part, 'batch', 0, 0, tiled=True).sum(axis=0)  9.63 us
    reduce_sum x4, other arithmetic, pick_rows(): return weighted.sum(axis=2).astype(jnp.bfloat16)  8.55 us
  transfers between devices with their start and end apart: 7, of which 5 were waited for; matrix products, arithmetic and copies ran while one was open for 37% of the time, Pallas kernels for 0%

profile of v10, /device:TPU:1, one launch (start us, length us, event | category | flops | bytes accessed | tf_op | source)
XLA Modules:
  0.0 214.2 jit_solution(13153309465987657422)
XLA Ops:
  0.7 0.8 iota_compare_fusion.1
  1.4 2.3 %pad_maximum_fusion.2 = bf16[16,264,128]{2,1,0:T(8,128)(2,1)} fusion(bf16[16,8,128]{2,1,0:T(8,128)(2,1)S(1)} %pad_convert_fusion, bf16[16,128,128]{2,1,0:T(8,128)(2,1)} %param.33, bf16[16,128,128]{2,1,0:T(8,128)(2,1)} %param.32), kind=kLoop, calls=%fused_computation.81 | loop fusion | flops 3244032 | bytes 2162688 | tf_op jit(solution)/shard_map/concatenate | solution.py:114
  3.7 7.6 %all-to-all-start.1 = ((bf16[16,264,128]{2,1,0:T(8,128)(2,1)}), bf16[16,264,128]{2,1,0:T(8,128)(2,1)S(1)}, u32[]{:S(2)}, u32[]{:S(2)}) async-start(bf16[16,264,128]{2,1,0:T(8,128)(2,1)} %pad_maximum_fusion.2), calls=%async_computation.1 | async-start | bytes 2162688 | tf_op jit(solution)/shard_map/all_to_all | solution.py:113
  11.9 1.5 copy-done.1
  13.7 0.9 copy.100
  14.8 0.8 copy.102
  17.9 1.4 reshape.527
  22.1 0.9 constant_dynamic-update-slice_fusion.4
  23.0 1.0 reshape.506
  24.0 1.9 copy.92
  25.9 1.1 convolution_bitcast_fusion.6
  27.1 0.8 copy.106
  27.8 1.0 reshape.504
  28.8 1.6 convert_reduce_fusion.2
  30.4 3.1 %multiply_reduce_fusion.6 = bf16[16,256,128]{2,1,0:T(8,128)(2,1)} fusion(f32[16,4]{1,0:T(8,128)} %get-tuple-element.133, f32[256,4,128]{2,0,1:T(8,128)} %copy.92), kind=kLoop, calls=%fused_computation.6 | loop fusion | flops 3670016 | bytes 1573120 | tf_op jit(solution)/shard_map/reduce_sum | solution.py:45
  33.5 2.6 %fusion.153 = (f32[1,4,64,512]{3,2,1,0:T(8,128)}, f32[1,4,64,512]{3,2,1,0:T(8,128)}, f32[1,4,64,512]{3,2,1,0:T(8,128)}) fusion(f32[1,4,320,512]{3,2,1,0:T(8,128)} %copy-done.1), kind=kLoop, calls=%fused_computation.197 | loop fusion | bytes 3145728 | tf_op jit(solution)/shard_map/slice | solution.py:211
  36.2 1.7 fusion.70
  37.9 6.7 %all-to-all-start = ((bf16[16,256,128]{2,1,0:T(8,128)(2,1)}), bf16[16,256,128]{2,1,0:T(8,128)(2,1)}, u32[]{:S(2)}, u32[]{:S(2)}) async-start(bf16[16,256,128]{2,1,0:T(8,128)(2,1)} %multiply_reduce_fusion.6), calls=%async_computation | async-start | bytes 2097152 | tf_op jit(solution)/shard_map/all_to_all | solution.py:125
  45.2 1.3 copy.93
  46.5 1.3 bitcast_convert_fusion
  47.8 1.4 copy.101
  49.2 1.4 copy.94
  50.5 0.8 mul.211
  51.9 2.6 %multiply_reduce_fusion.3 = (bf16[16,256,128]{2,1,0:T(8,128)(2,1)S(1)}, bf16[16,256,128]{2,1,0:T(8,128)(2,1)S(1)}) fusion(f32[16,4]{1,0:T(8,128)} %copy.101, f32[256,4,128]{2,0,1:T(8,128)} %copy.100, f32[256,4,128]{2,0,1:T(8,128)} %copy.102), kind=kLoop, calls=%fused_computation.3 | loop fusion | flops 7340032 | bytes 3145984 | tf_op jit(solution)/shard_map/reduce_sum | solution.py:45
  55.4 1.5 pad_maximum_fusion.1
  56.9 3.2 %all-to-all-done = bf16[16,256,128]{2,1,0:T(8,128)(2,1)} async-done(((bf16[16,256,128]{2,1,0:T(8,128)(2,1)}), bf16[16,256,128]{2,1,0:T(8,128)(2,1)}, u32[]{:S(2)}, u32[]{:S(2)}) %all-to-all-start) | async-done | bytes 1048608 | tf_op jit(solution)/shard_map/all_to_all | solution.py:125
  60.1 4.6 %all-to-all-start.3 = ((bf16[16,512,128]{2,1,0:T(8,128)(2,1)}), bf16[16,512,128]{2,1,0:T(8,128)(2,1)}, u32[]{:S(2)}, u32[]{:S(2)}) async-start(bf16[16,512,128]{2,1,0:T(8,128)(2,1)} %pad_maximum_fusion.1), calls=%async_computation.3 | async-start | bytes 4194304 | tf_op jit(solution)/shard_map/all_to_all | solution.py:125
  64.8 3.0 %fusion.23 = f32[256,512]{1,0:T(8,128)} fusion(bf16[16,256,128]{2,1,0:T(8,128)(2,1)} %all-to-all-done, bf16[16,512]{1,0:T(8,128)(2,1)} %bitcast.253, bf16[128,512]{1,0:T(8,128)(2,1)} %bitcast.241, bf16[16,264,128]{2,1,0:T(8,128)(2,1)S(1)} %all-to-all-done.1), kind=kOutput, calls=%fused_computation.44 | convolution fusion | flops 672661504 | bytes 2244608 | tf_op jit(solution)/shard_map/sma,san->mn/dot_general | solution.py:37
  67.8 1.4 fusion.64
  70.6 3.0 %fusion.26 = f32[256,512]{1,0:T(8,128)} fusion(bf16[16,256,128]{2,1,0:T(8,128)(2,1)} %all-to-all-done, bf16[16,512]{1,0:T(8,128)(2,1)} %bitcast.254, bf16[128,512]{1,0:T(8,128)(2,1)} %bitcast.242, bf16[16,264,128]{2,1,0:T(8,128)(2,1)S(1)} %all-to-all-done.1), kind=kOutput, calls=%fused_computation.45 | convolution fusion | flops 672661504 | bytes 2244608 | tf_op jit(solution)/shard_map/sma,san->mn/dot_general | solution.py:37
  73.6 1.4 fusion.66
  75.0 1.1 copy_bitcast_fusion.2
  76.2 1.4 multiply_reduce_fusion.5
  77.6 1.5 pad_maximum_fusion
  79.1 10.8 %all-to-all-done.3 = bf16[16,512,128]{2,1,0:T(8,128)(2,1)} async-done(((bf16[16,512,128]{2,1,0:T(8,128)(2,1)}), bf16[16,512,128]{2,1,0:T(8,128)(2,1)}, u32[]{:S(2)}, u32[]{:S(2)}) %all-to-all-start.3) | async-done | bytes 2097184 | tf_op jit(solution)/shard_map/all_to_all | solution.py:125
  89.9 7.5 %all-to-all-start.2 = ((bf16[16,512,128]{2,1,0:T(8,128)(2,1)}), bf16[16,512,128]{2,1,0:T(8,128)(2,1)}, u32[]{:S(2)}, u32[]{:S(2)}) async-start(bf16[16,512,128]{2,1,0:T(8,128)(2,1)} %pad_maximum_fusion), calls=%async_computation.2 | async-start | bytes 4194304 | tf_op jit(solution)/shard_map/all_to_all | solution.py:125
  97.4 2.0 fusion.38
  99.5 2.0 fusion.35
  103.6 1.4 multiply_reduce_fusion
  105.5 1.4 add_convert_fusion
  106.9 16.1 %all-to-all-done.2 = bf16[16,512,128]{2,1,0:T(8,128)(2,1)} async-done(((bf16[16,512,128]{2,1,0:T(8,128)(2,1)}), bf16[16,512,128]{2,1,0:T(8,128)(2,1)}, u32[]{:S(2)}, u32[]{:S(2)}) %all-to-all-start.2) | async-done | bytes 2097184 | tf_op jit(solution)/shard_map/all_to_all | solution.py:125
  123.0 7.8 %all-to-all-start.4 = ((bf16[16,256,128]{2,1,0:T(8,128)(2,1)}), bf16[16,256,128]{2,1,0:T(8,128)(2,1)}, u32[]{:S(2)}, u32[]{:S(2)}) async-start(bf16[16,256,128]{2,1,0:T(8,128)(2,1)} %add_convert_fusion), calls=%async_computation.4 | async-start | bytes 2097152 | tf_op jit(solution)/shard_map/all_to_all | solution.py:125
  130.8 3.0 %fusion.29 = f32[256,512]{1,0:T(8,128)} fusion(bf16[16,512,128]{2,1,0:T(8,128)(2,1)} %all-to-all-done.2, bf16[16,512]{1,0:T(8,128)(2,1)} %bitcast.255, bf16[128,512]{1,0:T(8,128)(2,1)} %bitcast.244, bf16[16,264,128]{2,1,0:T(8,128)(2,1)S(1)} %all-to-all-done.1), kind=kOutput, calls=%fused_computation.46 | convolution fusion | flops 672661504 | bytes 2244608 | tf_op jit(solution)/shard_map/sma,san->mn/dot_general | solution.py:37
  133.8 2.2 %fusion.65 = bf16[256,512]{1,0:T(8,128)(2,1)} fusion(f32[256,512]{1,0:T(8,128)} %fusion.29, bf16[256,512]{1,0:T(8,128)(2,1)} %copy-done.4, bf16[64,8,4,128]{3,2,1,0:T(4,128)(2,1)S(1)} %bitcast.223), kind=kOutput, calls=%fused_computation.72 | convolution fusion | flops 134479872 | bytes 1572864 | tf_op jit(solution)/shard_map/mn,kn->mk/dot_general | solution.py:29
  136.0 3.0 %fusion.32 = f32[256,512]{1,0:T(8,128)} fusion(bf16[16,512,128]{2,1,0:T(8,128)(2,1)} %all-to-all-done.2, bf16[16,512]{1,0:T(8,128)(2,1)} %bitcast.256, bf16[128,512]{1,0:T(8,128)(2,1)} %bitcast.245, bf16[16,264,128]{2,1,0:T(8,128)(2,1)S(1)} %all-to-all-done.1), kind=kOutput, calls=%fused_computation.47 | convolution fusion | flops 672661504 | bytes 2244608 | tf_op jit(solution)/shard_map/sma,san->mn/dot_general | solution.py:37
  139.0 1.8 constant_dynamic-update-slice_fusion.2
  140.8 1.7 constant_dynamic-update-slice_fusion.1
  142.4 1.5 fusion.67
  144.7 1.8 fusion.71
  147.3 1.3 convolution_add_fusion.2
  148.6 2.0 fusion.41
  152.0 0.9 convolution_bitcast_fusion
  153.4 0.8 convert_reduce_fusion.1
  154.2 4.5 %concatenate.57 = f32[53696]{0:T(1024)S(1)} concatenate(f32[16384]{0:T(1024)} %convolution_bitcast_fusion, f32[128]{0:T(128)} %convert_reduce_fusion, f32[20480]{0:T(1024)} %reshape.503, f32[64]{0:T(128)} %get-tuple-element.130, f32[16384]{0:T(1024)S(1)} %reshape.504, f32[256]{0:T(256)} %convert_reduce_fusion.2), dimensions={0} | concatenate | bytes 429568 | tf_op jit(solution)/shard_map/concatenate | solution.py:50
  159.0 13.7 %all_to_all.46 = f32[16,1,3356]{2,1,0:T(1,128)S(1)} all-to-all(f32[16,1,3356]{2,1,0:T(1,128)S(1)} %all_to_all.34), channel_id=1, replica_groups=mesh['node'=16,'batch'=16] {'node'}, dimensions={0} | all-to-all | bytes 429568 | tf_op jit(solution)/shard_map/all_to_all | solution.py:56
  172.9 0.8 broadcast_in_dim.4
  173.7 12.3 %all-to-all-start.6 = ((f32[16,1,3356]{2,1,0:T(1,128)}), f32[16,1,3356]{2,1,0:T(1,128)S(1)}, u32[]{:S(2)}, u32[]{:S(2)}) async-start(f32[16,1,3356]{2,1,0:T(1,128)} %broadcast_in_dim.4), calls=%async_computation.6 | async-start | bytes 442368 | tf_op jit(solution)/shard_map/all_to_all | solution.py:60
  186.2 0.8 copy.109
  187.1 9.6 %all-to-all-done.6 = f32[16,1,3356]{2,1,0:T(1,128)S(1)} async-done(((f32[16,1,3356]{2,1,0:T(1,128)}), f32[16,1,3356]{2,1,0:T(1,128)S(1)}, u32[]{:S(2)}, u32[]{:S(2)}) %all-to-all-start.6) | async-done | bytes 214816 | tf_op jit(solution)/shard_map/all_to_all | solution.py:60
  196.9 0.8 broadcast_in_dim.5
  197.7 3.5 %all-to-all-start.7 = ((f32[16,1,3356]{2,1,0:T(1,128)}), f32[16,1,3356]{2,1,0:T(1,128)S(1)}, u32[]{:S(2)}, u32[]{:S(2)}) async-start(f32[16,1,3356]{2,1,0:T(1,128)} %broadcast_in_dim.5), calls=%async_computation.7 | async-start | bytes 442368 | tf_op jit(solution)/shard_map/all_to_all | solution.py:62
  201.2 1.1 fusion.60
  202.3 0.8 convert_element_type.326
  203.1 6.4 %all-to-all-done.7 = f32[16,1,3356]{2,1,0:T(1,128)S(1)} async-done(((f32[16,1,3356]{2,1,0:T(1,128)}), f32[16,1,3356]{2,1,0:T(1,128)S(1)}, u32[]{:S(2)}, u32[]{:S(2)}) %all-to-all-start.7) | async-done | bytes 214816 | tf_op jit(solution)/shard_map/all_to_all | solution.py:62
  (129 shorter events, 20.8 us)
Async XLA Ops:
  0.6 10.7 %copy-start = (bf16[64,320]{1,0:T(8,128)(2,1)S(1)}, bf16[64,320]{1,0:T(8,128)(2,1)}, u32[]{:S(2)}) copy-start(bf16[64,320]{1,0:T(8,128)(2,1)} %param.26) | copy-start | bytes 122884
  1.4 9.9 %copy-start.5 = (bf16[1,4,64,512]{3,2,1,0:T(8,128)(2,1)S(1)}, bf16[1,4,64,512]{3,2,1,0:T(8,128)(2,1)}, u32[]{:S(2)}) copy-start(bf16[1,4,64,512]{3,2,1,0:T(8,128)(2,1)} %param.36) | copy-start | bytes 786436
  3.7 34.1 %all-to-all-start.1 = ((bf16[16,264,128]{2,1,0:T(8,128)(2,1)}), bf16[16,264,128]{2,1,0:T(8,128)(2,1)S(1)}, u32[]{:S(2)}, u32[]{:S(2)}) async-start(bf16[16,264,128]{2,1,0:T(8,128)(2,1)} %pad_maximum_fusion.2), calls=%async_computation.1 | async-start | bytes 2162688 | tf_op jit(solution)/shard_map/all_to_all | solution.py:113
  11.9 1.5 copy-start.1
  13.5 4.3 %copy-start.8 = (bf16[1,4,64,512]{3,2,1,0:T(8,128)(2,1)}, bf16[1,4,64,512]{3,2,1,0:T(8,128)(2,1)S(1)}, u32[]{:S(2)}) copy-start(bf16[1,4,64,512]{3,2,1,0:T(8,128)(2,1)S(1)} %get-tuple-element.125) | copy-start | bytes 786436
  13.5 4.3 %copy-start.10 = (bf16[1,4,64,512]{3,2,1,0:T(8,128)(2,1)}, bf16[1,4,64,512]{3,2,1,0:T(8,128)(2,1)S(1)}, u32[]{:S(2)}) copy-start(bf16[1,4,64,512]{3,2,1,0:T(8,128)(2,1)S(1)} %get-tuple-element.124) | copy-start | bytes 786436
  13.5 2.8 %copy-start.36 = (s32[16]{0:T(128)S(1)}, s32[16]{0:T(128)}, u32[]{:S(2)}) copy-start(s32[16]{0:T(128)} %param.34) | copy-start | bytes 196
  13.5 4.1 %copy-start.24 = (bf16[512,384]{1,0:T(8,128)(2,1)S(1)}, bf16[512,384]{1,0:T(8,128)(2,1)}, u32[]{:S(2)}) copy-start(bf16[512,384]{1,0:T(8,128)(2,1)} %param.30) | copy-start | bytes 1179652
  19.4 1.5 copy-start.18
  19.4 2.4 %copy-start.25 = (bf16[128,128]{1,0:T(8,128)(2,1)S(1)}, bf16[128,128]{1,0:T(8,128)(2,1)}, u32[]{:S(2)}) copy-start(bf16[128,128]{1,0:T(8,128)(2,1)} %param.24) | copy-start | bytes 98308
  19.4 2.4 %copy-start.35 = (f32[128]{0:T(128)S(1)}, f32[128]{0:T(128)}, u32[]{:S(2)}) copy-start(f32[128]{0:T(128)} %param.25) | copy-start | bytes 1540
  21.0 0.7 copy-start.20
  21.0 0.8 copy-start.22
  30.4 5.7 %copy-start.7 = (bf16[1,256,512]{2,1,0:T(8,128)(2,1)S(1)}, bf16[1,256,512]{2,1,0:T(8,128)(2,1)}, u32[]{:S(2)}) copy-start(bf16[1,256,512]{2,1,0:T(8,128)(2,1)} %param.37) | copy-start | bytes 786436
  30.4 5.7 %copy-start.28 = (bf16[256,64]{0,1:T(8,128)(2,1)S(1)}, bf16[256,64]{0,1:T(8,128)(2,1)}, u32[]{:S(2)}) copy-start(bf16[256,64]{0,1:T(8,128)(2,1)} %param.28) | copy-start | bytes 98308
  37.9 22.2 %all-to-all-start = ((bf16[16,256,128]{2,1,0:T(8,128)(2,1)}), bf16[16,256,128]{2,1,0:T(8,128)(2,1)}, u32[]{:S(2)}, u32[]{:S(2)}) async-start(bf16[16,256,128]{2,1,0:T(8,128)(2,1)} %multiply_reduce_fusion.6), calls=%async_computation | async-start | bytes 2097152 | tf_op jit(solution)/shard_map/all_to_all | solution.py:125
  60.1 29.8 %all-to-all-start.3 = ((bf16[16,512,128]{2,1,0:T(8,128)(2,1)}), bf16[16,512,128]{2,1,0:T(8,128)(2,1)}, u32[]{:S(2)}, u32[]{:S(2)}) async-start(bf16[16,512,128]{2,1,0:T(8,128)(2,1)} %pad_maximum_fusion.1), calls=%async_computation.3 | async-start | bytes 4194304 | tf_op jit(solution)/shard_map/all_to_all | solution.py:125
  69.2 0.7 copy-start.4
  73.6 2.5 %copy-start.31 = (f32[16,4]{1,0:T(8,128)S(1)}, f32[16,4]{1,0:T(8,128)}, u32[]{:S(2)}) copy-start(f32[16,4]{1,0:T(8,128)} %get-tuple-element.133) | copy-start | bytes 772
  75.0 1.1 copy-start.3
  89.9 33.0 %all-to-all-start.2 = ((bf16[16,512,128]{2,1,0:T(8,128)(2,1)}), bf16[16,512,128]{2,1,0:T(8,128)(2,1)}, u32[]{:S(2)}, u32[]{:S(2)}) async-start(bf16[16,512,128]{2,1,0:T(8,128)(2,1)} %pad_maximum_fusion), calls=%async_computation.2 | async-start | bytes 4194304 | tf_op jit(solution)/shard_map/all_to_all | solution.py:125
  97.4 2.0 copy-start.27
  97.4 2.0 copy-start.32
  99.5 2.1 copy-start.11
  99.5 2.1 copy-start.17
  101.5 1.0 copy-start.9
  101.5 1.1 copy-start.16
  101.8 1.2 copy-start.14
  101.9 1.8 copy-start.30
  102.9 0.7 copy-start.12
  123.0 25.6 %all-to-all-start.4 = ((bf16[16,256,128]{2,1,0:T(8,128)(2,1)}), bf16[16,256,128]{2,1,0:T(8,128)(2,1)}, u32[]{:S(2)}, u32[]{:S(2)}) async-start(bf16[16,256,128]{2,1,0:T(8,128)(2,1)} %add_convert_fusion), calls=%async_computation.4 | async-start | bytes 2097152 | tf_op jit(solution)/shard_map/all_to_all | solution.py:125
  139.0 5.7 %copy-start.6 = (bf16[1,4,64,512]{3,2,1,0:T(8,128)(2,1)S(1)}, bf16[1,4,64,512]{3,2,1,0:T(8,128)(2,1)}, u32[]{:S(2)}) copy-start(bf16[1,4,64,512]{3,2,1,0:T(8,128)(2,1)} %param.36) | copy-start | bytes 786436
  142.4 4.8 %copy-start.13 = (bf16[256,512]{1,0:T(8,128)(2,1)S(1)}, bf16[256,512]{1,0:T(8,128)(2,1)}, u32[]{:S(2)}) copy-start(bf16[256,512]{1,0:T(8,128)(2,1)} %copy-done.12) | copy-start | bytes 786436
  143.9 4.7 %copy-start.33 = (bf16[2,8,4,128]{3,1,2,0:T(8,128)(2,1)S(1)}, bf16[2,8,4,128]{3,1,2,0:T(8,128)(2,1)}, u32[]{:S(2)}) copy-start(bf16[2,8,4,128]{3,1,2,0:T(8,128)(2,1)} %copy.168) | copy-start | bytes 49156
  148.6 2.0 copy-start.15
  150.6 1.3 copy-start.21
  150.6 1.3 copy-start.23
  151.0 1.9 copy-start.26
  153.4 32.6 %copy-start.29 = (bf16[256,64]{0,1:T(8,128)(2,1)S(1)}, bf16[256,64]{0,1:T(8,128)(2,1)}, u32[]{:S(2)}) copy-start(bf16[256,64]{0,1:T(8,128)(2,1)} %param.28) | copy-start | bytes 98308
  154.2 31.8 %copy-start.34 = (f32[256]{0:T(256)S(1)}, f32[256]{0:T(256)}, u32[]{:S(2)}) copy-start(f32[256]{0:T(256)} %param.29) | copy-start | bytes 3076
  154.2 47.0 %copy-start.2 = (bf16[1,4,320,512]{3,2,1,0:T(8,128)(2,1)S(1)}, bf16[1,4,320,512]{3,2,1,0:T(8,128)(2,1)}, u32[]{:S(2)}) copy-start(bf16[1,4,320,512]{3,2,1,0:T(8,128)(2,1)} %constant_dynamic-update-slice_fusion) | copy-start | bytes 3932164
  154.2 47.0 %copy-start.19 = (bf16[1,6,64,512]{3,2,1,0:T(8,128)(2,1)S(1)}, bf16[1,6,64,512]{3,2,1,0:T(8,128)(2,1)}, u32[]{:S(2)}) copy-start(bf16[1,6,64,512]{3,2,1,0:T(8,128)(2,1)} %param.23) | copy-start | bytes 1179652
  154.2 47.0 %copy-start.37 = (f32[64]{0:T(128)S(1)}, f32[64]{0:T(128)}, u32[]{:S(2)}) copy-start(f32[64]{0:T(128)} %param.27) | copy-start | bytes 772
  173.7 23.1 %all-to-all-start.6 = ((f32[16,1,3356]{2,1,0:T(1,128)}), f32[16,1,3356]{2,1,0:T(1,128)S(1)}, u32[]{:S(2)}, u32[]{:S(2)}) async-start(f32[16,1,3356]{2,1,0:T(1,128)} %broadcast_in_dim.4), calls=%async_computation.6 | async-start | bytes 442368 | tf_op jit(solution)/shard_map/all_to_all | solution.py:60
  197.7 11.8 %all-to-all-start.7 = ((f32[16,1,3356]{2,1,0:T(1,128)}), f32[16,1,3356]{2,1,0:T(1,128)S(1)}, u32[]{:S(2)}, u32[]{:S(2)}) async-start(f32[16,1,3356]{2,1,0:T(1,128)} %broadcast_in_dim.5), calls=%async_computation.7 | async-start | bytes 442368 | tf_op jit(solution)/shard_map/all_to_all | solution.py:62

commit v11 on v7

--- a/solution.py
+++ b/solution.py
@@ -43,7 +43,7 @@
     ).astype(jnp.bfloat16)
 
 
-def exchange_sum(pieces):
+def exchange_sum(pieces, rider):
     sizes = [piece.size for piece in pieces]
     flat = jnp.concatenate([piece.reshape(-1) for piece in pieces])
     node_count = lax.axis_size("node")
@@ -54,6 +54,7 @@
     part = lax.all_to_all(
         flat.reshape(node_count, padded // node_count), "node", 0, 0, tiled=True
     ).sum(axis=0)
+    part, rider = lax.optimization_barrier((part, rider))
     part = jnp.broadcast_to(part[None], (batch_count, padded // node_count))
     part = lax.all_to_all(part, "batch", 0, 0, tiled=True).sum(axis=0)
     spread = jnp.broadcast_to(part[None], (node_count, padded // node_count))
@@ -63,7 +64,7 @@
     for piece, size in zip(pieces, sizes):
         results.append(spread[offset : offset + size].reshape(piece.shape))
         offset += size
-    return tuple(results)
+    return tuple(results), rider
 
 
 def shards(
@@ -225,19 +226,21 @@
         ],
         axis=2,
     ).astype(jnp.bfloat16)
+    grad_wconv = jnp.einsum(
+        "wton,wtcn->oc", grad_pre, paired_taps, preferred_element_type=jnp.float32
+    )
+    grad_bconv = jnp.sum(grad_pre.astype(jnp.float32), axis=(0, 1, 3))
+    totals, late_pre = exchange_sum(
+        (grad_wconv, grad_bconv, grad_mix, grad_bmix, grad_skip, grad_bskip), grad_pre
+    )
     tap_gradients = jnp.einsum(
-        "oc,wton->wtcn", w_conv, grad_pre, preferred_element_type=jnp.float32
+        "oc,wton->wtcn", w_conv, late_pre, preferred_element_type=jnp.float32
     )
     input_gradient = jnp.zeros((windows, input_steps, channel_count, local_nodes), jnp.float32)
     input_gradient = input_gradient.at[:, :output_steps].add(tap_gradients[:, :, :channel_count])
     input_gradient = input_gradient.at[:, DILATION_GAP:].add(
         tap_gradients[:, :, channel_count:] + residual_cotangent.astype(jnp.float32)
     )
-    grad_wconv = jnp.einsum(
-        "wton,wtcn->oc", grad_pre, paired_taps, preferred_element_type=jnp.float32
-    )
-    grad_bconv = jnp.sum(grad_pre.astype(jnp.float32), axis=(0, 1, 3))
-    totals = exchange_sum((grad_wconv, grad_bconv, grad_mix, grad_bmix, grad_skip, grad_bskip))
     grad_count = (
         windows * lax.axis_size("batch") * local_nodes * lax.axis_size("node") * output_steps
     )

time: 201 us -> 199 us (0.990)
  blocking collectives: 13.8 us -> 0 us
  starting transfers between devices: 48.4 us -> 55.8 us
  waiting for transfers between devices: 38.8 us -> 44.6 us
  matrix products: 58.5 us -> 56.2 us
    all_to_all x1 -> x0, blocking collectives: 13.8 us -> none  [exchange_sum(): lax.all_to_all(flat.reshape(node_count, padded // node_count), 'node', 0,...]
    all_to_all x0 -> x1, starting transfers between devices: none -> 6.61 us  [exchange_sum(): lax.all_to_all(flat.reshape(node_count, padded // node_count), 'node', 0,...]
    all_to_all x0 -> x1, waiting for transfers between devices: none -> 5.39 us  [exchange_sum(): lax.all_to_all(flat.reshape(node_count, padded // node_count), 'node', 0,...]
    unnamed x80 -> x88, local copies, waits for them, and re-layouts: 8.44 us -> 9 us
  transfers between devices with their start and end apart: 7 -> 8, of which waited for: 6 -> 7; matrix products, arithmetic and copies ran while one was open for 38% -> 39% of each run, Pallas kernels for 0% -> 0%
where the time goes in v11:
time: 199 us; the launch traced here: 197 us
  matrix products  56.2 us (28%)
  starting transfers between devices  55.8 us (28%)
  waiting for transfers between devices  44.6 us (22%)
  local copies, waits for them, and re-layouts  22.6 us (11%)
  other arithmetic  16.6 us (8%)
    all_to_all x4, starting transfers between devices, swap(): lax.all_to_all(jnp.concatenate(pieces, axis=1), 'node', split_axis=0, con...  25.9 us
    dot_general x7, matrix products, place_rows(): jnp.einsum('sma,san->mn', pieces, placer, preferred_element_type=jnp.floa...  18.8 us
    dot_general x4, matrix products, row_terms(): jnp.einsum('sma,sac->smc', wanted, tiles, preferred_element_type=jnp.floa...  14.7 us
    all_to_all x4, waiting for transfers between devices, swap(): lax.all_to_all(jnp.concatenate(pieces, axis=1), 'node', split_axis=0, con...  14 us
    all_to_all x1, starting transfers between devices, exchange_sum(): part = lax.all_to_all(part, 'batch', 0, 0, tiled=True).sum(axis=0)  12.1 us
    all_to_all x1, waiting for transfers between devices, exchange_sum(): part = lax.all_to_all(part, 'batch', 0, 0, tiled=True).sum(axis=0)  9.17 us
    unnamed x88, local copies, waits for them, and re-layouts  9 us
    all_to_all x1, waiting for transfers between devices, shards(): lax.all_to_all(jnp.concatenate([remote_fwd, remote_bwd, dst_rows], axis=1...  8.68 us
  transfers between devices with their start and end apart: 8, of which 7 were waited for; matrix products, arithmetic and copies ran while one was open for 39% of the time, Pallas kernels for 0%

profile of v11, /device:TPU:1, one launch (start us, length us, event | category | flops | bytes accessed | tf_op | source)
XLA Modules:
  0.0 197.3 jit_solution(6194388799895320160)
XLA Ops:
  0.7 0.8 iota_compare_fusion.1
  1.5 2.3 %pad_maximum_fusion.2 = bf16[16,264,128]{2,1,0:T(8,128)(2,1)} fusion(bf16[16,8,128]{2,1,0:T(8,128)(2,1)S(1)} %pad_convert_fusion, bf16[16,128,128]{2,1,0:T(8,128)(2,1)} %param.33, bf16[16,128,128]{2,1,0:T(8,128)(2,1)} %param.32), kind=kLoop, calls=%fused_computation.99 | loop fusion | flops 3244032 | bytes 2162688 | tf_op jit(solution)/shard_map/concatenate | solution.py:113
  3.8 7.6 %all-to-all-start.1 = ((bf16[16,264,128]{2,1,0:T(8,128)(2,1)}), bf16[16,264,128]{2,1,0:T(8,128)(2,1)}, u32[]{:S(2)}, u32[]{:S(2)}) async-start(bf16[16,264,128]{2,1,0:T(8,128)(2,1)} %pad_maximum_fusion.2), calls=%async_computation.1 | async-start | bytes 2162688 | tf_op jit(solution)/shard_map/all_to_all | solution.py:112
  12.1 1.2 fusion.231
  15.5 0.7 copy-done.16
  17.4 1.7 fusion.55
  19.2 8.7 %all-to-all-done.1 = bf16[16,264,128]{2,1,0:T(8,128)(2,1)} async-done(((bf16[16,264,128]{2,1,0:T(8,128)(2,1)}), bf16[16,264,128]{2,1,0:T(8,128)(2,1)}, u32[]{:S(2)}, u32[]{:S(2)}) %all-to-all-start.1) | async-done | bytes 1081376 | tf_op jit(solution)/shard_map/all_to_all | solution.py:112
  27.9 4.8 %all-to-all-start = ((bf16[16,256,128]{1,2,0:T(8,128)(2,1)}), bf16[16,256,128]{1,2,0:T(8,128)(2,1)}, u32[]{:S(2)}, u32[]{:S(2)}) async-start(bf16[16,256,128]{1,2,0:T(8,128)(2,1)} %fusion.55), calls=%async_computation | async-start | bytes 2097152 | tf_op jit(solution)/shard_map/all_to_all | solution.py:124
  34.1 2.1 %fusion.232 = (bf16[1,4,64,512]{3,2,1,0:T(8,128)(2,1)}, bf16[1,4,64,512]{3,2,1,0:T(8,128)(2,1)}) fusion(f32[1,4,320,512]{3,2,1,0:T(8,128)} %copy-done.1), kind=kLoop, calls=%fused_computation.222 | loop fusion | bytes 1048576 | tf_op jit(solution)/shard_map/slice | solution.py:183
  36.2 0.8 slice.216
  37.2 3.4 %convolution_convert_fusion = bf16[16,256,128]{2,1,0:T(8,128)(2,1)} fusion(bf16[256,512,1]{1,0,2:T(8,128)(2,1)} %bitcast.239, bf16[16,512]{1,0:T(8,128)(2,1)S(1)} %bitcast.266, bf16[128,512]{1,0:T(8,128)(2,1)} %bitcast.245, bf16[16,264,128]{2,1,0:T(8,128)(2,1)} %all-to-all-done.1), kind=kOutput, calls=%fused_computation.42 | convolution fusion | flops 673185792 | bytes 1982464 | tf_op jit(solution)/shard_map/sma,sac->smc/dot_general | solution.py:136
  40.6 3.4 %convolution_convert_fusion.1 = bf16[16,256,128]{2,1,0:T(8,128)(2,1)} fusion(bf16[256,512,1]{1,0,2:T(8,128)(2,1)} %bitcast.241, bf16[16,512]{1,0:T(8,128)(2,1)S(1)} %bitcast.267, bf16[128,512]{1,0:T(8,128)(2,1)} %bitcast.246, bf16[16,264,128]{2,1,0:T(8,128)(2,1)} %all-to-all-done.1), kind=kOutput, calls=%fused_computation.43 | convolution fusion | flops 673185792 | bytes 1982464 | tf_op jit(solution)/shard_map/sma,sac->smc/dot_general | solution.py:136
  44.0 3.1 %pad_maximum_fusion.1 = bf16[16,512,128]{2,1,0:T(8,128)(2,1)} fusion(bf16[16,256,128]{2,1,0:T(8,128)(2,1)} %convolution_convert_fusion, bf16[16,256,128]{2,1,0:T(8,128)(2,1)} %convolution_convert_fusion.1), kind=kLoop, calls=%fused_computation.30 | loop fusion | flops 4194304 | bytes 4194304 | tf_op jit(solution)/shard_map/concatenate | solution.py:125
  47.7 6.1 %all-to-all-start.3 = ((bf16[16,512,128]{2,1,0:T(8,128)(2,1)}), bf16[16,512,128]{2,1,0:T(8,128)(2,1)}, u32[]{:S(2)}, u32[]{:S(2)}) async-start(bf16[16,512,128]{2,1,0:T(8,128)(2,1)} %pad_maximum_fusion.1), calls=%async_computation.3 | async-start | bytes 4194304 | tf_op jit(solution)/shard_map/all_to_all | solution.py:124
  53.8 1.2 convolution_bitcast_fusion.6
  55.0 3.2 %fusion.79 = f32[256,512]{1,0:T(8,128)} fusion(bf16[16,256,128]{1,2,0:T(8,128)(2,1)} %all-to-all-done, bf16[16,512]{1,0:T(8,128)(2,1)S(1)} %bitcast.268, bf16[128,512]{1,0:T(8,128)(2,1)} %bitcast.247, bf16[16,264,128]{2,1,0:T(8,128)(2,1)} %all-to-all-done.1), kind=kOutput, calls=%fused_computation.63 | convolution fusion | flops 672661504 | bytes 2244608 | tf_op jit(solution)/shard_map/sma,san->mn/dot_general | solution.py:37
  58.2 1.5 fusion.119
  59.7 0.7 copy-done.7
  60.4 2.6 %fusion.49 = bf16[16,256,128]{1,2,0:T(8,128)(2,1)} fusion(bf16[16,512]{1,0:T(8,128)(2,1)S(1)} %bitcast.261, bf16[128,512]{1,0:T(8,128)(2,1)} %bitcast.248, bf16[256,512]{1,0:T(8,128)(2,1)S(1)} %fusion.119), kind=kOutput, calls=%fused_computation.48 | convolution fusion | flops 538443776 | bytes 1458176 | tf_op jit(solution)/shard_map/mn,san->sma/dot_general | solution.py:41
  63.0 3.2 %fusion.76 = f32[256,512]{1,0:T(8,128)} fusion(bf16[16,256,128]{1,2,0:T(8,128)(2,1)} %all-to-all-done, bf16[16,512]{1,0:T(8,128)(2,1)S(1)} %bitcast.269, bf16[128,512]{1,0:T(8,128)(2,1)} %bitcast.249, bf16[16,264,128]{2,1,0:T(8,128)(2,1)} %all-to-all-done.1), kind=kOutput, calls=%fused_computation.62 | convolution fusion | flops 672661504 | bytes 2244608 | tf_op jit(solution)/shard_map/sma,san->mn/dot_general | solution.py:37
  66.2 1.5 fusion.117
  67.7 0.7 copy-done.8
  68.4 1.7 fusion.52
  70.1 1.6 pad_maximum_fusion
  71.7 7.7 %all-to-all-done.3 = bf16[16,512,128]{2,1,0:T(8,128)(2,1)} async-done(((bf16[16,512,128]{2,1,0:T(8,128)(2,1)}), bf16[16,512,128]{2,1,0:T(8,128)(2,1)}, u32[]{:S(2)}, u32[]{:S(2)}) %all-to-all-start.3) | async-done | bytes 2097184 | tf_op jit(solution)/shard_map/all_to_all | solution.py:124
  79.4 7.8 %all-to-all-start.2 = ((bf16[16,512,128]{1,2,0:T(8,128)(2,1)}), bf16[16,512,128]{1,2,0:T(8,128)(2,1)}, u32[]{:S(2)}, u32[]{:S(2)}) async-start(bf16[16,512,128]{1,2,0:T(8,128)(2,1)} %pad_maximum_fusion), calls=%async_computation.2 | async-start | bytes 4194304 | tf_op jit(solution)/shard_map/all_to_all | solution.py:124
  87.2 1.6 convert_reduce_fusion.2
  88.8 0.8 copy.110
  89.6 1.6 reshape.435
  91.2 1.6 convert_reduce_fusion.1
  92.8 1.0 constant_dynamic-update-slice_fusion.3
  93.8 2.0 %fusion.88 = f32[256,512]{1,0:T(8,128)S(1)} fusion(bf16[16,512,128]{2,1,0:T(8,128)(2,1)} %all-to-all-done.3, bf16[16,512]{1,0:T(8,128)(2,1)S(1)} %bitcast.263, bf16[128,512]{1,0:T(8,128)(2,1)} %bitcast.251), kind=kOutput, calls=%fused_computation.66 | convolution fusion | flops 537919488 | bytes 1720320 | tf_op jit(solution)/shard_map/sma,san->mn/dot_general | solution.py:37
  95.8 2.0 %fusion.91 = f32[256,512]{1,0:T(8,128)S(1)} fusion(bf16[16,512,128]{2,1,0:T(8,128)(2,1)} %all-to-all-done.3, bf16[16,512]{1,0:T(8,128)(2,1)S(1)} %bitcast.264, bf16[128,512]{1,0:T(8,128)(2,1)S(1)} %bitcast.257), kind=kOutput, calls=%fused_computation.67 | convolution fusion | flops 537919488 | bytes 1720320 | tf_op jit(solution)/shard_map/sma,san->mn/dot_general | solution.py:37
  97.9 1.0 fusion.110
  98.9 1.0 fusion.111
  99.9 3.7 %fusion.59 = f32[16,256,128]{2,1,0:T(8,128)} fusion(bf16[16,512]{1,0:T(8,128)(2,1)S(1)} %bitcast.270, bf16[128,512]{1,0:T(8,128)(2,1)} %bitcast.252, bf16[16,264,128]{2,1,0:T(8,128)(2,1)} %all-to-all-done.1, bf16[256,512]{1,0:T(8,128)(2,1)} %fusion.110), kind=kOutput, calls=%fused_computation.53 | convolution fusion | flops 672661504 | bytes 3031040 | tf_op jit(solution)/shard_map/sma,sac->smc/dot_general | solution.py:136
  103.7 4.2 %add_convert_fusion = bf16[16,256,128]{2,1,0:T(8,128)(2,1)} fusion(f32[16,256,128]{2,1,0:T(8,128)} %fusion.59, bf16[16,512]{1,0:T(8,128)(2,1)S(1)} %bitcast.271, bf16[128,512]{1,0:T(8,128)(2,1)} %bitcast.253, bf16[16,264,128]{2,1,0:T(8,128)(2,1)} %all-to-all-done.1, bf16[256,512]{1,0:T(8,128)(2,1)} %fusion.111), kind=kOutput, calls=%fused_computation.31 | convolution fusion | flops 673710080 | bytes 4079616 | tf_op jit(solution)/shard_map/sma,sac->smc/dot_general | solution.py:136
  107.8 5.8 %all-to-all-done.2 = bf16[16,512,128]{1,2,0:T(8,128)(2,1)} async-done(((bf16[16,512,128]{1,2,0:T(8,128)(2,1)}), bf16[16,512,128]{1,2,0:T(8,128)(2,1)}, u32[]{:S(2)}, u32[]{:S(2)}) %all-to-all-start.2) | async-done | bytes 2097184 | tf_op jit(solution)/shard_map/all_to_all | solution.py:124
  113.7 7.3 %all-to-all-start.4 = ((bf16[16,256,128]{2,1,0:T(8,128)(2,1)}), bf16[16,256,128]{2,1,0:T(8,128)(2,1)}, u32[]{:S(2)}, u32[]{:S(2)}) async-start(bf16[16,256,128]{2,1,0:T(8,128)(2,1)} %add_convert_fusion), calls=%async_computation.4 | async-start | bytes 2097152 | tf_op jit(solution)/shard_map/all_to_all | solution.py:124
  120.9 3.2 %fusion.82 = f32[256,512]{1,0:T(8,128)} fusion(bf16[16,512,128]{1,2,0:T(8,128)(2,1)} %all-to-all-done.2, bf16[16,512]{1,0:T(8,128)(2,1)S(1)} %bitcast.272, bf16[128,512]{1,0:T(8,128)(2,1)} %bitcast.254, bf16[16,264,128]{2,1,0:T(8,128)(2,1)} %all-to-all-done.1), kind=kOutput, calls=%fused_computation.64 | convolution fusion | flops 672661504 | bytes 2244608 | tf_op jit(solution)/shard_map/sma,san->mn/dot_general | solution.py:37
  124.1 2.2 %fusion.118 = bf16[256,512]{1,0:T(8,128)(2,1)} fusion(f32[256,512]{1,0:T(8,128)} %fusion.82, bf16[256,512]{1,0:T(8,128)(2,1)} %copy-done.8, bf16[64,8,4,128]{3,2,1,0:T(4,128)(2,1)S(1)} %bitcast.224), kind=kOutput, calls=%fused_computation.90 | convolution fusion | flops 134479872 | bytes 1572864 | tf_op jit(solution)/shard_map/mn,kn->mk/dot_general | solution.py:29
  126.3 3.2 %fusion.85 = f32[256,512]{1,0:T(8,128)} fusion(bf16[16,512,128]{1,2,0:T(8,128)(2,1)} %all-to-all-done.2, bf16[16,512]{1,0:T(8,128)(2,1)S(1)} %bitcast.273, bf16[128,512]{1,0:T(8,128)(2,1)} %bitcast.255, bf16[16,264,128]{2,1,0:T(8,128)(2,1)} %all-to-all-done.1), kind=kOutput, calls=%fused_computation.65 | convolution fusion | flops 672661504 | bytes 2244608 | tf_op jit(solution)/shard_map/sma,san->mn/dot_general | solution.py:37
  129.5 1.0 constant_dynamic-update-slice_fusion.2
  130.5 1.0 constant_dynamic-update-slice_fusion.1
  131.5 1.5 fusion.120
  133.5 0.7 reshape.434
  134.2 2.2 %convolution_add_fusion.2 = f32[256,512]{1,0:T(8,128)} fusion(f32[256,512]{1,0:T(8,128)} %bitcast.233, bf16[256,512]{1,0:T(8,128)(2,1)} %fusion.110, bf16[64,8,4,128]{3,2,1,0:T(4,128)(2,1)S(1)} %bitcast.225), kind=kOutput, calls=%fused_computation.73 | convolution fusion | flops 134348800 | bytes 1835008 | tf_op jit(solution)/shard_map/mk,kn->mn/dot_general | solution.py:33
  136.5 2.0 %fusion.94 = f32[256,512]{1,0:T(8,128)S(1)} fusion(bf16[16,256,128]{2,1,0:T(8,128)(2,1)} %all-to-all-done.4, bf16[16,512]{1,0:T(8,128)(2,1)} %bitcast.265, bf16[128,512]{1,0:T(8,128)(2,1)} %bitcast.256), kind=kOutput, calls=%fused_computation.68 | convolution fusion | flops 537919488 | bytes 1720320 | tf_op jit(solution)/shard_map/sma,san->mn/dot_general | solution.py:37
  139.9 1.0 concatenate.59
  140.9 1.0 all_to_all.34
  141.9 6.6 %all-to-all-start.5 = ((f32[16,1,3356]{2,1,0:T(1,128)}), f32[16,1,3356]{2,1,0:T(1,128)S(1)}, u32[]{:S(2)}, u32[]{:S(2)}) async-start(f32[16,1,3356]{2,1,0:T(1,128)} %all_to_all.34), calls=%async_computation.5 | async-start | bytes 442368 | tf_op jit(solution)/shard_map/all_to_all | solution.py:54
  148.6 1.1 fusion.121
  149.7 0.8 copy.114
  150.6 5.4 %all-to-all-done.5 = f32[16,1,3356]{2,1,0:T(1,128)S(1)} async-done(((f32[16,1,3356]{2,1,0:T(1,128)}), f32[16,1,3356]{2,1,0:T(1,128)S(1)}, u32[]{:S(2)}, u32[]{:S(2)}) %all-to-all-start.5) | async-done | bytes 214816 | tf_op jit(solution)/shard_map/all_to_all | solution.py:54
  156.1 0.8 broadcast_in_dim.4
  156.9 12.1 %all-to-all-start.6 = ((f32[16,1,3356]{2,1,0:T(1,128)}), f32[16,1,3356]{2,1,0:T(1,128)S(1)}, u32[]{:S(2)}, u32[]{:S(2)}) async-start(f32[16,1,3356]{2,1,0:T(1,128)} %broadcast_in_dim.4), calls=%async_computation.6 | async-start | bytes 442368 | tf_op jit(solution)/shard_map/all_to_all | solution.py:59
  169.1 1.1 fusion.113
  170.6 9.2 %all-to-all-done.6 = f32[16,1,3356]{2,1,0:T(1,128)S(1)} async-done(((f32[16,1,3356]{2,1,0:T(1,128)}), f32[16,1,3356]{2,1,0:T(1,128)S(1)}, u32[]{:S(2)}, u32[]{:S(2)}) %all-to-all-start.6) | async-done | bytes 214816 | tf_op jit(solution)/shard_map/all_to_all | solution.py:59
  180.0 0.8 broadcast_in_dim.5
  180.8 3.5 %all-to-all-start.7 = ((f32[16,1,3356]{2,1,0:T(1,128)}), f32[16,1,3356]{2,1,0:T(1,128)S(1)}, u32[]{:S(2)}, u32[]{:S(2)}) async-start(f32[16,1,3356]{2,1,0:T(1,128)} %broadcast_in_dim.5), calls=%async_computation.7 | async-start | bytes 442368 | tf_op jit(solution)/shard_map/all_to_all | solution.py:61
  184.5 0.8 convert_element_type.228
  185.3 7.3 %all-to-all-done.7 = f32[16,1,3356]{2,1,0:T(1,128)S(1)} async-done(((f32[16,1,3356]{2,1,0:T(1,128)}), f32[16,1,3356]{2,1,0:T(1,128)S(1)}, u32[]{:S(2)}, u32[]{:S(2)}) %all-to-all-start.7) | async-done | bytes 214816 | tf_op jit(solution)/shard_map/all_to_all | solution.py:61
  195.8 0.7 copy.115
  196.5 0.7 mul.151
  (125 shorter events, 12.3 us)
Async XLA Ops:
  0.6 10.9 %copy-start = (bf16[64,320]{1,0:T(8,128)(2,1)S(1)}, bf16[64,320]{1,0:T(8,128)(2,1)}, u32[]{:S(2)}) copy-start(bf16[64,320]{1,0:T(8,128)(2,1)} %param.26) | copy-start | bytes 122884
  1.4 10.0 %copy-start.38 = (s32[16]{0:T(128)S(1)}, s32[16]{0:T(128)}, u32[]{:S(2)}) copy-start(s32[16]{0:T(128)} %param.34) | copy-start | bytes 196
  1.4 10.1 %copy-start.2 = (bf16[1,4,64,512]{3,2,1,0:T(8,128)(2,1)S(1)}, bf16[1,4,64,512]{3,2,1,0:T(8,128)(2,1)}, u32[]{:S(2)}) copy-start(bf16[1,4,64,512]{3,2,1,0:T(8,128)(2,1)} %param.36) | copy-start | bytes 786436
  3.8 24.1 %all-to-all-start.1 = ((bf16[16,264,128]{2,1,0:T(8,128)(2,1)}), bf16[16,264,128]{2,1,0:T(8,128)(2,1)}, u32[]{:S(2)}, u32[]{:S(2)}) async-start(bf16[16,264,128]{2,1,0:T(8,128)(2,1)} %pad_maximum_fusion.2), calls=%async_computation.1 | async-start | bytes 2162688 | tf_op jit(solution)/shard_map/all_to_all | solution.py:112
  12.1 1.8 copy-start.1
  12.1 1.8 copy-start.6
  12.1 1.8 copy-start.31
  12.1 2.8 %copy-start.23 = (bf16[512,384]{1,0:T(8,128)(2,1)S(1)}, bf16[512,384]{1,0:T(8,128)(2,1)}, u32[]{:S(2)}) copy-start(bf16[512,384]{1,0:T(8,128)(2,1)} %param.31) | copy-start | bytes 1179652
  13.3 1.8 copy-start.24
  14.1 0.8 copy-start.10
  14.1 1.3 copy-start.13
  14.2 2.6 %copy-start.29 = (bf16[16,8,4,128]{3,1,2,0:T(8,128)(2,1)}, bf16[16,8,4,128]{3,1,2,0:T(8,128)(2,1)S(1)}, u32[]{:S(2)}) copy-start(bf16[16,8,4,128]{3,1,2,0:T(8,128)(2,1)S(1)} %copy.172) | copy-start | bytes 393220
  14.9 80.8 %copy-start.33 = (bf16[2,8,4,128]{3,1,2,0:T(8,128)(2,1)}, bf16[2,8,4,128]{3,1,2,0:T(8,128)(2,1)S(1)}, u32[]{:S(2)}) copy-start(bf16[2,8,4,128]{3,1,2,0:T(8,128)(2,1)S(1)} %copy.174) | copy-start | bytes 49156
  15.1 1.2 copy-start.27
  15.1 1.2 copy-start.37
  15.4 0.7 copy-start.16
  15.4 0.8 copy-start.18
  16.7 0.7 copy-start.5
  27.9 19.8 %all-to-all-start = ((bf16[16,256,128]{1,2,0:T(8,128)(2,1)}), bf16[16,256,128]{1,2,0:T(8,128)(2,1)}, u32[]{:S(2)}, u32[]{:S(2)}) async-start(bf16[16,256,128]{1,2,0:T(8,128)(2,1)} %fusion.55), calls=%async_computation | async-start | bytes 2097152 | tf_op jit(solution)/shard_map/all_to_all | solution.py:124
  47.7 31.7 %all-to-all-start.3 = ((bf16[16,512,128]{2,1,0:T(8,128)(2,1)}), bf16[16,512,128]{2,1,0:T(8,128)(2,1)}, u32[]{:S(2)}, u32[]{:S(2)}) async-start(bf16[16,512,128]{2,1,0:T(8,128)(2,1)} %pad_maximum_fusion.1), calls=%async_computation.3 | async-start | bytes 4194304 | tf_op jit(solution)/shard_map/all_to_all | solution.py:124
  59.7 0.7 copy-start.7
  67.7 0.7 copy-start.8
  68.4 1.7 copy-start.15
  79.4 34.3 %all-to-all-start.2 = ((bf16[16,512,128]{1,2,0:T(8,128)(2,1)}), bf16[16,512,128]{1,2,0:T(8,128)(2,1)}, u32[]{:S(2)}, u32[]{:S(2)}) async-start(bf16[16,512,128]{1,2,0:T(8,128)(2,1)} %pad_maximum_fusion), calls=%async_computation.2 | async-start | bytes 4194304 | tf_op jit(solution)/shard_map/all_to_all | solution.py:124
  93.8 2.0 %copy-start.30 = (bf16[16,8,4,128]{3,1,2,0:T(8,128)(2,1)S(1)}, bf16[16,8,4,128]{3,1,2,0:T(8,128)(2,1)}, u32[]{:S(2)}) copy-start(bf16[16,8,4,128]{3,1,2,0:T(8,128)(2,1)} %copy-done.29) | copy-start | bytes 393220
  95.8 2.1 %copy-start.12 = (f32[1,4,64,512]{3,2,1,0:T(8,128)S(1)}, f32[1,4,64,512]{3,2,1,0:T(8,128)}, u32[]{:S(2)}) copy-start(f32[1,4,64,512]{3,2,1,0:T(8,128)} %get-tuple-element.121) | copy-start | bytes 1572868
  95.8 2.1 %copy-start.21 = (bf16[1,4,64,512]{3,2,1,0:T(8,128)(2,1)S(1)}, bf16[1,4,64,512]{3,2,1,0:T(8,128)(2,1)}, u32[]{:S(2)}) copy-start(bf16[1,4,64,512]{3,2,1,0:T(8,128)(2,1)} %get-tuple-element.122) | copy-start | bytes 786436
  97.8 1.1 copy-start.11
  97.8 1.1 copy-start.20
  113.7 22.8 %all-to-all-start.4 = ((bf16[16,256,128]{2,1,0:T(8,128)(2,1)}), bf16[16,256,128]{2,1,0:T(8,128)(2,1)}, u32[]{:S(2)}, u32[]{:S(2)}) async-start(bf16[16,256,128]{2,1,0:T(8,128)(2,1)} %add_convert_fusion), calls=%async_computation.4 | async-start | bytes 2097152 | tf_op jit(solution)/shard_map/all_to_all | solution.py:124
  129.5 3.5 %copy-start.3 = (bf16[1,4,64,512]{3,2,1,0:T(8,128)(2,1)S(1)}, bf16[1,4,64,512]{3,2,1,0:T(8,128)(2,1)}, u32[]{:S(2)}) copy-start(bf16[1,4,64,512]{3,2,1,0:T(8,128)(2,1)} %param.36) | copy-start | bytes 786436
  136.5 2.0 %copy-start.9 = (f32[256,512]{1,0:T(8,128)S(1)}, f32[256,512]{1,0:T(8,128)}, u32[]{:S(2)}) copy-start(f32[256,512]{1,0:T(8,128)} %convolution_add_fusion.2) | copy-start | bytes 1572868
  136.5 2.1 %copy-start.22 = (bf16[256,512]{1,0:T(8,128)(2,1)S(1)}, bf16[256,512]{1,0:T(8,128)(2,1)}, u32[]{:S(2)}) copy-start(bf16[256,512]{1,0:T(8,128)(2,1)} %fusion.111) | copy-start | bytes 786436
  138.5 1.0 copy-start.17
  138.5 1.0 copy-start.19
  138.9 1.0 copy-start.25
  138.9 1.0 copy-start.26
  138.9 1.0 copy-start.34
  138.9 1.0 copy-start.35
  139.2 9.3 %copy-start.32 = (bf16[256,64]{0,1:T(8,128)(2,1)S(1)}, bf16[256,64]{0,1:T(8,128)(2,1)}, u32[]{:S(2)}) copy-start(bf16[256,64]{0,1:T(8,128)(2,1)} %param.28) | copy-start | bytes 98308
  139.2 9.3 %copy-start.36 = (f32[256]{0:T(256)S(1)}, f32[256]{0:T(256)}, u32[]{:S(2)}) copy-start(f32[256]{0:T(256)} %param.29) | copy-start | bytes 3076
  139.9 29.2 %copy-start.14 = (bf16[1,6,64,512]{3,2,1,0:T(8,128)(2,1)S(1)}, bf16[1,6,64,512]{3,2,1,0:T(8,128)(2,1)}, u32[]{:S(2)}) copy-start(bf16[1,6,64,512]{3,2,1,0:T(8,128)(2,1)} %param.23) | copy-start | bytes 1179652
  139.9 29.2 %copy-start.39 = (f32[64]{0:T(128)S(1)}, f32[64]{0:T(128)}, u32[]{:S(2)}) copy-start(f32[64]{0:T(128)} %param.27) | copy-start | bytes 772
  141.9 14.0 %all-to-all-start.5 = ((f32[16,1,3356]{2,1,0:T(1,128)}), f32[16,1,3356]{2,1,0:T(1,128)S(1)}, u32[]{:S(2)}, u32[]{:S(2)}) async-start(f32[16,1,3356]{2,1,0:T(1,128)} %all_to_all.34), calls=%async_computation.5 | async-start | bytes 442368 | tf_op jit(solution)/shard_map/all_to_all | solution.py:54
  149.7 20.5 %copy-start.28 = (bf16[128,128]{1,0:T(8,128)(2,1)S(1)}, bf16[128,128]{1,0:T(8,128)(2,1)}, u32[]{:S(2)}) copy-start(bf16[128,128]{1,0:T(8,128)(2,1)} %param.24) | copy-start | bytes 98308
  156.9 22.9 %all-to-all-start.6 = ((f32[16,1,3356]{2,1,0:T(1,128)}), f32[16,1,3356]{2,1,0:T(1,128)S(1)}, u32[]{:S(2)}, u32[]{:S(2)}) async-start(f32[16,1,3356]{2,1,0:T(1,128)} %broadcast_in_dim.4), calls=%async_computation.6 | async-start | bytes 442368 | tf_op jit(solution)/shard_map/all_to_all | solution.py:59
  170.2 14.1 %copy-start.4 = (bf16[1,4,64,512]{3,2,1,0:T(8,128)(2,1)S(1)}, bf16[1,4,64,512]{3,2,1,0:T(8,128)(2,1)}, u32[]{:S(2)}) copy-start(bf16[1,4,64,512]{3,2,1,0:T(8,128)(2,1)} %param.36) | copy-start | bytes 786436
  180.8 11.8 %all-to-all-start.7 = ((f32[16,1,3356]{2,1,0:T(1,128)}), f32[16,1,3356]{2,1,0:T(1,128)S(1)}, u32[]{:S(2)}, u32[]{:S(2)}) async-start(f32[16,1,3356]{2,1,0:T(1,128)} %broadcast_in_dim.5), calls=%async_computation.7 | async-start | bytes 442368 | tf_op jit(solution)/shard_map/all_to_all | solution.py:61
